TPU v7x, 32 devices: a whole 2x2x4 slice. The times are simulated.
32 devices in a mesh: pulse: 16 (over z, y, core), range: 2 (over x).
Axes of the slice: x: 2, y: 2, z: 4, core: 2. Of those that a mesh axis runs over, the one named last changes fastest.
Arguments:
- raw: bfloat16 [2, 256, 8192], P(None, 'pulse', 'range'), may hold values from -6 to 6
- filt: bfloat16 [2, 512], replicated, may hold values from -0.1875 to 0.1875
- tap_index: int32 [8, 2, 4], replicated, may hold values from 0 to 7
- tap_weight: float32 [8, 2, 4], replicated, may hold values from 0.25 to 0.7
- beam_shift: int32 [2, 510], replicated, may hold values from 0 to 7
- beam_phase: float32 [2, 510], replicated, may hold values from -3.140625 to 3.140625
Outputs:
- image: float32 [2, 256, 8192], P(None, 'pulse', 'range')
All inputs are finite; a program needn't handle non-finite values.
Results may differ from a plain program's by a relative error of at most 0.0003.
Values may be sent and summed in bfloat16 or wider, within the bound.
No kernel may reach another device: no remote copies, remote signals or barrier semaphores. Data moves between devices by JAX's collectives and lax.ppermute only.
A program may use at most 128 MiB of HBM per device.

v0:
```python
import jax
import jax.numpy as jnp
from jax import lax
from jax.sharding import PartitionSpec as P
from jax.experimental import pallas as pl
from jax.experimental.pallas import tpu as pltpu

TAPS = 4
MAXOFF = 8
MARGIN = 15
BLOCK = 256
LANE = 128


half_root = 0.7071067811865476


def shifted(shard, axis, by):
    count = lax.axis_size(axis)
    pairs = [(i, i + by) for i in range(count) if 0 <= i + by < count]
    return lax.ppermute(shard, axis, pairs)


def toeplitz_rows(vector, block, rows):
    taps_len = vector.shape[0]
    width = rows + 1
    line = jnp.concatenate([vector, jnp.zeros((width - taps_len,), vector.dtype)])
    return jnp.tile(line, block)[: block * rows].reshape(block, rows)


def band_matrix(filt, block, rows):
    real_band = toeplitz_rows(filt[0], block, rows).T
    imag_band = toeplitz_rows(filt[1], block, rows).T
    upper = jnp.concatenate([real_band, imag_band], axis=1)
    lower = jnp.concatenate([-imag_band, real_band], axis=1)
    return jnp.concatenate([upper, lower], axis=0)


def compress(wide, filt, blocks):
    parts, count, length = wide.shape
    taps_len = filt.shape[1]
    reach = -(-(BLOCK + taps_len - 1) // BLOCK)
    rows = reach * BLOCK
    cut = wide.reshape(parts, count, length // BLOCK, BLOCK)
    window = jnp.concatenate([cut[:, :, c : c + blocks] for c in range(reach)], axis=3)
    segments = jnp.concatenate([window[0], window[1]], axis=2)
    product = lax.dot_general(
        segments,
        band_matrix(filt, BLOCK, rows),
        (((2,), (0,)), ((), ())),
        preferred_element_type=jnp.float32,
    )
    real_part = product[:, :, :BLOCK].reshape(count, blocks * BLOCK)
    imag_part = product[:, :, BLOCK:].reshape(count, blocks * BLOCK)
    return jnp.stack([real_part, imag_part])


def merge_kernel(weight_ref, kid_ref, table_ref, out_ref):
    length = kid_ref.shape[-1]
    reach = MARGIN - MAXOFF + 1
    acc = [[None, None], [None, None]]
    for c in range(2):
        interp = []
        for part in range(2):
            x = kid_ref[c, part]
            total = weight_ref[c, 0] * x
            for offset in range(1, reach):
                total = total + weight_ref[c, offset] * pltpu.roll(x, length - offset, 1)
            interp.append(total)
        for half in range(2):
            moved = []
            for part in range(2):
                pick = interp[part]
                for bit in (2, 1, 0):
                    hit = table_ref[bit, c, half][:, 0:1] > 0.5
                    pick = jnp.where(hit, pltpu.roll(pick, length - (1 << bit), 1), pick)
                moved.append(pick)
            cos_row = table_ref[3, c, half][:, 0:1]
            sin_row = table_ref[4, c, half][:, 0:1]
            real_part = cos_row * moved[0] - sin_row * moved[1]
            imag_part = sin_row * moved[0] + cos_row * moved[1]
            if c == 0:
                acc[half] = [real_part, imag_part]
            else:
                acc[half] = [acc[half][0] + real_part, acc[half][1] + imag_part]
    for half in range(2):
        for part in range(2):
            out_ref[half, part] = acc[half][part] * half_root


def merge_call(weights, kids, table):
    _, _, rows, length = kids.shape
    vmem = pltpu.VMEM
    elems = 2 * 2 * rows * length
    return pl.pallas_call(
        merge_kernel,
        out_shape=jax.ShapeDtypeStruct((2, 2, rows, length), jnp.float32),
        in_specs=[
            pl.BlockSpec(memory_space=pltpu.SMEM),
            pl.BlockSpec(memory_space=vmem),
            pl.BlockSpec(memory_space=vmem),
        ],
        out_specs=pl.BlockSpec(memory_space=vmem),
        cost_estimate=pl.CostEstimate(flops=60 * elems, transcendentals=0, bytes_accessed=8 * elems),
    )(weights, kids, table)


def tap_weights(taps, weights):
    reach = MARGIN - MAXOFF + 1
    hit = taps[..., :, None] == jnp.arange(reach, dtype=taps.dtype)
    return jnp.sum(jnp.where(hit, weights[..., :, None], 0.0), axis=-2)


def per_row(table, groups):
    beams = table.shape[-1] // 2
    halves = table.reshape(table.shape[:-1] + (2, beams))
    return jnp.tile(halves, (1,) * (halves.ndim - 1) + (groups,))


def merge_section(level, beams, weights, chosen, cosine, sine):
    parts, rows, length = level.shape
    groups = rows // (2 * beams)
    pairs = level.reshape(parts, groups, 2, beams, length)
    kids = jnp.stack([pairs[:, :, c].reshape(parts, rows // 2, length) for c in range(2)])
    bits = [((chosen >> bit) & 1).astype(jnp.float32) for bit in range(3)]
    packed = jnp.stack(bits + [cosine, sine])
    table = jnp.broadcast_to(per_row(packed, groups)[..., None], (5, 2, 2, rows // 2, LANE))
    out = merge_call(weights, kids, table)
    merged = jnp.stack([out[h].reshape(parts, groups, beams, length) for h in range(2)], axis=2)
    return merged.reshape(parts, rows, length)


def padded_lanes(level, width):
    length = level.shape[-1]
    target = -(-width // LANE) * LANE
    if target > length:
        return jnp.pad(level, ((0, 0), (0, 0), (0, target - length)))
    return level[..., :target]


def on_device(raw, filt, tap_index, tap_weight, beam_shift, beam_phase):
    pulse_count = lax.axis_size("pulse")
    parts, local_beams, bins = raw.shape
    taps_len = filt.shape[1]
    local_sections = local_beams.bit_length() - 1
    cross_sections = pulse_count.bit_length() - 1
    sections = local_sections + cross_sections
    extra = sections * MARGIN
    blocks = -(-(bins + extra) // BLOCK)
    reach = -(-(BLOCK + taps_len - 1) // BLOCK)
    rim_len = (blocks + reach - 1) * BLOCK - bins
    rim = shifted(raw[:, :, :rim_len], "range", -1)
    wide = jnp.concatenate([raw, rim], axis=2)
    level = padded_lanes(compress(wide, filt, blocks), bins + extra)
    all_weights = tap_weights(tap_index, tap_weight)
    all_cos = jnp.cos(beam_phase)
    all_sin = jnp.sin(beam_phase)

    def run_section(level, section, beams):
        start = 2 * beams - 2
        stop = start + 2 * beams
        return merge_section(
            level,
            beams,
            all_weights[section],
            beam_shift[:, start:stop],
            all_cos[:, start:stop],
            all_sin[:, start:stop],
        )

    for section in range(local_sections):
        level = run_section(level, section, 1 << section)
    piece_bins = bins // pulse_count
    need = cross_sections * MARGIN
    flat = level[:, :, : bins + need]
    flat = jnp.pad(flat, ((0, 0), (0, 0), (0, piece_bins - need)))
    head = flat[:, :, :bins].reshape(parts, local_beams, pulse_count, piece_bins)
    tail = flat[:, :, piece_bins:].reshape(parts, local_beams, pulse_count, piece_bins)[
        :, :, :, :need
    ]
    pieces = jnp.transpose(jnp.concatenate([head, tail], axis=3), (0, 2, 1, 3))
    level = lax.all_to_all(pieces, "pulse", split_axis=1, concat_axis=1, tiled=True)
    level = padded_lanes(level.reshape(parts, pulse_count * local_beams, piece_bins + need), piece_bins + need)
    for bit in range(cross_sections):
        section = local_sections + bit
        level = run_section(level, section, local_beams << bit)
    level = level[..., :piece_bins].reshape(parts, pulse_count, local_beams, piece_bins)
    level = lax.all_to_all(level, "pulse", split_axis=1, concat_axis=3, tiled=True)
    return level.reshape(parts, local_beams, bins)


def solution(mesh):
    return jax.shard_map(
        on_device,
        mesh=mesh,
        in_specs=(P(None, "pulse", "range"), P(), P(), P(), P(), P()),
        out_specs=P(None, "pulse", "range"),
        check_vma=False,
    )
```

profile of v0, /device:TPU:0, one launch (start us, length us, event | category | flops | bytes accessed | tf_op | source)
XLA Modules:
  0.0 141.1 jit_solution(4059674725883745514)
XLA Ops:
  0.0 0.8 slice.256
  0.8 1.3 collective-permute-start
  2.8 0.8 and_convert_fusion.18
  3.5 0.8 and_convert_fusion.15
  4.3 0.8 fusion.26
  5.2 0.8 and_convert_fusion.12
  6.2 0.8 and_convert_fusion.9
  7.1 0.8 and_convert_fusion.6
  8.0 0.8 and_convert_fusion.3
  8.7 0.8 and_convert_fusion
  9.5 0.8 slice_reduce_fusion
  18.1 0.8 fusion
  19.5 0.9 pad_maximum_fusion.10.kid_ref
  20.3 0.7 broadcast_in_dim.34.table_ref
  21.0 4.6 %shard_map.64 = f32[2,2,8,4224]{3,2,1,0:T(8,128)} custom-call(f32[2,8]{1,0:T(2,128)} %bitcast.187, f32[2,2,8,4224]{3,2,1,0:T(8,128)} %pad_maximum_fusion.10.kid_ref, f32[5,2,2,8,128]{4,3,2,1,0:T(8,128)} %broadcast_in_dim.34.table_ref), custom_call_target="tpu_custom_call" | custom-call | flops 8110080 | bytes 1081344 | tf_op jit(solution)/shard_map/pallas_call | solution.py:95
  25.6 1.1 fusion.22
  28.5 0.9 pad_maximum_fusion.11.kid_ref
  29.3 0.7 broadcast_in_dim.62.table_ref
  30.0 4.6 %shard_map.65 = f32[2,2,8,4224]{3,2,1,0:T(8,128)} custom-call(f32[2,8]{1,0:T(2,128)} %bitcast.186, f32[2,2,8,4224]{3,2,1,0:T(8,128)} %pad_maximum_fusion.11.kid_ref, f32[5,2,2,8,128]{4,3,2,1,0:T(8,128)} %broadcast_in_dim.62.table_ref), custom_call_target="tpu_custom_call" | custom-call | flops 8110080 | bytes 1081344 | tf_op jit(solution)/shard_map/pallas_call | solution.py:95
  34.6 1.1 fusion.21
  36.3 1.0 pad_maximum_fusion.13.kid_ref
  37.4 0.7 broadcast_in_dim.63.table_ref
  38.1 4.6 %shard_map.66 = f32[2,2,8,4224]{3,2,1,0:T(8,128)} custom-call(f32[2,8]{1,0:T(2,128)} %bitcast.185, f32[2,2,8,4224]{3,2,1,0:T(8,128)} %pad_maximum_fusion.13.kid_ref, f32[5,2,2,8,128]{4,3,2,1,0:T(8,128)} %broadcast_in_dim.63.table_ref), custom_call_target="tpu_custom_call" | custom-call | flops 8110080 | bytes 1081344 | tf_op jit(solution)/shard_map/pallas_call | solution.py:95
  42.7 1.1 fusion.19
  44.3 0.9 pad_maximum_fusion.15.kid_ref
  45.9 4.6 %shard_map.67 = f32[2,2,8,4224]{3,2,1,0:T(8,128)} custom-call(f32[2,8]{1,0:T(2,128)} %bitcast.184, f32[2,2,8,4224]{3,2,1,0:T(8,128)} %pad_maximum_fusion.15.kid_ref, f32[5,2,2,8,128]{4,3,2,1,0:T(8,128)} %broadcast_in_dim.65.table_ref), custom_call_target="tpu_custom_call" | custom-call | flops 8110080 | bytes 1081344 | tf_op jit(solution)/shard_map/pallas_call | solution.py:95
  50.5 1.1 slice_bitcast_fusion.7
  52.0 1.0 maximum_bitcast_fusion.2
  53.0 7.4 %all-to-all-start = ((f32[2,16,16,316]{3,2,0,1:T(8,128)}), f32[2,16,16,316]{3,2,0,1:T(8,128)S(1)}, u32[]{:S(2)}, u32[]{:S(2)}) async-start(f32[2,16,16,316]{3,2,0,1:T(8,128)} %maximum_bitcast_fusion.2), calls=%async_computation | async-start | bytes 1572864 | tf_op jit(solution)/shard_map/all_to_all | solution.py:182
  60.6 18.5 %all-to-all-done = f32[2,16,16,316]{3,2,0,1:T(8,128)S(1)} async-done(((f32[2,16,16,316]{3,2,0,1:T(8,128)}), f32[2,16,16,316]{3,2,0,1:T(8,128)S(1)}, u32[]{:S(2)}, u32[]{:S(2)}) %all-to-all-start) | async-done | bytes 647200 | tf_op jit(solution)/shard_map/all_to_all | solution.py:182
  79.3 0.9 pad_maximum_fusion.1.kid_ref
  80.2 1.5 %broadcast_in_dim.66.table_ref = f32[5,2,2,128,128]{4,3,2,1,0:T(8,128)} broadcast(f32[5,2,2,128]{3,2,1,0:T(2,128)S(1)} %tile.78), dimensions={0,1,2,3} | broadcast | bytes 1320960 | tf_op jit(solution)/shard_map/broadcast_in_dim | solution.py:127
  81.7 6.4 %shard_map.68 = f32[2,2,128,384]{3,2,1,0:T(8,128)} custom-call(f32[2,8]{1,0:T(2,128)} %bitcast.183, f32[2,2,128,384]{3,2,1,0:T(8,128)} %pad_maximum_fusion.1.kid_ref, f32[5,2,2,128,128]{4,3,2,1,0:T(8,128)} %broadcast_in_dim.66.table_ref), custom_call_target="tpu_custom_call" | custom-call | flops 11796480 | bytes 1572864 | tf_op jit(solution)/shard_map/pallas_call | solution.py:95
  88.1 1.2 fusion.16
  89.4 0.9 pad_maximum_fusion.3.kid_ref
  90.4 1.5 %broadcast_in_dim.67.table_ref = f32[5,2,2,128,128]{4,3,2,1,0:T(8,128)} broadcast(f32[5,2,2,128]{3,2,1,0:T(2,128)S(1)} %tile.81), dimensions={0,1,2,3} | broadcast | bytes 1320960 | tf_op jit(solution)/shard_map/broadcast_in_dim | solution.py:127
  91.8 6.4 %shard_map.69 = f32[2,2,128,384]{3,2,1,0:T(8,128)} custom-call(f32[2,8]{1,0:T(2,128)} %bitcast.182, f32[2,2,128,384]{3,2,1,0:T(8,128)} %pad_maximum_fusion.3.kid_ref, f32[5,2,2,128,128]{4,3,2,1,0:T(8,128)} %broadcast_in_dim.67.table_ref), custom_call_target="tpu_custom_call" | custom-call | flops 11796480 | bytes 1572864 | tf_op jit(solution)/shard_map/pallas_call | solution.py:95
  98.3 1.2 fusion.14
  99.6 0.9 pad_maximum_fusion.5.kid_ref
  100.5 1.5 %broadcast_in_dim.68.table_ref = f32[5,2,2,128,128]{4,3,2,1,0:T(8,128)} broadcast(f32[5,2,2,128]{3,2,1,0:T(2,128)S(1)} %tile.84), dimensions={0,1,2,3} | broadcast | bytes 1320960 | tf_op jit(solution)/shard_map/broadcast_in_dim | solution.py:127
  102.0 6.4 %shard_map.70 = f32[2,2,128,384]{3,2,1,0:T(8,128)} custom-call(f32[2,8]{1,0:T(2,128)} %bitcast.181, f32[2,2,128,384]{3,2,1,0:T(8,128)} %pad_maximum_fusion.5.kid_ref, f32[5,2,2,128,128]{4,3,2,1,0:T(8,128)} %broadcast_in_dim.68.table_ref), custom_call_target="tpu_custom_call" | custom-call | flops 11796480 | bytes 1572864 | tf_op jit(solution)/shard_map/pallas_call | solution.py:95
  108.4 1.2 fusion.12
  109.7 0.9 pad_maximum_fusion.7.kid_ref
  110.7 1.5 %broadcast_in_dim.70.table_ref = f32[5,2,2,128,128]{4,3,2,1,0:T(8,128)} broadcast(f32[5,2,2,128]{3,2,1,0:T(2,128)S(1)} %bitcast.174), dimensions={0,1,2,3} | broadcast | bytes 1320960 | tf_op jit(solution)/shard_map/broadcast_in_dim | solution.py:127
  112.2 6.6 %shard_map.71 = f32[2,2,128,384]{3,2,1,0:T(8,128)} custom-call(f32[2,8]{1,0:T(2,128)} %bitcast.180, f32[2,2,128,384]{3,2,1,0:T(8,128)} %pad_maximum_fusion.7.kid_ref, f32[5,2,2,128,128]{4,3,2,1,0:T(8,128)} %broadcast_in_dim.70.table_ref), custom_call_target="tpu_custom_call" | custom-call | flops 11796480 | bytes 1572864 | tf_op jit(solution)/shard_map/pallas_call | solution.py:95
  118.8 1.2 slice_bitcast_fusion.3
  120.2 19.7 %all_to_all.20 = f32[2,16,16,256]{3,2,0,1:T(8,128)S(1)} all-to-all(f32[2,16,16,256]{3,2,0,1:T(8,128)S(1)} %copy.177), channel_id=1, replica_groups=mesh['pulse'=16,'range'=2] {'pulse'}, dimensions={1} | all-to-all | bytes 1048576 | tf_op jit(solution)/shard_map/all_to_all | solution.py:188
  140.2 0.9 reshape.154
  (173 shorter events, 14.7 us)
Async XLA Ops:
  0.8 16.6 %collective-permute-start = (bf16[2,16,768]{2,1,0:T(8,128)(2,1)S(1)}, bf16[2,16,768]{2,1,0:T(8,128)(2,1)S(1)}, u32[]{:S(2)}, u32[]{:S(2)}) collective-permute-start(bf16[2,16,768]{2,1,0:T(8,128)(2,1)S(1)} %slice.256), channel_id=1, source_target_pairs={{1,0},{3,2},{5,4},{7,6},{9,8},{11,10},{13,12},{15,14},{17,16},{19,... | collective-permute-start | bytes 147464 | tf_op jit(solution)/shard_map/ppermute | solution.py:21
  11.0 0.7 copy-start.1
  11.0 0.7 copy-start.2
  11.1 0.7 copy-start.3
  15.8 1.6 %copy-start = (bf16[2,16,4096]{2,1,0:T(8,128)(2,1)S(1)}, bf16[2,16,4096]{2,1,0:T(8,128)(2,1)}, u32[]{:S(2)}) copy-start(bf16[2,16,4096]{2,1,0:T(8,128)(2,1)} %param.6) | copy-start | bytes 786436
  53.0 26.1 %all-to-all-start = ((f32[2,16,16,316]{3,2,0,1:T(8,128)}), f32[2,16,16,316]{3,2,0,1:T(8,128)S(1)}, u32[]{:S(2)}, u32[]{:S(2)}) async-start(f32[2,16,16,316]{3,2,0,1:T(8,128)} %maximum_bitcast_fusion.2), calls=%async_computation | async-start | bytes 1572864 | tf_op jit(solution)/shard_map/all_to_all | solution.py:182
where the time goes:
time: 142 us; the launch traced here: 141 us
  Pallas kernels  44.1 us (31%)
  local copies, waits for them, and re-layouts  32.9 us (23%)
  blocking collectives  19.7 us (14%)
  waiting for transfers between devices  18.5 us (13%)
  other arithmetic  15.7 us (11%)
  starting transfers between devices  8.67 us (6%)
    pallas_call x8, Pallas kernels, merge_call(): pl.pallas_call(merge_kernel, out_shape=jax.ShapeDtypeStruct((2, 2, rows,...  44.1 us
    all_to_all x1, blocking collectives, on_device(): lax.all_to_all(level, 'pulse', split_axis=1, concat_axis=3, tiled=True)  19.7 us
    all_to_all x1, waiting for transfers between devices, on_device(): lax.all_to_all(pieces, 'pulse', split_axis=1, concat_axis=1, tiled=True)  18.5 us
    broadcast_in_dim x8, local copies, waits for them, and re-layouts, merge_section(): jnp.broadcast_to(per_row(packed, groups)[..., None], (5, 2, 2, rows // 2,...  8.81 us
    all_to_all x1, starting transfers between devices, on_device(): lax.all_to_all(pieces, 'pulse', split_axis=1, concat_axis=1, tiled=True)  7.39 us
    another operation x8, other arithmetic, merge_section(): jnp.stack([pairs[:, :, c].reshape(parts, rows // 2, length) for c in rang...  7.37 us
    slice x6, local copies, waits for them, and re-layouts, merge_section(): out[h].reshape(parts, groups, beams, length)  6.71 us
    convert_element_type x7, other arithmetic, merge_section(): bits = [(chosen >> bit & 1).astype(jnp.float32) for bit in range(3)]  5.28 us
  transfers between devices with their start and end apart: 2, of which 1 were waited for; matrix products, arithmetic and copies ran while one was open for 11% of the time, Pallas kernels for 0%

commit v1 on v0

--- a/solution.py
+++ b/solution.py
@@ -117,13 +117,11 @@
     return jnp.tile(halves, (1,) * (halves.ndim - 1) + (groups,))
 
 
-def merge_section(level, beams, weights, chosen, cosine, sine):
+def merge_section(level, beams, weights, packed):
     parts, rows, length = level.shape
     groups = rows // (2 * beams)
     pairs = level.reshape(parts, groups, 2, beams, length)
     kids = jnp.stack([pairs[:, :, c].reshape(parts, rows // 2, length) for c in range(2)])
-    bits = [((chosen >> bit) & 1).astype(jnp.float32) for bit in range(3)]
-    packed = jnp.stack(bits + [cosine, sine])
     table = jnp.broadcast_to(per_row(packed, groups)[..., None], (5, 2, 2, rows // 2, LANE))
     out = merge_call(weights, kids, table)
     merged = jnp.stack([out[h].reshape(parts, groups, beams, length) for h in range(2)], axis=2)
@@ -153,8 +151,8 @@
     wide = jnp.concatenate([raw, rim], axis=2)
     level = padded_lanes(compress(wide, filt, blocks), bins + extra)
     all_weights = tap_weights(tap_index, tap_weight)
-    all_cos = jnp.cos(beam_phase)
-    all_sin = jnp.sin(beam_phase)
+    bits = [((beam_shift >> bit) & 1).astype(jnp.float32) for bit in range(3)]
+    all_rows = jnp.stack(bits + [jnp.cos(beam_phase), jnp.sin(beam_phase)])
 
     def run_section(level, section, beams):
         start = 2 * beams - 2
@@ -163,9 +161,7 @@
             level,
             beams,
             all_weights[section],
-            beam_shift[:, start:stop],
-            all_cos[:, start:stop],
-            all_sin[:, start:stop],
+            all_rows[:, :, start:stop],
         )
 
     for section in range(local_sections):

time: 142 us -> 132 us (0.930)
  other arithmetic: 15.7 us -> 9.55 us
  local copies, waits for them, and re-layouts: 32.9 us -> 29.5 us
    convert_element_type x7 -> x0, other arithmetic: 5.28 us -> none  [merge_section(): bits = [(chosen >> bit & 1).astype(jnp.float32) for bit in range(3)]]
    another operation x43 -> x1, local copies, waits for them, and re-layouts: 2.67 us -> 0.08 us  [on_device(): all_rows = jnp.stack(bits + [jnp.cos(beam_phase), jnp.sin(beam_phase)])]
    broadcast_in_dim x8 -> x10, local copies, waits for them, and re-layouts: 8.81 us -> 8.91 us  [merge_section(): jnp.broadcast_to(per_row(packed, groups)[..., None], (5, 2, 2, rows // 2,...]
  transfers between devices with their start and end apart: 2 -> 2, of which waited for: 1 -> 1; matrix products, arithmetic and copies ran while one was open for 11% -> 4% of each run, Pallas kernels for 0% -> 0%
where the time goes in v1:
time: 132 us; the launch traced here: 131 us
  Pallas kernels  44.2 us (33%)
  local copies, waits for them, and re-layouts  29.5 us (22%)
  blocking collectives  19.7 us (15%)
  waiting for transfers between devices  17.8 us (13%)
  other arithmetic  9.55 us (7%)
  starting transfers between devices  8.67 us (7%)
    pallas_call x8, Pallas kernels, merge_call(): pl.pallas_call(merge_kernel, out_shape=jax.ShapeDtypeStruct((2, 2, rows,...  44.2 us
    all_to_all x1, blocking collectives, on_device(): lax.all_to_all(level, 'pulse', split_axis=1, concat_axis=3, tiled=True)  19.7 us
    all_to_all x1, waiting for transfers between devices, on_device(): lax.all_to_all(pieces, 'pulse', split_axis=1, concat_axis=1, tiled=True)  17.8 us
    broadcast_in_dim x10, local copies, waits for them, and re-layouts, merge_section(): jnp.broadcast_to(per_row(packed, groups)[..., None], (5, 2, 2, rows // 2,...  8.91 us
    all_to_all x1, starting transfers between devices, on_device(): lax.all_to_all(pieces, 'pulse', split_axis=1, concat_axis=1, tiled=True)  7.39 us
    another operation x8, other arithmetic, merge_section(): jnp.stack([pairs[:, :, c].reshape(parts, rows // 2, length) for c in rang...  7.19 us
    slice x6, local copies, waits for them, and re-layouts, merge_section(): out[h].reshape(parts, groups, beams, length)  6.71 us
    another operation x13, local copies, waits for them, and re-layouts, merge_section(): jnp.stack([out[h].reshape(parts, groups, beams, length) for h in range(2)...  3.69 us
  transfers between devices with their start and end apart: 2, of which 1 were waited for; matrix products, arithmetic and copies ran while one was open for 4% of the time, Pallas kernels for 0%

profile of v1, /device:TPU:0, one launch (start us, length us, event | category | flops | bytes accessed | tf_op | source)
XLA Modules:
  0.0 130.9 jit_solution(14572905424675932628)
XLA Ops:
  0.0 0.8 slice.208
  0.8 1.3 collective-permute-start
  2.1 0.8 slice_reduce_fusion
  2.9 0.7 tile.69
  3.7 0.4 reshape.82
  4.5 0.6 fusion.25
  5.6 0.7 tile.67
  6.3 0.4 reshape.81
  8.0 0.8 fusion
  9.4 0.8 pad_maximum_fusion.10.kid_ref
  10.2 0.7 broadcast_in_dim.34.table_ref
  10.9 4.5 %shard_map.64 = f32[2,2,8,4224]{3,2,1,0:T(8,128)} custom-call(f32[2,8]{1,0:T(2,128)} %bitcast.161, f32[2,2,8,4224]{3,2,1,0:T(8,128)} %pad_maximum_fusion.10.kid_ref, f32[5,2,2,8,128]{4,3,2,1,0:T(8,128)} %broadcast_in_dim.34.table_ref), custom_call_target="tpu_custom_call" | custom-call | flops 8110080 | bytes 1081344 | tf_op jit(solution)/shard_map/pallas_call | solution.py:95
  15.5 1.1 fusion.22
  17.5 0.5 fusion.10
  18.3 0.8 pad_maximum_fusion.11.kid_ref
  19.2 0.7 broadcast_in_dim.62.table_ref
  19.9 4.5 %shard_map.65 = f32[2,2,8,4224]{3,2,1,0:T(8,128)} custom-call(f32[2,8]{1,0:T(2,128)} %bitcast.160, f32[2,2,8,4224]{3,2,1,0:T(8,128)} %pad_maximum_fusion.11.kid_ref, f32[5,2,2,8,128]{4,3,2,1,0:T(8,128)} %broadcast_in_dim.62.table_ref), custom_call_target="tpu_custom_call" | custom-call | flops 8110080 | bytes 1081344 | tf_op jit(solution)/shard_map/pallas_call | solution.py:95
  24.5 1.1 fusion.21
  26.2 0.8 pad_maximum_fusion.13.kid_ref
  27.0 0.7 broadcast_in_dim.63.table_ref
  27.8 4.7 %shard_map.66 = f32[2,2,8,4224]{3,2,1,0:T(8,128)} custom-call(f32[2,8]{1,0:T(2,128)} %bitcast.159, f32[2,2,8,4224]{3,2,1,0:T(8,128)} %pad_maximum_fusion.13.kid_ref, f32[5,2,2,8,128]{4,3,2,1,0:T(8,128)} %broadcast_in_dim.63.table_ref), custom_call_target="tpu_custom_call" | custom-call | flops 8110080 | bytes 1081344 | tf_op jit(solution)/shard_map/pallas_call | solution.py:95
  32.4 1.1 fusion.19
  34.1 0.8 pad_maximum_fusion.15.kid_ref
  34.9 0.7 broadcast_in_dim.65.table_ref
  35.7 4.5 %shard_map.67 = f32[2,2,8,4224]{3,2,1,0:T(8,128)} custom-call(f32[2,8]{1,0:T(2,128)} %bitcast.158, f32[2,2,8,4224]{3,2,1,0:T(8,128)} %pad_maximum_fusion.15.kid_ref, f32[5,2,2,8,128]{4,3,2,1,0:T(8,128)} %broadcast_in_dim.65.table_ref), custom_call_target="tpu_custom_call" | custom-call | flops 8110080 | bytes 1081344 | tf_op jit(solution)/shard_map/pallas_call | solution.py:95
  40.2 1.1 slice_bitcast_fusion.7
  41.8 1.0 maximum_bitcast_fusion.2
  42.7 7.4 %all-to-all-start = ((f32[2,16,16,316]{3,2,0,1:T(8,128)}), f32[2,16,16,316]{3,2,0,1:T(8,128)S(1)}, u32[]{:S(2)}, u32[]{:S(2)}) async-start(f32[2,16,16,316]{3,2,0,1:T(8,128)} %maximum_bitcast_fusion.2), calls=%async_computation | async-start | bytes 1572864 | tf_op jit(solution)/shard_map/all_to_all | solution.py:178
  51.0 17.8 %all-to-all-done = f32[2,16,16,316]{3,2,0,1:T(8,128)S(1)} async-done(((f32[2,16,16,316]{3,2,0,1:T(8,128)}), f32[2,16,16,316]{3,2,0,1:T(8,128)S(1)}, u32[]{:S(2)}, u32[]{:S(2)}) %all-to-all-start) | async-done | bytes 647200 | tf_op jit(solution)/shard_map/all_to_all | solution.py:178
  69.0 0.9 pad_maximum_fusion.1.kid_ref
  70.0 1.5 %broadcast_in_dim.66.table_ref = f32[5,2,2,128,128]{4,3,2,1,0:T(8,128)} broadcast(f32[5,2,2,128]{3,2,1,0:T(2,128)S(1)} %tile.78), dimensions={0,1,2,3} | broadcast | bytes 1320960 | tf_op jit(solution)/shard_map/broadcast_in_dim | solution.py:125
  71.5 6.4 %shard_map.68 = f32[2,2,128,384]{3,2,1,0:T(8,128)} custom-call(f32[2,8]{1,0:T(2,128)} %bitcast.157, f32[2,2,128,384]{3,2,1,0:T(8,128)} %pad_maximum_fusion.1.kid_ref, f32[5,2,2,128,128]{4,3,2,1,0:T(8,128)} %broadcast_in_dim.66.table_ref), custom_call_target="tpu_custom_call" | custom-call | flops 11796480 | bytes 1572864 | tf_op jit(solution)/shard_map/pallas_call | solution.py:95
  77.9 1.2 fusion.16
  79.2 0.9 pad_maximum_fusion.3.kid_ref
  80.1 1.5 %broadcast_in_dim.67.table_ref = f32[5,2,2,128,128]{4,3,2,1,0:T(8,128)} broadcast(f32[5,2,2,128]{3,2,1,0:T(2,128)S(1)} %tile.81), dimensions={0,1,2,3} | broadcast | bytes 1320960 | tf_op jit(solution)/shard_map/broadcast_in_dim | solution.py:125
  81.6 6.4 %shard_map.69 = f32[2,2,128,384]{3,2,1,0:T(8,128)} custom-call(f32[2,8]{1,0:T(2,128)} %bitcast.156, f32[2,2,128,384]{3,2,1,0:T(8,128)} %pad_maximum_fusion.3.kid_ref, f32[5,2,2,128,128]{4,3,2,1,0:T(8,128)} %broadcast_in_dim.67.table_ref), custom_call_target="tpu_custom_call" | custom-call | flops 11796480 | bytes 1572864 | tf_op jit(solution)/shard_map/pallas_call | solution.py:95
  88.0 1.2 fusion.14
  89.3 0.9 pad_maximum_fusion.5.kid_ref
  90.3 1.5 %broadcast_in_dim.68.table_ref = f32[5,2,2,128,128]{4,3,2,1,0:T(8,128)} broadcast(f32[5,2,2,128]{3,2,1,0:T(2,128)S(1)} %tile.84), dimensions={0,1,2,3} | broadcast | bytes 1320960 | tf_op jit(solution)/shard_map/broadcast_in_dim | solution.py:125
  91.7 6.4 %shard_map.70 = f32[2,2,128,384]{3,2,1,0:T(8,128)} custom-call(f32[2,8]{1,0:T(2,128)} %bitcast.155, f32[2,2,128,384]{3,2,1,0:T(8,128)} %pad_maximum_fusion.5.kid_ref, f32[5,2,2,128,128]{4,3,2,1,0:T(8,128)} %broadcast_in_dim.68.table_ref), custom_call_target="tpu_custom_call" | custom-call | flops 11796480 | bytes 1572864 | tf_op jit(solution)/shard_map/pallas_call | solution.py:95
  98.2 1.2 fusion.12
  99.5 0.9 pad_maximum_fusion.7.kid_ref
  100.5 1.5 %broadcast_in_dim.70.table_ref = f32[5,2,2,128,128]{4,3,2,1,0:T(8,128)} broadcast(f32[5,2,2,128]{3,2,1,0:T(2,128)S(1)} %broadcast_in_dim.69), dimensions={0,1,2,3} | broadcast | bytes 1320960 | tf_op jit(solution)/shard_map/broadcast_in_dim | solution.py:125
  101.9 6.6 %shard_map.71 = f32[2,2,128,384]{3,2,1,0:T(8,128)} custom-call(f32[2,8]{1,0:T(2,128)} %bitcast.154, f32[2,2,128,384]{3,2,1,0:T(8,128)} %pad_maximum_fusion.7.kid_ref, f32[5,2,2,128,128]{4,3,2,1,0:T(8,128)} %broadcast_in_dim.70.table_ref), custom_call_target="tpu_custom_call" | custom-call | flops 11796480 | bytes 1572864 | tf_op jit(solution)/shard_map/pallas_call | solution.py:95
  108.6 1.2 slice_bitcast_fusion.3
  109.9 19.7 %all_to_all.20 = f32[2,16,16,256]{3,2,0,1:T(8,128)S(1)} all-to-all(f32[2,16,16,256]{3,2,0,1:T(8,128)S(1)} %copy.128), channel_id=1, replica_groups=mesh['pulse'=16,'range'=2] {'pulse'}, dimensions={1} | all-to-all | bytes 1048576 | tf_op jit(solution)/shard_map/all_to_all | solution.py:184
  129.7 0.3 copy.129
  130.0 0.9 reshape.91
  (102 shorter events, 7.2 us)
Async XLA Ops:
  0.8 6.5 %collective-permute-start = (bf16[2,16,768]{2,1,0:T(8,128)(2,1)S(1)}, bf16[2,16,768]{2,1,0:T(8,128)(2,1)S(1)}, u32[]{:S(2)}, u32[]{:S(2)}) collective-permute-start(bf16[2,16,768]{2,1,0:T(8,128)(2,1)S(1)} %slice.208), channel_id=1, source_target_pairs={{1,0},{3,2},{5,4},{7,6},{9,8},{11,10},{13,12},{15,14},{17,16},{19,... | collective-permute-start | bytes 147464 | tf_op jit(solution)/shard_map/ppermute | solution.py:21
  3.7 0.7 copy-start.1
  3.7 0.7 copy-start.3
  3.7 0.7 copy-start.4
  3.7 1.4 %copy-start.2 = (f32[2,510]{1,0:T(2,128)S(1)}, f32[2,510]{1,0:T(2,128)}, u32[]{:S(2)}) copy-start(f32[2,510]{1,0:T(2,128)} %param.11) | copy-start | bytes 12244
  6.2 1.1 copy-start
  42.7 26.1 %all-to-all-start = ((f32[2,16,16,316]{3,2,0,1:T(8,128)}), f32[2,16,16,316]{3,2,0,1:T(8,128)S(1)}, u32[]{:S(2)}, u32[]{:S(2)}) async-start(f32[2,16,16,316]{3,2,0,1:T(8,128)} %maximum_bitcast_fusion.2), calls=%async_computation | async-start | bytes 1572864 | tf_op jit(solution)/shard_map/all_to_all | solution.py:178

commit v2 on v1

--- a/solution.py
+++ b/solution.py
@@ -1,3 +1,5 @@
+import functools
+
 import jax
 import jax.numpy as jnp
 from jax import lax
@@ -55,7 +57,7 @@
     return jnp.stack([real_part, imag_part])
 
 
-def merge_kernel(weight_ref, kid_ref, table_ref, out_ref):
+def merge_kernel(beams, chained, weight_ref, kid_ref, table_ref, out_ref):
     length = kid_ref.shape[-1]
     reach = MARGIN - MAXOFF + 1
     acc = [[None, None], [None, None]]
@@ -83,18 +85,28 @@
                 acc[half] = [real_part, imag_part]
             else:
                 acc[half] = [acc[half][0] + real_part, acc[half][1] + imag_part]
+    rows = kid_ref.shape[2]
     for half in range(2):
         for part in range(2):
-            out_ref[half, part] = acc[half][part] * half_root
-
-
-def merge_call(weights, kids, table):
+            value = acc[half][part] * half_root
+            for group in range(rows // beams):
+                block = value[group * beams : (group + 1) * beams]
+                if chained:
+                    start = (group // 2) * 2 * beams + half * beams
+                    out_ref[group % 2, part, start : start + beams] = block
+                else:
+                    start = group * 2 * beams + half * beams
+                    out_ref[part, start : start + beams] = block
+
+
+def merge_call(beams, chained, weights, kids, table):
     _, _, rows, length = kids.shape
     vmem = pltpu.VMEM
     elems = 2 * 2 * rows * length
+    shape = (2, 2, rows, length) if chained else (2, 2 * rows, length)
     return pl.pallas_call(
-        merge_kernel,
-        out_shape=jax.ShapeDtypeStruct((2, 2, rows, length), jnp.float32),
+        functools.partial(merge_kernel, beams, chained),
+        out_shape=jax.ShapeDtypeStruct(shape, jnp.float32),
         in_specs=[
             pl.BlockSpec(memory_space=pltpu.SMEM),
             pl.BlockSpec(memory_space=vmem),
@@ -117,15 +129,18 @@
     return jnp.tile(halves, (1,) * (halves.ndim - 1) + (groups,))
 
 
-def merge_section(level, beams, weights, packed):
+def split_kids(level, beams):
     parts, rows, length = level.shape
     groups = rows // (2 * beams)
     pairs = level.reshape(parts, groups, 2, beams, length)
-    kids = jnp.stack([pairs[:, :, c].reshape(parts, rows // 2, length) for c in range(2)])
-    table = jnp.broadcast_to(per_row(packed, groups)[..., None], (5, 2, 2, rows // 2, LANE))
-    out = merge_call(weights, kids, table)
-    merged = jnp.stack([out[h].reshape(parts, groups, beams, length) for h in range(2)], axis=2)
-    return merged.reshape(parts, rows, length)
+    return jnp.stack([pairs[:, :, c].reshape(parts, rows // 2, length) for c in range(2)])
+
+
+def merge_section(kids, beams, chained, weights, packed):
+    rows = kids.shape[2]
+    groups = rows // beams
+    table = jnp.broadcast_to(per_row(packed, groups)[..., None], (5, 2, 2, rows, LANE))
+    return merge_call(beams, chained, weights, kids, table)
 
 
 def padded_lanes(level, width):
@@ -154,18 +169,14 @@
     bits = [((beam_shift >> bit) & 1).astype(jnp.float32) for bit in range(3)]
     all_rows = jnp.stack(bits + [jnp.cos(beam_phase), jnp.sin(beam_phase)])
 
-    def run_section(level, section, beams):
+    def run_section(kids, section, beams, chained):
         start = 2 * beams - 2
         stop = start + 2 * beams
-        return merge_section(
-            level,
-            beams,
-            all_weights[section],
-            all_rows[:, :, start:stop],
-        )
-
+        return merge_section(kids, beams, chained, all_weights[section], all_rows[:, :, start:stop])
+
+    level = split_kids(level, 1)
     for section in range(local_sections):
-        level = run_section(level, section, 1 << section)
+        level = run_section(level, section, 1 << section, section < local_sections - 1)
     piece_bins = bins // pulse_count
     need = cross_sections * MARGIN
     flat = level[:, :, : bins + need]
@@ -177,9 +188,10 @@
     pieces = jnp.transpose(jnp.concatenate([head, tail], axis=3), (0, 2, 1, 3))
     level = lax.all_to_all(pieces, "pulse", split_axis=1, concat_axis=1, tiled=True)
     level = padded_lanes(level.reshape(parts, pulse_count * local_beams, piece_bins + need), piece_bins + need)
+    level = split_kids(level, local_beams)
     for bit in range(cross_sections):
         section = local_sections + bit
-        level = run_section(level, section, local_beams << bit)
+        level = run_section(level, section, local_beams << bit, bit < cross_sections - 1)
     level = level[..., :piece_bins].reshape(parts, pulse_count, local_beams, piece_bins)
     level = lax.all_to_all(level, "pulse", split_axis=1, concat_axis=3, tiled=True)
     return level.reshape(parts, local_beams, bins)

time: 132 us -> 116 us (0.88)
  local copies, waits for them, and re-layouts: 29.5 us -> 20.5 us
  other arithmetic: 9.55 us -> 3.01 us
    slice x11 -> x2, local copies, waits for them, and re-layouts: 6.96 us -> 0.11 us  [split_kids(): pairs[:, :, c].reshape(parts, rows // 2, length)]
    another operation x15 -> x2, other arithmetic: 8.27 us -> 1.77 us  [split_kids(): jnp.stack([pairs[:, :, c].reshape(parts, rows // 2, length) for c in rang...]
    another operation x21 -> x1, local copies, waits for them, and re-layouts: 4.42 us -> 0.04 us  [split_kids(): jnp.stack([pairs[:, :, c].reshape(parts, rows // 2, length) for c in rang...]
  transfers between devices with their start and end apart: 2 -> 2, of which waited for: 1 -> 1; matrix products, arithmetic and copies ran while one was open for 4% -> 5% of each run, Pallas kernels for 0% -> 0%
where the time goes in v2:
time: 116 us; the launch traced here: 115 us
  Pallas kernels  44.5 us (38%)
  local copies, waits for them, and re-layouts  20.5 us (18%)
  blocking collectives  19.7 us (17%)
  waiting for transfers between devices  17.8 us (15%)
  starting transfers between devices  8.67 us (7%)
  other arithmetic  3.01 us (3%)
    pallas_call x8, Pallas kernels, merge_call(): pl.pallas_call(functools.partial(merge_kernel, beams, chained), out_shape...  44.5 us
    all_to_all x1, blocking collectives, on_device(): lax.all_to_all(level, 'pulse', split_axis=1, concat_axis=3, tiled=True)  19.7 us
    all_to_all x1, waiting for transfers between devices, on_device(): lax.all_to_all(pieces, 'pulse', split_axis=1, concat_axis=1, tiled=True)  17.8 us
    broadcast_in_dim x10, local copies, waits for them, and re-layouts, merge_section(): jnp.broadcast_to(per_row(packed, groups)[..., None], (5, 2, 2, rows, LANE))  8.98 us
    all_to_all x1, starting transfers between devices, on_device(): lax.all_to_all(pieces, 'pulse', split_axis=1, concat_axis=1, tiled=True)  7.39 us
  transfers between devices with their start and end apart: 2, of which 1 were waited for; matrix products, arithmetic and copies ran while one was open for 5% of the time, Pallas kernels for 0%

profile of v2, /device:TPU:0, one launch (start us, length us, event | category | flops | bytes accessed | tf_op | source)
XLA Modules:
  0.0 115.4 jit_solution(7105488915534303292)
XLA Ops:
  0.0 0.8 slice.124
  0.8 1.3 %collective-permute-start = (bf16[2,16,768]{2,1,0:T(8,128)(2,1)S(1)}, bf16[2,16,768]{2,1,0:T(8,128)(2,1)S(1)}, u32[]{:S(2)}, u32[]{:S(2)}) collective-permute-start(bf16[2,16,768]{2,1,0:T(8,128)(2,1)S(1)} %slice.124), channel_id=1, source_target_pairs={{1,0},{3,2},{5,4},{7,6},{9,8},{11,10},{13,12},{15,14},{17,16},{19,... | collective-permute-start | bytes 147464 | tf_op jit(solution)/shard_map/ppermute | solution.py:23
  2.1 0.8 slice_reduce_fusion
  2.9 0.7 tile.69
  3.7 0.4 reshape.72
  4.1 0.2 copy.52
  4.5 0.6 fusion.15
  5.6 0.7 tile.67
  6.3 0.4 reshape.71
  6.7 0.2 copy.51
  6.8 0.1 copy.56
  6.9 0.1 copy.57
  7.1 0.1 tile.75
  7.4 0.2 reshape.70
  7.6 0.2 fusion.14
  7.8 0.1 pad_maximum_fusion
  8.0 0.8 fusion
  9.0 0.3 copy.53
  9.4 0.8 pad_maximum_fusion.3.kid_ref
  10.2 0.7 broadcast_in_dim.34.table_ref
  10.9 4.7 %shard_map.64.kid_ref = f32[2,2,8,4224]{3,2,1,0:T(8,128)} custom-call(f32[2,8]{1,0:T(2,128)} %bitcast.83, f32[2,2,8,4224]{3,2,1,0:T(8,128)} %pad_maximum_fusion.3.kid_ref, f32[5,2,2,8,128]{4,3,2,1,0:T(8,128)} %broadcast_in_dim.34.table_ref), custom_call_target="tpu_custom_call" | custom-call | flops 8110080 | bytes 1081344 | tf_op jit(solution)/shard_map/pallas_call | solution.py:107
  15.7 0.7 broadcast_in_dim.62.table_ref
  16.4 4.6 %shard_map.65.kid_ref = f32[2,2,8,4224]{3,2,1,0:T(8,128)} custom-call(f32[2,8]{1,0:T(2,128)} %bitcast.82, f32[2,2,8,4224]{3,2,1,0:T(8,128)} %shard_map.64.kid_ref, f32[5,2,2,8,128]{4,3,2,1,0:T(8,128)} %broadcast_in_dim.62.table_ref), custom_call_target="tpu_custom_call" | custom-call | flops 8110080 | bytes 1081344 | tf_op jit(solution)/shard_map/pallas_call | solution.py:107
  21.0 0.7 broadcast_in_dim.63.table_ref
  21.7 4.6 %shard_map.66.kid_ref = f32[2,2,8,4224]{3,2,1,0:T(8,128)} custom-call(f32[2,8]{1,0:T(2,128)} %bitcast.81, f32[2,2,8,4224]{3,2,1,0:T(8,128)} %shard_map.65.kid_ref, f32[5,2,2,8,128]{4,3,2,1,0:T(8,128)} %broadcast_in_dim.63.table_ref), custom_call_target="tpu_custom_call" | custom-call | flops 8110080 | bytes 1081344 | tf_op jit(solution)/shard_map/pallas_call | solution.py:107
  26.3 0.7 broadcast_in_dim.65.table_ref
  27.0 4.7 %shard_map.67 = f32[2,16,4224]{2,1,0:T(8,128)} custom-call(f32[2,8]{1,0:T(2,128)} %bitcast.80, f32[2,2,8,4224]{3,2,1,0:T(8,128)} %shard_map.66.kid_ref, f32[5,2,2,8,128]{4,3,2,1,0:T(8,128)} %broadcast_in_dim.65.table_ref), custom_call_target="tpu_custom_call" | custom-call | flops 8110080 | bytes 1081344 | tf_op jit(solution)/shard_map/pallas_call | solution.py:107
  31.7 1.1 slice.177
  33.0 0.2 copy.67
  33.3 1.0 maximum_bitcast_fusion.2
  34.3 7.4 %all-to-all-start = ((f32[2,16,16,316]{3,2,0,1:T(8,128)}), f32[2,16,16,316]{3,2,0,1:T(8,128)S(1)}, u32[]{:S(2)}, u32[]{:S(2)}) async-start(f32[2,16,16,316]{3,2,0,1:T(8,128)} %maximum_bitcast_fusion.2), calls=%async_computation | async-start | bytes 1572864 | tf_op jit(solution)/shard_map/all_to_all | solution.py:189
  42.1 0.1 tile.78
  42.3 0.1 tile.81
  42.5 0.1 tile.84
  42.6 17.8 %all-to-all-done = f32[2,16,16,316]{3,2,0,1:T(8,128)S(1)} async-done(((f32[2,16,16,316]{3,2,0,1:T(8,128)}), f32[2,16,16,316]{3,2,0,1:T(8,128)S(1)}, u32[]{:S(2)}, u32[]{:S(2)}) %all-to-all-start) | async-done | bytes 647200 | tf_op jit(solution)/shard_map/all_to_all | solution.py:189
  60.6 0.9 pad_maximum_fusion.1.kid_ref
  61.5 1.5 %broadcast_in_dim.66.table_ref = f32[5,2,2,128,128]{4,3,2,1,0:T(8,128)} broadcast(f32[5,2,2,128]{3,2,1,0:T(2,128)S(1)} %tile.78), dimensions={0,1,2,3} | broadcast | bytes 1320960 | tf_op jit(solution)/shard_map/broadcast_in_dim | solution.py:142
  63.0 6.4 %shard_map.68.kid_ref = f32[2,2,128,384]{3,2,1,0:T(8,128)} custom-call(f32[2,8]{1,0:T(2,128)} %bitcast.79, f32[2,2,128,384]{3,2,1,0:T(8,128)} %pad_maximum_fusion.1.kid_ref, f32[5,2,2,128,128]{4,3,2,1,0:T(8,128)} %broadcast_in_dim.66.table_ref), custom_call_target="tpu_custom_call" | custom-call | flops 11796480 | bytes 1572864 | tf_op jit(solution)/shard_map/pallas_call | solution.py:107
  69.4 1.5 %broadcast_in_dim.67.table_ref = f32[5,2,2,128,128]{4,3,2,1,0:T(8,128)} broadcast(f32[5,2,2,128]{3,2,1,0:T(2,128)S(1)} %tile.81), dimensions={0,1,2,3} | broadcast | bytes 1320960 | tf_op jit(solution)/shard_map/broadcast_in_dim | solution.py:142
  70.9 6.4 %shard_map.69.kid_ref = f32[2,2,128,384]{3,2,1,0:T(8,128)} custom-call(f32[2,8]{1,0:T(2,128)} %bitcast.78, f32[2,2,128,384]{3,2,1,0:T(8,128)} %shard_map.68.kid_ref, f32[5,2,2,128,128]{4,3,2,1,0:T(8,128)} %broadcast_in_dim.67.table_ref), custom_call_target="tpu_custom_call" | custom-call | flops 11796480 | bytes 1572864 | tf_op jit(solution)/shard_map/pallas_call | solution.py:107
  77.3 1.5 %broadcast_in_dim.68.table_ref = f32[5,2,2,128,128]{4,3,2,1,0:T(8,128)} broadcast(f32[5,2,2,128]{3,2,1,0:T(2,128)S(1)} %tile.84), dimensions={0,1,2,3} | broadcast | bytes 1320960 | tf_op jit(solution)/shard_map/broadcast_in_dim | solution.py:142
  78.8 6.4 %shard_map.70.kid_ref = f32[2,2,128,384]{3,2,1,0:T(8,128)} custom-call(f32[2,8]{1,0:T(2,128)} %bitcast.77, f32[2,2,128,384]{3,2,1,0:T(8,128)} %shard_map.69.kid_ref, f32[5,2,2,128,128]{4,3,2,1,0:T(8,128)} %broadcast_in_dim.68.table_ref), custom_call_target="tpu_custom_call" | custom-call | flops 11796480 | bytes 1572864 | tf_op jit(solution)/shard_map/pallas_call | solution.py:107
  85.3 1.5 %broadcast_in_dim.70.table_ref = f32[5,2,2,128,128]{4,3,2,1,0:T(8,128)} broadcast(f32[5,2,2,128]{3,2,1,0:T(2,128)S(1)} %broadcast_in_dim.69), dimensions={0,1,2,3} | broadcast | bytes 1320960 | tf_op jit(solution)/shard_map/broadcast_in_dim | solution.py:142
  86.8 6.6 %shard_map.71 = f32[2,256,384]{2,1,0:T(8,128)} custom-call(f32[2,8]{1,0:T(2,128)} %bitcast.76, f32[2,2,128,384]{3,2,1,0:T(8,128)} %shard_map.70.kid_ref, f32[5,2,2,128,128]{4,3,2,1,0:T(8,128)} %broadcast_in_dim.70.table_ref), custom_call_target="tpu_custom_call" | custom-call | flops 11796480 | bytes 1572864 | tf_op jit(solution)/shard_map/pallas_call | solution.py:107
  93.4 1.0 slice-done
  94.5 19.7 %all_to_all.20 = f32[2,16,16,256]{3,2,0,1:T(8,128)S(1)} all-to-all(f32[2,16,16,256]{3,2,0,1:T(8,128)S(1)} %copy.61), channel_id=1, replica_groups=mesh['pulse'=16,'range'=2] {'pulse'}, dimensions={1} | all-to-all | bytes 1048576 | tf_op jit(solution)/shard_map/all_to_all | solution.py:196
  114.2 0.3 copy.62
  114.5 0.9 reshape.79
  (62 shorter events, 2.4 us)
Async XLA Ops:
  0.8 6.5 %collective-permute-start = (bf16[2,16,768]{2,1,0:T(8,128)(2,1)S(1)}, bf16[2,16,768]{2,1,0:T(8,128)(2,1)S(1)}, u32[]{:S(2)}, u32[]{:S(2)}) collective-permute-start(bf16[2,16,768]{2,1,0:T(8,128)(2,1)S(1)} %slice.124), channel_id=1, source_target_pairs={{1,0},{3,2},{5,4},{7,6},{9,8},{11,10},{13,12},{15,14},{17,16},{19,... | collective-permute-start | bytes 147464 | tf_op jit(solution)/shard_map/ppermute | solution.py:23
  3.7 0.7 copy-start.2
  3.7 0.7 copy-start.4
  3.7 0.7 copy-start.5
  3.7 1.4 %copy-start.3 = (f32[2,510]{1,0:T(2,128)S(1)}, f32[2,510]{1,0:T(2,128)}, u32[]{:S(2)}) copy-start(f32[2,510]{1,0:T(2,128)} %param.11) | copy-start | bytes 12244
  6.3 1.1 copy-start.1
  31.7 1.2 %copy-start = (f32[2,16,4224]{2,1,0:T(8,128)S(1)}, f32[2,16,4224]{2,1,0:T(8,128)}, u32[]{:S(2)}) copy-start(f32[2,16,4224]{2,1,0:T(8,128)} %shard_map.67) | copy-start | bytes 1622020
  34.3 26.1 %all-to-all-start = ((f32[2,16,16,316]{3,2,0,1:T(8,128)}), f32[2,16,16,316]{3,2,0,1:T(8,128)S(1)}, u32[]{:S(2)}, u32[]{:S(2)}) async-start(f32[2,16,16,316]{3,2,0,1:T(8,128)} %maximum_bitcast_fusion.2), calls=%async_computation | async-start | bytes 1572864 | tf_op jit(solution)/shard_map/all_to_all | solution.py:189
  93.4 1.0 slice-start

commit v3 on v2

--- a/solution.py
+++ b/solution.py
@@ -136,10 +136,13 @@
     return jnp.stack([pairs[:, :, c].reshape(parts, rows // 2, length) for c in range(2)])
 
 
-def merge_section(kids, beams, chained, weights, packed):
-    rows = kids.shape[2]
-    groups = rows // beams
-    table = jnp.broadcast_to(per_row(packed, groups)[..., None], (5, 2, 2, rows, LANE))
+def row_table(packed, beams, rows):
+    return jnp.broadcast_to(per_row(packed, rows // beams)[..., None], (5, 2, 2, rows, LANE))
+
+
+def merge_section(kids, beams, chained, weights, packed, table=None):
+    if table is None:
+        table = row_table(packed, beams, kids.shape[2])
     return merge_call(beams, chained, weights, kids, table)
 
 
@@ -169,10 +172,12 @@
     bits = [((beam_shift >> bit) & 1).astype(jnp.float32) for bit in range(3)]
     all_rows = jnp.stack(bits + [jnp.cos(beam_phase), jnp.sin(beam_phase)])
 
-    def run_section(kids, section, beams, chained):
+    def section_rows(beams):
         start = 2 * beams - 2
-        stop = start + 2 * beams
-        return merge_section(kids, beams, chained, all_weights[section], all_rows[:, :, start:stop])
+        return all_rows[:, :, start : start + 2 * beams]
+
+    def run_section(kids, section, beams, chained, table=None):
+        return merge_section(kids, beams, chained, all_weights[section], section_rows(beams), table)
 
     level = split_kids(level, 1)
     for section in range(local_sections):
@@ -186,12 +191,16 @@
         :, :, :, :need
     ]
     pieces = jnp.transpose(jnp.concatenate([head, tail], axis=3), (0, 2, 1, 3))
+    cross_rows = pulse_count * local_beams // 2
+    tables = [row_table(section_rows(local_beams << bit), local_beams << bit, cross_rows) for bit in range(cross_sections)]
+    tables = lax.optimization_barrier(tables)
     level = lax.all_to_all(pieces, "pulse", split_axis=1, concat_axis=1, tiled=True)
+    level, tables = lax.optimization_barrier((level, tables))
     level = padded_lanes(level.reshape(parts, pulse_count * local_beams, piece_bins + need), piece_bins + need)
     level = split_kids(level, local_beams)
     for bit in range(cross_sections):
         section = local_sections + bit
-        level = run_section(level, section, local_beams << bit, bit < cross_sections - 1)
+        level = run_section(level, section, local_beams << bit, bit < cross_sections - 1, tables[bit])
     level = level[..., :piece_bins].reshape(parts, pulse_count, local_beams, piece_bins)
     level = lax.all_to_all(level, "pulse", split_axis=1, concat_axis=3, tiled=True)
     return level.reshape(parts, local_beams, bins)

time: 116 us -> 113 us (0.974)
  waiting for transfers between devices: 17.8 us -> 11.9 us
  other arithmetic: 3.01 us -> 5.82 us
    all_to_all x1, waiting for transfers between devices: 17.8 us -> 11.9 us  [on_device(): lax.all_to_all(pieces, 'pulse', split_axis=1, concat_axis=1, tiled=True)]
    unnamed x3, other arithmetic: 0.03 us -> 2.09 us
  transfers between devices with their start and end apart: 2 -> 2, of which waited for: 1 -> 1; matrix products, arithmetic and copies ran while one was open for 5% -> 13% of each run, Pallas kernels for 0% -> 0%
where the time goes in v3:
time: 113 us
  Pallas kernels  44.6 us (39%)
  local copies, waits for them, and re-layouts  20.7 us (18%)
  blocking collectives  19.7 us (17%)
  waiting for transfers between devices  11.9 us (11%)
  starting transfers between devices  8.66 us (8%)
  other arithmetic  5.82 us (5%)
    pallas_call x8, Pallas kernels, merge_call(): pl.pallas_call(functools.partial(merge_kernel, beams, chained), out_shape...  44.6 us
    all_to_all x1, blocking collectives, on_device(): lax.all_to_all(level, 'pulse', split_axis=1, concat_axis=3, tiled=True)  19.7 us
    all_to_all x1, waiting for transfers between devices, on_device(): lax.all_to_all(pieces, 'pulse', split_axis=1, concat_axis=1, tiled=True)  11.9 us
    broadcast_in_dim x10, local copies, waits for them, and re-layouts, row_table(): jnp.broadcast_to(per_row(packed, rows // beams)[..., None], (5, 2, 2, row...  8.85 us
    all_to_all x1, starting transfers between devices, on_device(): lax.all_to_all(pieces, 'pulse', split_axis=1, concat_axis=1, tiled=True)  7.38 us
  transfers between devices with their start and end apart: 2, of which 1 were waited for; matrix products, arithmetic and copies ran while one was open for 13% of the time, Pallas kernels for 0%

profile of v3, /device:TPU:0, one launch (start us, length us, event | category | flops | bytes accessed | tf_op | source)
XLA Modules:
  0.0 112.6 jit_solution(6350104913268026961)
XLA Ops:
  0.0 0.8 slice.124
  0.8 1.3 %collective-permute-start = (bf16[2,16,768]{2,1,0:T(8,128)(2,1)S(1)}, bf16[2,16,768]{2,1,0:T(8,128)(2,1)S(1)}, u32[]{:S(2)}, u32[]{:S(2)}) collective-permute-start(bf16[2,16,768]{2,1,0:T(8,128)(2,1)S(1)} %slice.124), channel_id=1, source_target_pairs={{1,0},{3,2},{5,4},{7,6},{9,8},{11,10},{13,12},{15,14},{17,16},{19,... | collective-permute-start | bytes 147464 | tf_op jit(solution)/shard_map/ppermute | solution.py:23
  2.1 0.8 slice_reduce_fusion
  2.9 0.8 select_reduce_fusion
  3.7 0.6 fusion.15
  4.3 0.7 constant_dynamic-update-slice_fusion.4
  5.0 0.7 constant_dynamic-update-slice_fusion.3
  5.7 0.7 constant_dynamic-update-slice_fusion.2
  6.4 0.7 tile.69
  7.2 0.4 reshape.72
  7.5 0.2 copy.52
  7.7 0.1 copy-done.2
  8.6 0.1 copy.57
  8.8 0.7 tile.67
  9.5 0.4 reshape.71
  9.9 0.2 copy.51
  10.0 0.4 copy-done.1
  10.4 0.2 reshape.70
  10.6 0.2 fusion.14
  11.0 0.8 fusion
  12.1 0.3 copy.53
  12.4 0.8 pad_maximum_fusion.3.kid_ref
  13.3 0.7 broadcast_in_dim.34.table_ref
  14.0 4.7 %shard_map.64.kid_ref = f32[2,2,8,4224]{3,2,1,0:T(8,128)} custom-call(f32[2,8]{1,0:T(2,128)} %bitcast.83, f32[2,2,8,4224]{3,2,1,0:T(8,128)} %pad_maximum_fusion.3.kid_ref, f32[5,2,2,8,128]{4,3,2,1,0:T(8,128)} %broadcast_in_dim.34.table_ref), custom_call_target="tpu_custom_call" | custom-call | flops 8110080 | bytes 1081344 | tf_op jit(solution)/shard_map/pallas_call | solution.py:107
  18.7 0.7 broadcast_in_dim.62.table_ref
  19.4 4.6 %shard_map.65.kid_ref = f32[2,2,8,4224]{3,2,1,0:T(8,128)} custom-call(f32[2,8]{1,0:T(2,128)} %bitcast.82, f32[2,2,8,4224]{3,2,1,0:T(8,128)} %shard_map.64.kid_ref, f32[5,2,2,8,128]{4,3,2,1,0:T(8,128)} %broadcast_in_dim.62.table_ref), custom_call_target="tpu_custom_call" | custom-call | flops 8110080 | bytes 1081344 | tf_op jit(solution)/shard_map/pallas_call | solution.py:107
  24.1 0.7 broadcast_in_dim.63.table_ref
  24.8 4.6 %shard_map.66.kid_ref = f32[2,2,8,4224]{3,2,1,0:T(8,128)} custom-call(f32[2,8]{1,0:T(2,128)} %bitcast.81, f32[2,2,8,4224]{3,2,1,0:T(8,128)} %shard_map.65.kid_ref, f32[5,2,2,8,128]{4,3,2,1,0:T(8,128)} %broadcast_in_dim.63.table_ref), custom_call_target="tpu_custom_call" | custom-call | flops 8110080 | bytes 1081344 | tf_op jit(solution)/shard_map/pallas_call | solution.py:107
  29.4 0.7 broadcast_in_dim.65.table_ref
  30.1 4.7 %shard_map.67 = f32[2,16,4224]{2,1,0:T(8,128)} custom-call(f32[2,8]{1,0:T(2,128)} %bitcast.80, f32[2,2,8,4224]{3,2,1,0:T(8,128)} %shard_map.66.kid_ref, f32[5,2,2,8,128]{4,3,2,1,0:T(8,128)} %broadcast_in_dim.65.table_ref), custom_call_target="tpu_custom_call" | custom-call | flops 8110080 | bytes 1081344 | tf_op jit(solution)/shard_map/pallas_call | solution.py:107
  34.8 1.1 %slice.177 = f32[2,16,4096]{2,1,0:T(8,128)S(1)} slice(f32[2,16,4224]{2,1,0:T(8,128)} %shard_map.67), slice={[0:2], [0:16], [0:4096]} | slice | bytes 1048576 | tf_op jit(solution)/shard_map/slice | solution.py:189
  36.1 0.2 copy.67
  36.4 1.0 maximum_bitcast_fusion.2
  37.4 7.4 %all-to-all-start = ((f32[2,16,16,316]{3,2,0,1:T(8,128)}), f32[2,16,16,316]{3,2,0,1:T(8,128)S(1)}, u32[]{:S(2)}, u32[]{:S(2)}) async-start(f32[2,16,16,316]{3,2,0,1:T(8,128)} %maximum_bitcast_fusion.2), calls=%async_computation | async-start | bytes 1572864 | tf_op jit(solution)/shard_map/all_to_all | solution.py:197
  45.7 1.5 %broadcast_in_dim.66.table_ref = f32[5,2,2,128,128]{4,3,2,1,0:T(8,128)} broadcast(f32[5,2,2,128]{3,2,1,0:T(2,128)S(1)} %tile.78), dimensions={0,1,2,3} | broadcast | bytes 1320960 | tf_op jit(solution)/shard_map/broadcast_in_dim | solution.py:140
  47.2 1.5 %broadcast_in_dim.67.table_ref = f32[5,2,2,128,128]{4,3,2,1,0:T(8,128)} broadcast(f32[5,2,2,128]{3,2,1,0:T(2,128)S(1)} %tile.81), dimensions={0,1,2,3} | broadcast | bytes 1320960 | tf_op jit(solution)/shard_map/broadcast_in_dim | solution.py:140
  48.6 1.5 %broadcast_in_dim.68.table_ref = f32[5,2,2,128,128]{4,3,2,1,0:T(8,128)} broadcast(f32[5,2,2,128]{3,2,1,0:T(2,128)S(1)} %tile.84), dimensions={0,1,2,3} | broadcast | bytes 1320960 | tf_op jit(solution)/shard_map/broadcast_in_dim | solution.py:140
  50.1 1.5 %broadcast_in_dim.70.table_ref = f32[5,2,2,128,128]{4,3,2,1,0:T(8,128)} broadcast(f32[5,2,2,128]{3,2,1,0:T(2,128)S(1)} %broadcast_in_dim.69), dimensions={0,1,2,3} | broadcast | bytes 1320960 | tf_op jit(solution)/shard_map/broadcast_in_dim | solution.py:140
  51.6 11.9 %all-to-all-done = f32[2,16,16,316]{3,2,0,1:T(8,128)S(1)} async-done(((f32[2,16,16,316]{3,2,0,1:T(8,128)}), f32[2,16,16,316]{3,2,0,1:T(8,128)S(1)}, u32[]{:S(2)}, u32[]{:S(2)}) %all-to-all-start) | async-done | bytes 647200 | tf_op jit(solution)/shard_map/all_to_all | solution.py:197
  63.7 0.9 pad_maximum_fusion.1.kid_ref
  64.7 6.4 %shard_map.68.kid_ref = f32[2,2,128,384]{3,2,1,0:T(8,128)} custom-call(f32[2,8]{1,0:T(2,128)} %bitcast.79, f32[2,2,128,384]{3,2,1,0:T(8,128)} %pad_maximum_fusion.1.kid_ref, f32[5,2,2,128,128]{4,3,2,1,0:T(8,128)} %broadcast_in_dim.66.table_ref), custom_call_target="tpu_custom_call" | custom-call | flops 11796480 | bytes 1572864 | tf_op jit(solution)/shard_map/pallas_call | solution.py:107
  71.1 6.4 %shard_map.69.kid_ref = f32[2,2,128,384]{3,2,1,0:T(8,128)} custom-call(f32[2,8]{1,0:T(2,128)} %bitcast.78, f32[2,2,128,384]{3,2,1,0:T(8,128)} %shard_map.68.kid_ref, f32[5,2,2,128,128]{4,3,2,1,0:T(8,128)} %broadcast_in_dim.67.table_ref), custom_call_target="tpu_custom_call" | custom-call | flops 11796480 | bytes 1572864 | tf_op jit(solution)/shard_map/pallas_call | solution.py:107
  77.5 6.4 %shard_map.70.kid_ref = f32[2,2,128,384]{3,2,1,0:T(8,128)} custom-call(f32[2,8]{1,0:T(2,128)} %bitcast.77, f32[2,2,128,384]{3,2,1,0:T(8,128)} %shard_map.69.kid_ref, f32[5,2,2,128,128]{4,3,2,1,0:T(8,128)} %broadcast_in_dim.68.table_ref), custom_call_target="tpu_custom_call" | custom-call | flops 11796480 | bytes 1572864 | tf_op jit(solution)/shard_map/pallas_call | solution.py:107
  83.9 6.6 %shard_map.71 = f32[2,256,384]{2,1,0:T(8,128)} custom-call(f32[2,8]{1,0:T(2,128)} %bitcast.76, f32[2,2,128,384]{3,2,1,0:T(8,128)} %shard_map.70.kid_ref, f32[5,2,2,128,128]{4,3,2,1,0:T(8,128)} %broadcast_in_dim.70.table_ref), custom_call_target="tpu_custom_call" | custom-call | flops 11796480 | bytes 1572864 | tf_op jit(solution)/shard_map/pallas_call | solution.py:107
  90.6 1.0 slice-done
  91.7 19.7 %all_to_all.20 = f32[2,16,16,256]{3,2,0,1:T(8,128)S(1)} all-to-all(f32[2,16,16,256]{3,2,0,1:T(8,128)S(1)} %copy.61), channel_id=1, replica_groups=mesh['pulse'=16,'range'=2] {'pulse'}, dimensions={1} | all-to-all | bytes 1048576 | tf_op jit(solution)/shard_map/all_to_all | solution.py:205
  111.4 0.3 copy.62
  111.7 0.9 reshape.79
  (56 shorter events, 2.7 us)
Async XLA Ops:
  0.8 9.2 %collective-permute-start = (bf16[2,16,768]{2,1,0:T(8,128)(2,1)S(1)}, bf16[2,16,768]{2,1,0:T(8,128)(2,1)S(1)}, u32[]{:S(2)}, u32[]{:S(2)}) collective-permute-start(bf16[2,16,768]{2,1,0:T(8,128)(2,1)S(1)} %slice.124), channel_id=1, source_target_pairs={{1,0},{3,2},{5,4},{7,6},{9,8},{11,10},{13,12},{15,14},{17,16},{19,... | collective-permute-start | bytes 147464 | tf_op jit(solution)/shard_map/ppermute | solution.py:23
  7.1 0.7 copy-start.2
  9.4 1.0 copy-start.1
  34.8 1.2 %copy-start = (f32[2,16,4224]{2,1,0:T(8,128)S(1)}, f32[2,16,4224]{2,1,0:T(8,128)}, u32[]{:S(2)}) copy-start(f32[2,16,4224]{2,1,0:T(8,128)} %shard_map.67) | copy-start | bytes 1622020
  37.4 26.1 %all-to-all-start = ((f32[2,16,16,316]{3,2,0,1:T(8,128)}), f32[2,16,16,316]{3,2,0,1:T(8,128)S(1)}, u32[]{:S(2)}, u32[]{:S(2)}) async-start(f32[2,16,16,316]{3,2,0,1:T(8,128)} %maximum_bitcast_fusion.2), calls=%async_computation | async-start | bytes 1572864 | tf_op jit(solution)/shard_map/all_to_all | solution.py:197
  90.6 1.0 slice-start

commit v4 on v3

--- a/solution.py
+++ b/solution.py
@@ -192,7 +192,9 @@
     ]
     pieces = jnp.transpose(jnp.concatenate([head, tail], axis=3), (0, 2, 1, 3))
     cross_rows = pulse_count * local_beams // 2
-    tables = [row_table(section_rows(local_beams << bit), local_beams << bit, cross_rows) for bit in range(cross_sections)]
+    sources = [section_rows(local_beams << bit) for bit in range(cross_sections)]
+    pieces, sources = lax.optimization_barrier((pieces, sources))
+    tables = [row_table(sources[bit], local_beams << bit, cross_rows) for bit in range(cross_sections)]
     tables = lax.optimization_barrier(tables)
     level = lax.all_to_all(pieces, "pulse", split_axis=1, concat_axis=1, tiled=True)
     level, tables = lax.optimization_barrier((level, tables))

time: 113 us -> 114 us (level)
  no operation moved by 1% of the time
where the time goes in v4:
time: 114 us; the launch traced here: 113 us
  Pallas kernels  44.6 us (39%)
  local copies, waits for them, and re-layouts  20.7 us (18%)
  blocking collectives  19.7 us (17%)
  waiting for transfers between devices  12.2 us (11%)
  starting transfers between devices  8.66 us (8%)
  other arithmetic  5.82 us (5%)
    pallas_call x8, Pallas kernels, merge_call(): pl.pallas_call(functools.partial(merge_kernel, beams, chained), out_shape...  44.6 us
    all_to_all x1, blocking collectives, on_device(): lax.all_to_all(level, 'pulse', split_axis=1, concat_axis=3, tiled=True)  19.7 us
    all_to_all x1, waiting for transfers between devices, on_device(): lax.all_to_all(pieces, 'pulse', split_axis=1, concat_axis=1, tiled=True)  12.2 us
    broadcast_in_dim x10, local copies, waits for them, and re-layouts, row_table(): jnp.broadcast_to(per_row(packed, rows // beams)[..., None], (5, 2, 2, row...  8.85 us
    all_to_all x1, starting transfers between devices, on_device(): lax.all_to_all(pieces, 'pulse', split_axis=1, concat_axis=1, tiled=True)  7.38 us
  transfers between devices with their start and end apart: 2, of which 1 were waited for; matrix products, arithmetic and copies ran while one was open for 13% of the time, Pallas kernels for 0%

profile of v4, /device:TPU:0, one launch (start us, length us, event | category | flops | bytes accessed | tf_op | source)
XLA Modules:
  0.0 112.9 jit_solution(1004867619366168663)
XLA Ops:
  0.0 0.8 slice.124
  0.8 1.3 %collective-permute-start = (bf16[2,16,768]{2,1,0:T(8,128)(2,1)S(1)}, bf16[2,16,768]{2,1,0:T(8,128)(2,1)S(1)}, u32[]{:S(2)}, u32[]{:S(2)}) collective-permute-start(bf16[2,16,768]{2,1,0:T(8,128)(2,1)S(1)} %slice.124), channel_id=1, source_target_pairs={{1,0},{3,2},{5,4},{7,6},{9,8},{11,10},{13,12},{15,14},{17,16},{19,... | collective-permute-start | bytes 147464 | tf_op jit(solution)/shard_map/ppermute | solution.py:23
  2.1 0.8 slice_reduce_fusion
  2.9 0.8 select_reduce_fusion
  3.7 0.6 fusion.15
  4.3 0.7 constant_dynamic-update-slice_fusion.4
  5.0 0.7 constant_dynamic-update-slice_fusion.3
  5.7 0.7 constant_dynamic-update-slice_fusion.2
  6.4 0.7 tile.69
  7.2 0.4 reshape.72
  7.5 0.2 copy.52
  7.7 0.1 copy-done.2
  8.9 0.1 copy.57
  9.1 0.7 tile.67
  9.8 0.4 reshape.71
  10.2 0.2 copy.51
  10.3 0.4 copy-done.1
  10.7 0.2 reshape.70
  10.9 0.2 fusion.14
  11.4 0.8 fusion
  12.4 0.3 copy.53
  12.8 0.8 pad_maximum_fusion.3.kid_ref
  13.6 0.7 broadcast_in_dim.34.table_ref
  14.3 4.7 %shard_map.64.kid_ref = f32[2,2,8,4224]{3,2,1,0:T(8,128)} custom-call(f32[2,8]{1,0:T(2,128)} %bitcast.83, f32[2,2,8,4224]{3,2,1,0:T(8,128)} %pad_maximum_fusion.3.kid_ref, f32[5,2,2,8,128]{4,3,2,1,0:T(8,128)} %broadcast_in_dim.34.table_ref), custom_call_target="tpu_custom_call" | custom-call | flops 8110080 | bytes 1081344 | tf_op jit(solution)/shard_map/pallas_call | solution.py:107
  19.0 0.7 broadcast_in_dim.62.table_ref
  19.8 4.6 %shard_map.65.kid_ref = f32[2,2,8,4224]{3,2,1,0:T(8,128)} custom-call(f32[2,8]{1,0:T(2,128)} %bitcast.82, f32[2,2,8,4224]{3,2,1,0:T(8,128)} %shard_map.64.kid_ref, f32[5,2,2,8,128]{4,3,2,1,0:T(8,128)} %broadcast_in_dim.62.table_ref), custom_call_target="tpu_custom_call" | custom-call | flops 8110080 | bytes 1081344 | tf_op jit(solution)/shard_map/pallas_call | solution.py:107
  24.4 0.7 broadcast_in_dim.63.table_ref
  25.1 4.6 %shard_map.66.kid_ref = f32[2,2,8,4224]{3,2,1,0:T(8,128)} custom-call(f32[2,8]{1,0:T(2,128)} %bitcast.81, f32[2,2,8,4224]{3,2,1,0:T(8,128)} %shard_map.65.kid_ref, f32[5,2,2,8,128]{4,3,2,1,0:T(8,128)} %broadcast_in_dim.63.table_ref), custom_call_target="tpu_custom_call" | custom-call | flops 8110080 | bytes 1081344 | tf_op jit(solution)/shard_map/pallas_call | solution.py:107
  29.7 0.7 broadcast_in_dim.65.table_ref
  30.4 4.7 %shard_map.67 = f32[2,16,4224]{2,1,0:T(8,128)} custom-call(f32[2,8]{1,0:T(2,128)} %bitcast.80, f32[2,2,8,4224]{3,2,1,0:T(8,128)} %shard_map.66.kid_ref, f32[5,2,2,8,128]{4,3,2,1,0:T(8,128)} %broadcast_in_dim.65.table_ref), custom_call_target="tpu_custom_call" | custom-call | flops 8110080 | bytes 1081344 | tf_op jit(solution)/shard_map/pallas_call | solution.py:107
  35.1 1.1 %slice.177 = f32[2,16,4096]{2,1,0:T(8,128)S(1)} slice(f32[2,16,4224]{2,1,0:T(8,128)} %shard_map.67), slice={[0:2], [0:16], [0:4096]} | slice | bytes 1048576 | tf_op jit(solution)/shard_map/slice | solution.py:189
  36.4 0.2 copy.67
  36.7 1.0 maximum_bitcast_fusion.2
  37.7 7.4 %all-to-all-start = ((f32[2,16,16,316]{3,2,0,1:T(8,128)}), f32[2,16,16,316]{3,2,0,1:T(8,128)S(1)}, u32[]{:S(2)}, u32[]{:S(2)}) async-start(f32[2,16,16,316]{3,2,0,1:T(8,128)} %maximum_bitcast_fusion.2), calls=%async_computation | async-start | bytes 1572864 | tf_op jit(solution)/shard_map/all_to_all | solution.py:199
  45.7 1.5 %broadcast_in_dim.66.table_ref = f32[5,2,2,128,128]{4,3,2,1,0:T(8,128)} broadcast(f32[5,2,2,128]{3,2,1,0:T(2,128)S(1)} %tile.78), dimensions={0,1,2,3} | broadcast | bytes 1320960 | tf_op jit(solution)/shard_map/broadcast_in_dim | solution.py:140
  47.2 1.5 %broadcast_in_dim.67.table_ref = f32[5,2,2,128,128]{4,3,2,1,0:T(8,128)} broadcast(f32[5,2,2,128]{3,2,1,0:T(2,128)S(1)} %tile.81), dimensions={0,1,2,3} | broadcast | bytes 1320960 | tf_op jit(solution)/shard_map/broadcast_in_dim | solution.py:140
  48.6 1.5 %broadcast_in_dim.70.table_ref = f32[5,2,2,128,128]{4,3,2,1,0:T(8,128)} broadcast(f32[5,2,2,128]{3,2,1,0:T(2,128)S(1)} %broadcast_in_dim.69), dimensions={0,1,2,3} | broadcast | bytes 1320960 | tf_op jit(solution)/shard_map/broadcast_in_dim | solution.py:140
  50.1 1.5 %broadcast_in_dim.68.table_ref = f32[5,2,2,128,128]{4,3,2,1,0:T(8,128)} broadcast(f32[5,2,2,128]{3,2,1,0:T(2,128)S(1)} %tile.84), dimensions={0,1,2,3} | broadcast | bytes 1320960 | tf_op jit(solution)/shard_map/broadcast_in_dim | solution.py:140
  51.6 12.2 %all-to-all-done = f32[2,16,16,316]{3,2,0,1:T(8,128)S(1)} async-done(((f32[2,16,16,316]{3,2,0,1:T(8,128)}), f32[2,16,16,316]{3,2,0,1:T(8,128)S(1)}, u32[]{:S(2)}, u32[]{:S(2)}) %all-to-all-start) | async-done | bytes 647200 | tf_op jit(solution)/shard_map/all_to_all | solution.py:199
  64.0 0.9 pad_maximum_fusion.1.kid_ref
  65.0 6.4 %shard_map.68.kid_ref = f32[2,2,128,384]{3,2,1,0:T(8,128)} custom-call(f32[2,8]{1,0:T(2,128)} %bitcast.79, f32[2,2,128,384]{3,2,1,0:T(8,128)} %pad_maximum_fusion.1.kid_ref, f32[5,2,2,128,128]{4,3,2,1,0:T(8,128)} %broadcast_in_dim.66.table_ref), custom_call_target="tpu_custom_call" | custom-call | flops 11796480 | bytes 1572864 | tf_op jit(solution)/shard_map/pallas_call | solution.py:107
  71.4 6.4 %shard_map.69.kid_ref = f32[2,2,128,384]{3,2,1,0:T(8,128)} custom-call(f32[2,8]{1,0:T(2,128)} %bitcast.78, f32[2,2,128,384]{3,2,1,0:T(8,128)} %shard_map.68.kid_ref, f32[5,2,2,128,128]{4,3,2,1,0:T(8,128)} %broadcast_in_dim.67.table_ref), custom_call_target="tpu_custom_call" | custom-call | flops 11796480 | bytes 1572864 | tf_op jit(solution)/shard_map/pallas_call | solution.py:107
  77.8 6.4 %shard_map.70.kid_ref = f32[2,2,128,384]{3,2,1,0:T(8,128)} custom-call(f32[2,8]{1,0:T(2,128)} %bitcast.77, f32[2,2,128,384]{3,2,1,0:T(8,128)} %shard_map.69.kid_ref, f32[5,2,2,128,128]{4,3,2,1,0:T(8,128)} %broadcast_in_dim.68.table_ref), custom_call_target="tpu_custom_call" | custom-call | flops 11796480 | bytes 1572864 | tf_op jit(solution)/shard_map/pallas_call | solution.py:107
  84.2 6.7 %shard_map.71 = f32[2,256,384]{2,1,0:T(8,128)} custom-call(f32[2,8]{1,0:T(2,128)} %bitcast.76, f32[2,2,128,384]{3,2,1,0:T(8,128)} %shard_map.70.kid_ref, f32[5,2,2,128,128]{4,3,2,1,0:T(8,128)} %broadcast_in_dim.70.table_ref), custom_call_target="tpu_custom_call" | custom-call | flops 11796480 | bytes 1572864 | tf_op jit(solution)/shard_map/pallas_call | solution.py:107
  90.9 1.0 slice-done
  92.0 19.7 %all_to_all.20 = f32[2,16,16,256]{3,2,0,1:T(8,128)S(1)} all-to-all(f32[2,16,16,256]{3,2,0,1:T(8,128)S(1)} %copy.61), channel_id=1, replica_groups=mesh['pulse'=16,'range'=2] {'pulse'}, dimensions={1} | all-to-all | bytes 1048576 | tf_op jit(solution)/shard_map/all_to_all | solution.py:207
  111.7 0.3 copy.62
  112.0 0.9 reshape.79
  (56 shorter events, 2.7 us)
Async XLA Ops:
  0.8 9.5 %collective-permute-start = (bf16[2,16,768]{2,1,0:T(8,128)(2,1)S(1)}, bf16[2,16,768]{2,1,0:T(8,128)(2,1)S(1)}, u32[]{:S(2)}, u32[]{:S(2)}) collective-permute-start(bf16[2,16,768]{2,1,0:T(8,128)(2,1)S(1)} %slice.124), channel_id=1, source_target_pairs={{1,0},{3,2},{5,4},{7,6},{9,8},{11,10},{13,12},{15,14},{17,16},{19,... | collective-permute-start | bytes 147464 | tf_op jit(solution)/shard_map/ppermute | solution.py:23
  7.1 0.7 copy-start.2
  9.8 1.0 copy-start.1
  35.1 1.2 %copy-start = (f32[2,16,4224]{2,1,0:T(8,128)S(1)}, f32[2,16,4224]{2,1,0:T(8,128)}, u32[]{:S(2)}) copy-start(f32[2,16,4224]{2,1,0:T(8,128)} %shard_map.67) | copy-start | bytes 1622020
  37.7 26.1 %all-to-all-start = ((f32[2,16,16,316]{3,2,0,1:T(8,128)}), f32[2,16,16,316]{3,2,0,1:T(8,128)S(1)}, u32[]{:S(2)}, u32[]{:S(2)}) async-start(f32[2,16,16,316]{3,2,0,1:T(8,128)} %maximum_bitcast_fusion.2), calls=%async_computation | async-start | bytes 1572864 | tf_op jit(solution)/shard_map/all_to_all | solution.py:199
  90.9 1.0 slice-start

commit v5 on v3

--- a/solution.py
+++ b/solution.py
@@ -184,26 +184,49 @@
         level = run_section(level, section, 1 << section, section < local_sections - 1)
     piece_bins = bins // pulse_count
     need = cross_sections * MARGIN
-    flat = level[:, :, : bins + need]
-    flat = jnp.pad(flat, ((0, 0), (0, 0), (0, piece_bins - need)))
-    head = flat[:, :, :bins].reshape(parts, local_beams, pulse_count, piece_bins)
-    tail = flat[:, :, piece_bins:].reshape(parts, local_beams, pulse_count, piece_bins)[
-        :, :, :, :need
-    ]
-    pieces = jnp.transpose(jnp.concatenate([head, tail], axis=3), (0, 2, 1, 3))
-    cross_rows = pulse_count * local_beams // 2
-    tables = [row_table(section_rows(local_beams << bit), local_beams << bit, cross_rows) for bit in range(cross_sections)]
-    tables = lax.optimization_barrier(tables)
-    level = lax.all_to_all(pieces, "pulse", split_axis=1, concat_axis=1, tiled=True)
-    level, tables = lax.optimization_barrier((level, tables))
-    level = padded_lanes(level.reshape(parts, pulse_count * local_beams, piece_bins + need), piece_bins + need)
-    level = split_kids(level, local_beams)
-    for bit in range(cross_sections):
-        section = local_sections + bit
-        level = run_section(level, section, local_beams << bit, bit < cross_sections - 1, tables[bit])
-    level = level[..., :piece_bins].reshape(parts, pulse_count, local_beams, piece_bins)
-    level = lax.all_to_all(level, "pulse", split_axis=1, concat_axis=3, tiled=True)
-    return level.reshape(parts, local_beams, bins)
+    chunk_beams = local_beams // 2
+    outputs = []
+    for chunk in range(2):
+        flat = level[:, chunk * chunk_beams : (chunk + 1) * chunk_beams, : bins + need]
+        flat = jnp.pad(flat, ((0, 0), (0, 0), (0, piece_bins - need)))
+        head = flat[:, :, :bins].reshape(parts, chunk_beams, pulse_count, piece_bins)
+        tail = flat[:, :, piece_bins:].reshape(parts, chunk_beams, pulse_count, piece_bins)[
+            :, :, :, :need
+        ]
+        pieces = jnp.transpose(jnp.concatenate([head, tail], axis=3), (0, 2, 1, 3))
+        cross_rows = pulse_count * chunk_beams // 2
+        sources = []
+        for bit in range(cross_sections):
+            beams = local_beams << bit
+            first = 2 * beams - 2
+            picks = [
+                first + (g // chunk_beams) * local_beams + chunk * chunk_beams + g % chunk_beams
+                for g in range(2 * (chunk_beams << bit))
+            ]
+            sources.append(all_rows[:, :, jnp.array(picks, dtype=jnp.int32)])
+        pieces, sources = lax.optimization_barrier((pieces, sources))
+        tables = [
+            row_table(sources[bit], chunk_beams << bit, cross_rows) for bit in range(cross_sections)
+        ]
+        tables = lax.optimization_barrier(tables)
+        part = lax.all_to_all(pieces, "pulse", split_axis=1, concat_axis=1, tiled=True)
+        part, tables = lax.optimization_barrier((part, tables))
+        part = padded_lanes(part.reshape(parts, pulse_count * chunk_beams, piece_bins + need), piece_bins + need)
+        part = split_kids(part, chunk_beams)
+        for bit in range(cross_sections):
+            section = local_sections + bit
+            part = merge_section(
+                part,
+                chunk_beams << bit,
+                bit < cross_sections - 1,
+                all_weights[section],
+                None,
+                tables[bit],
+            )
+        part = part[..., :piece_bins].reshape(parts, pulse_count, chunk_beams, piece_bins)
+        part = lax.all_to_all(part, "pulse", split_axis=1, concat_axis=3, tiled=True)
+        outputs.append(part.reshape(parts, chunk_beams, bins))
+    return jnp.concatenate(outputs, axis=1)
 
 
 def solution(mesh):

time: 113 us -> 138 us (1.22)
  blocking collectives: 19.7 us -> 0 us
  starting transfers between devices: 8.66 us -> 24.2 us
  local copies, waits for them, and re-layouts: 20.7 us -> 31.8 us
  Pallas kernels: 44.6 us -> 53.1 us
  waiting for transfers between devices: 11.9 us -> 18.6 us
  other arithmetic: 5.82 us -> 7.87 us
    all_to_all x1 -> x0, blocking collectives: 19.7 us -> none  [on_device(): lax.all_to_all(level, 'pulse', split_axis=1, concat_axis=3, tiled=True)]
    all_to_all x0 -> x2, starting transfers between devices: none -> 12 us  [on_device(): lax.all_to_all(part, 'pulse', split_axis=1, concat_axis=3, tiled=True)]
    all_to_all x0 -> x2, waiting for transfers between devices: none -> 9.83 us  [on_device(): lax.all_to_all(part, 'pulse', split_axis=1, concat_axis=3, tiled=True)]
    pallas_call x8 -> x12, Pallas kernels: 44.6 us -> 53.1 us  [merge_call(): pl.pallas_call(functools.partial(merge_kernel, beams, chained), out_shape...]
    gather x0 -> x8, local copies, waits for them, and re-layouts: none -> 5.19 us  [on_device(): sources.append(all_rows[:, :, jnp.array(picks, dtype=jnp.int32)])]
    all_to_all x1 -> x2, starting transfers between devices: 7.38 us -> 10.9 us  [on_device(): lax.all_to_all(pieces, 'pulse', split_axis=1, concat_axis=1, tiled=True)]
    all_to_all x1 -> x2, waiting for transfers between devices: 11.9 us -> 8.72 us  [on_device(): lax.all_to_all(pieces, 'pulse', split_axis=1, concat_axis=1, tiled=True)]
    broadcast_in_dim x10 -> x15, local copies, waits for them, and re-layouts: 8.85 us -> 11.8 us  [row_table(): jnp.broadcast_to(per_row(packed, rows // beams)[..., None], (5, 2, 2, row...]
  transfers between devices with their start and end apart: 2 -> 5, of which waited for: 1 -> 2; matrix products, arithmetic and copies ran while one was open for 13% -> 22% of each run, Pallas kernels for 0% -> 25%
where the time goes in v5:
time: 138 us; the launch traced here: 137 us
  Pallas kernels  53.1 us (38%)
  local copies, waits for them, and re-layouts  31.8 us (23%)
  starting transfers between devices  24.2 us (18%)
  waiting for transfers between devices  18.6 us (13%)
  other arithmetic  7.87 us (6%)
    pallas_call x12, Pallas kernels, merge_call(): pl.pallas_call(functools.partial(merge_kernel, beams, chained), out_shape...  53.1 us
    all_to_all x2, starting transfers between devices, on_device(): lax.all_to_all(part, 'pulse', split_axis=1, concat_axis=3, tiled=True)  12 us
    broadcast_in_dim x15, local copies, waits for them, and re-layouts, row_table(): jnp.broadcast_to(per_row(packed, rows // beams)[..., None], (5, 2, 2, row...  11.8 us
    all_to_all x2, starting transfers between devices, on_device(): lax.all_to_all(pieces, 'pulse', split_axis=1, concat_axis=1, tiled=True)  10.9 us
    all_to_all x2, waiting for transfers between devices, on_device(): lax.all_to_all(part, 'pulse', split_axis=1, concat_axis=3, tiled=True)  9.83 us
    all_to_all x2, waiting for transfers between devices, on_device(): lax.all_to_all(pieces, 'pulse', split_axis=1, concat_axis=1, tiled=True)  8.72 us
    gather x8, local copies, waits for them, and re-layouts, on_device(): sources.append(all_rows[:, :, jnp.array(picks, dtype=jnp.int32)])  5.19 us
    reshape x4, local copies, waits for them, and re-layouts, on_device(): part[..., :piece_bins].reshape(parts, pulse_count, chunk_beams, piece_bins)  3.39 us
  transfers between devices with their start and end apart: 5, of which 2 were waited for; matrix products, arithmetic and copies ran while one was open for 22% of the time, Pallas kernels for 25%

profile of v5, /device:TPU:0, one launch (start us, length us, event | category | flops | bytes accessed | tf_op | source)
XLA Modules:
  0.0 137.0 jit_solution(9477515754296560892)
XLA Ops:
  0.0 0.8 slice.139
  0.8 1.3 collective-permute-start
  2.1 0.8 slice_reduce_fusion
  2.9 0.8 select_reduce_fusion
  6.4 0.8 constant_dynamic-update-slice_fusion.1
  7.1 0.8 constant_dynamic-update-slice_fusion
  13.6 0.7 gather_fusion.7
  15.0 0.8 fusion
  16.4 0.9 pad_maximum_fusion.2.kid_ref
  17.2 0.7 broadcast_in_dim.107.table_ref
  18.0 4.7 %shard_map.136.kid_ref = f32[2,2,8,4224]{3,2,1,0:T(8,128)} custom-call(f32[2,8]{1,0:T(2,128)} %bitcast.131, f32[2,2,8,4224]{3,2,1,0:T(8,128)} %pad_maximum_fusion.2.kid_ref, f32[5,2,2,8,128]{4,3,2,1,0:T(8,128)} %broadcast_in_dim.107.table_ref), custom_call_target="tpu_custom_call" | custom-call | flops 8110080 | bytes 1081344 | tf_op jit(solution)/shard_map/pallas_call | solution.py:107
  22.7 0.7 broadcast_in_dim.108.table_ref
  23.4 4.6 %shard_map.137.kid_ref = f32[2,2,8,4224]{3,2,1,0:T(8,128)} custom-call(f32[2,8]{1,0:T(2,128)} %bitcast.130, f32[2,2,8,4224]{3,2,1,0:T(8,128)} %shard_map.136.kid_ref, f32[5,2,2,8,128]{4,3,2,1,0:T(8,128)} %broadcast_in_dim.108.table_ref), custom_call_target="tpu_custom_call" | custom-call | flops 8110080 | bytes 1081344 | tf_op jit(solution)/shard_map/pallas_call | solution.py:107
  28.7 4.6 %shard_map.138.kid_ref = f32[2,2,8,4224]{3,2,1,0:T(8,128)} custom-call(f32[2,8]{1,0:T(2,128)} %bitcast.129, f32[2,2,8,4224]{3,2,1,0:T(8,128)} %shard_map.137.kid_ref, f32[5,2,2,8,128]{4,3,2,1,0:T(8,128)} %broadcast_in_dim.109.table_ref), custom_call_target="tpu_custom_call" | custom-call | flops 8110080 | bytes 1081344 | tf_op jit(solution)/shard_map/pallas_call | solution.py:107
  34.1 4.7 %shard_map.139 = f32[2,16,4224]{2,1,0:T(8,128)} custom-call(f32[2,8]{1,0:T(2,128)} %bitcast.128, f32[2,2,8,4224]{3,2,1,0:T(8,128)} %shard_map.138.kid_ref, f32[5,2,2,8,128]{4,3,2,1,0:T(8,128)} %broadcast_in_dim.111.table_ref), custom_call_target="tpu_custom_call" | custom-call | flops 8110080 | bytes 1081344 | tf_op jit(solution)/shard_map/pallas_call | solution.py:107
  38.8 1.1 fusion.12
  40.1 0.8 copy_bitcast_fusion
  40.9 7.4 %all-to-all-start.2 = ((f32[2,16,8,316]{3,2,0,1:T(8,128)}), f32[2,16,8,316]{3,2,0,1:T(8,128)S(1)}, u32[]{:S(2)}, u32[]{:S(2)}) async-start(f32[2,16,8,316]{3,2,0,1:T(8,128)} %copy_bitcast_fusion), calls=%async_computation.2 | async-start | bytes 786432 | tf_op jit(solution)/shard_map/all_to_all | solution.py:212
  50.2 0.7 gather_fusion.3
  51.0 0.8 copy_bitcast_fusion.1
  51.8 8.7 %all-to-all-done.2 = f32[2,16,8,316]{3,2,0,1:T(8,128)S(1)} async-done(((f32[2,16,8,316]{3,2,0,1:T(8,128)}), f32[2,16,8,316]{3,2,0,1:T(8,128)S(1)}, u32[]{:S(2)}, u32[]{:S(2)}) %all-to-all-start.2) | async-done | bytes 323616 | tf_op jit(solution)/shard_map/all_to_all | solution.py:212
  60.5 3.6 %all-to-all-start = ((f32[2,16,8,316]{3,2,0,1:T(8,128)}), f32[2,16,8,316]{3,2,0,1:T(8,128)S(1)}, u32[]{:S(2)}, u32[]{:S(2)}) async-start(f32[2,16,8,316]{3,2,0,1:T(8,128)} %copy_bitcast_fusion.1), calls=%async_computation | async-start | bytes 786432 | tf_op jit(solution)/shard_map/all_to_all | solution.py:212
  65.6 1.1 broadcast_in_dim.125.table_ref
  66.7 1.1 broadcast_in_dim.126.table_ref
  67.8 1.1 broadcast_in_dim.129.table_ref
  68.8 1.1 broadcast_in_dim.127.table_ref
  69.9 1.1 broadcast_in_dim.116.table_ref
  71.0 1.1 broadcast_in_dim.117.table_ref
  72.1 1.1 broadcast_in_dim.120.table_ref
  73.2 1.1 broadcast_in_dim.118.table_ref
  74.4 0.8 pad_maximum_fusion.7.kid_ref
  75.1 4.3 %shard_map.144.kid_ref = f32[2,2,64,384]{3,2,1,0:T(8,128)} custom-call(f32[2,8]{1,0:T(2,128)} %bitcast.126, f32[2,2,64,384]{3,2,1,0:T(8,128)} %pad_maximum_fusion.7.kid_ref, f32[5,2,2,64,128]{4,3,2,1,0:T(8,128)} %broadcast_in_dim.125.table_ref), custom_call_target="tpu_custom_call" | custom-call | flops 5898240 | bytes 786432 | tf_op jit(solution)/shard_map/pallas_call | solution.py:107
  79.4 4.3 %shard_map.145.kid_ref = f32[2,2,64,384]{3,2,1,0:T(8,128)} custom-call(f32[2,8]{1,0:T(2,128)} %bitcast.124, f32[2,2,64,384]{3,2,1,0:T(8,128)} %shard_map.144.kid_ref, f32[5,2,2,64,128]{4,3,2,1,0:T(8,128)} %broadcast_in_dim.126.table_ref), custom_call_target="tpu_custom_call" | custom-call | flops 5898240 | bytes 786432 | tf_op jit(solution)/shard_map/pallas_call | solution.py:107
  83.7 4.3 %shard_map.146.kid_ref = f32[2,2,64,384]{3,2,1,0:T(8,128)} custom-call(f32[2,8]{1,0:T(2,128)} %bitcast.122, f32[2,2,64,384]{3,2,1,0:T(8,128)} %shard_map.145.kid_ref, f32[5,2,2,64,128]{4,3,2,1,0:T(8,128)} %broadcast_in_dim.127.table_ref), custom_call_target="tpu_custom_call" | custom-call | flops 5898240 | bytes 786432 | tf_op jit(solution)/shard_map/pallas_call | solution.py:107
  88.0 4.3 %shard_map.147 = f32[2,128,384]{2,1,0:T(8,128)} custom-call(f32[2,8]{1,0:T(2,128)} %bitcast.120, f32[2,2,64,384]{3,2,1,0:T(8,128)} %shard_map.146.kid_ref, f32[5,2,2,64,128]{4,3,2,1,0:T(8,128)} %broadcast_in_dim.129.table_ref), custom_call_target="tpu_custom_call" | custom-call | flops 5898240 | bytes 786432 | tf_op jit(solution)/shard_map/pallas_call | solution.py:107
  92.4 1.0 slice_bitcast_fusion.2
  93.3 0.7 copy.236
  94.1 6.0 %all-to-all-start.3 = ((f32[2,16,8,256]{3,2,0,1:T(8,128)}), f32[2,16,8,256]{3,2,0,1:T(8,128)S(1)}, u32[]{:S(2)}, u32[]{:S(2)}) async-start(f32[2,16,8,256]{3,2,0,1:T(8,128)} %copy.236), calls=%async_computation.3 | async-start | bytes 524288 | tf_op jit(solution)/shard_map/all_to_all | solution.py:227
  100.2 0.8 pad_maximum_fusion.5.kid_ref
  100.9 4.3 %shard_map.140.kid_ref = f32[2,2,64,384]{3,2,1,0:T(8,128)} custom-call(f32[2,8]{1,0:T(2,128)} %bitcast.127, f32[2,2,64,384]{3,2,1,0:T(8,128)} %pad_maximum_fusion.5.kid_ref, f32[5,2,2,64,128]{4,3,2,1,0:T(8,128)} %broadcast_in_dim.116.table_ref), custom_call_target="tpu_custom_call" | custom-call | flops 5898240 | bytes 786432 | tf_op jit(solution)/shard_map/pallas_call | solution.py:107
  105.3 4.3 %shard_map.141.kid_ref = f32[2,2,64,384]{3,2,1,0:T(8,128)} custom-call(f32[2,8]{1,0:T(2,128)} %bitcast.125, f32[2,2,64,384]{3,2,1,0:T(8,128)} %shard_map.140.kid_ref, f32[5,2,2,64,128]{4,3,2,1,0:T(8,128)} %broadcast_in_dim.117.table_ref), custom_call_target="tpu_custom_call" | custom-call | flops 5898240 | bytes 786432 | tf_op jit(solution)/shard_map/pallas_call | solution.py:107
  109.6 4.3 %shard_map.142.kid_ref = f32[2,2,64,384]{3,2,1,0:T(8,128)} custom-call(f32[2,8]{1,0:T(2,128)} %bitcast.123, f32[2,2,64,384]{3,2,1,0:T(8,128)} %shard_map.141.kid_ref, f32[5,2,2,64,128]{4,3,2,1,0:T(8,128)} %broadcast_in_dim.118.table_ref), custom_call_target="tpu_custom_call" | custom-call | flops 5898240 | bytes 786432 | tf_op jit(solution)/shard_map/pallas_call | solution.py:107
  113.9 4.3 %shard_map.143 = f32[2,128,384]{2,1,0:T(8,128)} custom-call(f32[2,8]{1,0:T(2,128)} %bitcast.121, f32[2,2,64,384]{3,2,1,0:T(8,128)} %shard_map.142.kid_ref, f32[5,2,2,64,128]{4,3,2,1,0:T(8,128)} %broadcast_in_dim.120.table_ref), custom_call_target="tpu_custom_call" | custom-call | flops 5898240 | bytes 786432 | tf_op jit(solution)/shard_map/pallas_call | solution.py:107
  118.2 1.0 slice_bitcast_fusion.3
  119.1 0.7 copy.223
  119.9 6.0 %all-to-all-start.1 = ((f32[2,16,8,256]{3,2,0,1:T(8,128)}), f32[2,16,8,256]{3,2,0,1:T(8,128)S(1)}, u32[]{:S(2)}, u32[]{:S(2)}) async-start(f32[2,16,8,256]{3,2,0,1:T(8,128)} %copy.223), calls=%async_computation.1 | async-start | bytes 524288 | tf_op jit(solution)/shard_map/all_to_all | solution.py:227
  126.1 9.8 %all-to-all-done.1 = f32[2,16,8,256]{3,2,0,1:T(8,128)S(1)} async-done(((f32[2,16,8,256]{3,2,0,1:T(8,128)}), f32[2,16,8,256]{3,2,0,1:T(8,128)S(1)}, u32[]{:S(2)}, u32[]{:S(2)}) %all-to-all-start.1) | async-done | bytes 262176 | tf_op jit(solution)/shard_map/all_to_all | solution.py:227
  136.2 0.8 pad_maximum_fusion.3
  (111 shorter events, 14.9 us)
Async XLA Ops:
  0.8 13.5 %collective-permute-start = (bf16[2,16,768]{2,1,0:T(8,128)(2,1)S(1)}, bf16[2,16,768]{2,1,0:T(8,128)(2,1)S(1)}, u32[]{:S(2)}, u32[]{:S(2)}) collective-permute-start(bf16[2,16,768]{2,1,0:T(8,128)(2,1)S(1)} %slice.139), channel_id=1, source_target_pairs={{1,0},{3,2},{5,4},{7,6},{9,8},{11,10},{13,12},{15,14},{17,16},{19,... | collective-permute-start | bytes 147464 | tf_op jit(solution)/shard_map/ppermute | solution.py:23
  8.7 0.7 copy-start.8
  8.7 0.7 copy-start.9
  8.7 0.7 copy-start.6
  8.7 0.7 copy-start.7
  8.7 0.7 copy-start.4
  8.7 0.7 copy-start.5
  11.1 3.2 %copy-start.1 = (bf16[2,16,4096]{2,1,0:T(8,128)(2,1)S(1)}, bf16[2,16,4096]{2,1,0:T(8,128)(2,1)}, u32[]{:S(2)}) copy-start(bf16[2,16,4096]{2,1,0:T(8,128)(2,1)} %param.14) | copy-start | bytes 786436
  38.8 1.2 copy-start
  40.0 8.2 %copy-start.2 = (s32[128]{0:T(128)S(1)}, s32[128]{0:T(128)}, u32[]{:S(2)}) copy-start(s32[128]{0:T(128)} %constant.92) | copy-start | bytes 1540
  40.1 8.2 %copy-start.3 = (s32[64]{0:T(128)S(1)}, s32[64]{0:T(128)}, u32[]{:S(2)}) copy-start(s32[64]{0:T(128)} %constant.91) | copy-start | bytes 772
  40.9 19.6 %all-to-all-start.2 = ((f32[2,16,8,316]{3,2,0,1:T(8,128)}), f32[2,16,8,316]{3,2,0,1:T(8,128)S(1)}, u32[]{:S(2)}, u32[]{:S(2)}) async-start(f32[2,16,8,316]{3,2,0,1:T(8,128)} %copy_bitcast_fusion), calls=%async_computation.2 | async-start | bytes 786432 | tf_op jit(solution)/shard_map/all_to_all | solution.py:212
  60.5 33.6 %all-to-all-start = ((f32[2,16,8,316]{3,2,0,1:T(8,128)}), f32[2,16,8,316]{3,2,0,1:T(8,128)S(1)}, u32[]{:S(2)}, u32[]{:S(2)}) async-start(f32[2,16,8,316]{3,2,0,1:T(8,128)} %copy_bitcast_fusion.1), calls=%async_computation | async-start | bytes 786432 | tf_op jit(solution)/shard_map/all_to_all | solution.py:212
  94.1 25.8 %all-to-all-start.3 = ((f32[2,16,8,256]{3,2,0,1:T(8,128)}), f32[2,16,8,256]{3,2,0,1:T(8,128)S(1)}, u32[]{:S(2)}, u32[]{:S(2)}) async-start(f32[2,16,8,256]{3,2,0,1:T(8,128)} %copy.236), calls=%async_computation.3 | async-start | bytes 524288 | tf_op jit(solution)/shard_map/all_to_all | solution.py:227
  119.9 16.1 %all-to-all-start.1 = ((f32[2,16,8,256]{3,2,0,1:T(8,128)}), f32[2,16,8,256]{3,2,0,1:T(8,128)S(1)}, u32[]{:S(2)}, u32[]{:S(2)}) async-start(f32[2,16,8,256]{3,2,0,1:T(8,128)} %copy.223), calls=%async_computation.1 | async-start | bytes 524288 | tf_op jit(solution)/shard_map/all_to_all | solution.py:227

commit v6 on v3

--- a/solution.py
+++ b/solution.py
@@ -190,20 +190,22 @@
     tail = flat[:, :, piece_bins:].reshape(parts, local_beams, pulse_count, piece_bins)[
         :, :, :, :need
     ]
-    pieces = jnp.transpose(jnp.concatenate([head, tail], axis=3), (0, 2, 1, 3))
+    pieces = jnp.transpose(jnp.concatenate([head, tail], axis=3), (2, 0, 1, 3))
     cross_rows = pulse_count * local_beams // 2
     tables = [row_table(section_rows(local_beams << bit), local_beams << bit, cross_rows) for bit in range(cross_sections)]
     tables = lax.optimization_barrier(tables)
-    level = lax.all_to_all(pieces, "pulse", split_axis=1, concat_axis=1, tiled=True)
+    level = lax.all_to_all(pieces, "pulse", split_axis=0, concat_axis=0, tiled=True)
     level, tables = lax.optimization_barrier((level, tables))
+    level = jnp.transpose(level, (1, 0, 2, 3))
     level = padded_lanes(level.reshape(parts, pulse_count * local_beams, piece_bins + need), piece_bins + need)
     level = split_kids(level, local_beams)
     for bit in range(cross_sections):
         section = local_sections + bit
         level = run_section(level, section, local_beams << bit, bit < cross_sections - 1, tables[bit])
     level = level[..., :piece_bins].reshape(parts, pulse_count, local_beams, piece_bins)
-    level = lax.all_to_all(level, "pulse", split_axis=1, concat_axis=3, tiled=True)
-    return level.reshape(parts, local_beams, bins)
+    level = jnp.transpose(level, (1, 0, 2, 3))
+    level = lax.all_to_all(level, "pulse", split_axis=0, concat_axis=0, tiled=True)
+    return jnp.transpose(level, (1, 2, 0, 3)).reshape(parts, local_beams, bins)
 
 
 def solution(mesh):

time: 113 us -> 113 us (level)
  no operation moved by 1% of the time
where the time goes in v6:
time: 113 us; the launch traced here: 112 us
  Pallas kernels  44.4 us (39%)
  local copies, waits for them, and re-layouts  20.4 us (18%)
  blocking collectives  19.7 us (17%)
  waiting for transfers between devices  11.9 us (11%)
  starting transfers between devices  8.66 us (8%)
  other arithmetic  5.82 us (5%)
    pallas_call x8, Pallas kernels, merge_call(): pl.pallas_call(functools.partial(merge_kernel, beams, chained), out_shape...  44.4 us
    all_to_all x1, blocking collectives, on_device(): lax.all_to_all(level, 'pulse', split_axis=0, concat_axis=0, tiled=True)  19.7 us
    all_to_all x1, waiting for transfers between devices, on_device(): lax.all_to_all(pieces, 'pulse', split_axis=0, concat_axis=0, tiled=True)  11.9 us
    broadcast_in_dim x10, local copies, waits for them, and re-layouts, row_table(): jnp.broadcast_to(per_row(packed, rows // beams)[..., None], (5, 2, 2, row...  8.85 us
    all_to_all x1, starting transfers between devices, on_device(): lax.all_to_all(pieces, 'pulse', split_axis=0, concat_axis=0, tiled=True)  7.38 us
  transfers between devices with their start and end apart: 2, of which 1 were waited for; matrix products, arithmetic and copies ran while one was open for 13% of the time, Pallas kernels for 0%

profile of v6, /device:TPU:0, one launch (start us, length us, event | category | flops | bytes accessed | tf_op | source)
XLA Modules:
  0.0 112.0 jit_solution(15642969879492581837)
XLA Ops:
  0.0 0.8 slice.124
  0.8 1.3 %collective-permute-start = (bf16[2,16,768]{2,1,0:T(8,128)(2,1)S(1)}, bf16[2,16,768]{2,1,0:T(8,128)(2,1)S(1)}, u32[]{:S(2)}, u32[]{:S(2)}) collective-permute-start(bf16[2,16,768]{2,1,0:T(8,128)(2,1)S(1)} %slice.124), channel_id=1, source_target_pairs={{1,0},{3,2},{5,4},{7,6},{9,8},{11,10},{13,12},{15,14},{17,16},{19,... | collective-permute-start | bytes 147464 | tf_op jit(solution)/shard_map/ppermute | solution.py:23
  2.1 0.8 slice_reduce_fusion
  2.9 0.8 select_reduce_fusion
  3.7 0.6 fusion.15
  4.3 0.7 constant_dynamic-update-slice_fusion.4
  5.0 0.7 constant_dynamic-update-slice_fusion.3
  5.7 0.7 constant_dynamic-update-slice_fusion.2
  6.4 0.7 tile.69
  7.2 0.4 reshape.71
  7.5 0.2 copy.52
  7.7 0.1 copy-done.2
  8.4 0.1 copy.56
  8.6 0.1 copy.57
  8.8 0.7 tile.67
  9.5 0.4 reshape.70
  9.9 0.2 copy.51
  10.0 0.4 copy-done.1
  10.4 0.2 reshape.69
  10.6 0.2 fusion.14
  11.0 0.8 fusion
  12.1 0.3 copy.53
  12.4 0.8 pad_maximum_fusion.3.kid_ref
  13.3 0.7 broadcast_in_dim.34.table_ref
  14.0 4.7 %shard_map.64.kid_ref = f32[2,2,8,4224]{3,2,1,0:T(8,128)} custom-call(f32[2,8]{1,0:T(2,128)} %bitcast.85, f32[2,2,8,4224]{3,2,1,0:T(8,128)} %pad_maximum_fusion.3.kid_ref, f32[5,2,2,8,128]{4,3,2,1,0:T(8,128)} %broadcast_in_dim.34.table_ref), custom_call_target="tpu_custom_call" | custom-call | flops 8110080 | bytes 1081344 | tf_op jit(solution)/shard_map/pallas_call | solution.py:107
  18.7 0.7 broadcast_in_dim.62.table_ref
  19.4 4.6 %shard_map.65.kid_ref = f32[2,2,8,4224]{3,2,1,0:T(8,128)} custom-call(f32[2,8]{1,0:T(2,128)} %bitcast.84, f32[2,2,8,4224]{3,2,1,0:T(8,128)} %shard_map.64.kid_ref, f32[5,2,2,8,128]{4,3,2,1,0:T(8,128)} %broadcast_in_dim.62.table_ref), custom_call_target="tpu_custom_call" | custom-call | flops 8110080 | bytes 1081344 | tf_op jit(solution)/shard_map/pallas_call | solution.py:107
  24.1 0.7 broadcast_in_dim.63.table_ref
  24.8 4.6 %shard_map.66.kid_ref = f32[2,2,8,4224]{3,2,1,0:T(8,128)} custom-call(f32[2,8]{1,0:T(2,128)} %bitcast.83, f32[2,2,8,4224]{3,2,1,0:T(8,128)} %shard_map.65.kid_ref, f32[5,2,2,8,128]{4,3,2,1,0:T(8,128)} %broadcast_in_dim.63.table_ref), custom_call_target="tpu_custom_call" | custom-call | flops 8110080 | bytes 1081344 | tf_op jit(solution)/shard_map/pallas_call | solution.py:107
  29.4 0.7 broadcast_in_dim.65.table_ref
  30.1 4.7 %shard_map.67 = f32[2,16,4224]{2,1,0:T(8,128)} custom-call(f32[2,8]{1,0:T(2,128)} %bitcast.82, f32[2,2,8,4224]{3,2,1,0:T(8,128)} %shard_map.66.kid_ref, f32[5,2,2,8,128]{4,3,2,1,0:T(8,128)} %broadcast_in_dim.65.table_ref), custom_call_target="tpu_custom_call" | custom-call | flops 8110080 | bytes 1081344 | tf_op jit(solution)/shard_map/pallas_call | solution.py:107
  34.8 1.1 %slice.177 = f32[2,16,4096]{2,1,0:T(8,128)S(1)} slice(f32[2,16,4224]{2,1,0:T(8,128)} %shard_map.67), slice={[0:2], [0:16], [0:4096]} | slice | bytes 1048576 | tf_op jit(solution)/shard_map/slice | solution.py:189
  36.1 0.2 copy.68
  36.4 1.0 maximum_bitcast_fusion.2
  37.4 7.4 %all-to-all-start = ((f32[16,2,16,316]{3,2,1,0:T(8,128)}), f32[16,2,16,316]{3,2,1,0:T(8,128)S(1)}, u32[]{:S(2)}, u32[]{:S(2)}) async-start(f32[16,2,16,316]{3,2,1,0:T(8,128)} %maximum_bitcast_fusion.2), calls=%async_computation | async-start | bytes 1572864 | tf_op jit(solution)/shard_map/all_to_all | solution.py:197
  45.7 1.5 %broadcast_in_dim.66.table_ref = f32[5,2,2,128,128]{4,3,2,1,0:T(8,128)} broadcast(f32[5,2,2,128]{3,2,1,0:T(2,128)S(1)} %tile.78), dimensions={0,1,2,3} | broadcast | bytes 1320960 | tf_op jit(solution)/shard_map/broadcast_in_dim | solution.py:140
  47.2 1.5 %broadcast_in_dim.67.table_ref = f32[5,2,2,128,128]{4,3,2,1,0:T(8,128)} broadcast(f32[5,2,2,128]{3,2,1,0:T(2,128)S(1)} %tile.81), dimensions={0,1,2,3} | broadcast | bytes 1320960 | tf_op jit(solution)/shard_map/broadcast_in_dim | solution.py:140
  48.6 1.5 %broadcast_in_dim.68.table_ref = f32[5,2,2,128,128]{4,3,2,1,0:T(8,128)} broadcast(f32[5,2,2,128]{3,2,1,0:T(2,128)S(1)} %tile.84), dimensions={0,1,2,3} | broadcast | bytes 1320960 | tf_op jit(solution)/shard_map/broadcast_in_dim | solution.py:140
  50.1 1.5 %broadcast_in_dim.70.table_ref = f32[5,2,2,128,128]{4,3,2,1,0:T(8,128)} broadcast(f32[5,2,2,128]{3,2,1,0:T(2,128)S(1)} %broadcast_in_dim.69), dimensions={0,1,2,3} | broadcast | bytes 1320960 | tf_op jit(solution)/shard_map/broadcast_in_dim | solution.py:140
  51.6 11.9 %all-to-all-done = f32[16,2,16,316]{3,2,1,0:T(8,128)S(1)} async-done(((f32[16,2,16,316]{3,2,1,0:T(8,128)}), f32[16,2,16,316]{3,2,1,0:T(8,128)S(1)}, u32[]{:S(2)}, u32[]{:S(2)}) %all-to-all-start) | async-done | bytes 647200 | tf_op jit(solution)/shard_map/all_to_all | solution.py:197
  63.7 0.9 pad_maximum_fusion.1.kid_ref
  64.7 6.4 %shard_map.68.kid_ref = f32[2,2,128,384]{3,2,1,0:T(8,128)} custom-call(f32[2,8]{1,0:T(2,128)} %bitcast.81, f32[2,2,128,384]{3,2,1,0:T(8,128)} %pad_maximum_fusion.1.kid_ref, f32[5,2,2,128,128]{4,3,2,1,0:T(8,128)} %broadcast_in_dim.66.table_ref), custom_call_target="tpu_custom_call" | custom-call | flops 11796480 | bytes 1572864 | tf_op jit(solution)/shard_map/pallas_call | solution.py:107
  71.1 6.4 %shard_map.69.kid_ref = f32[2,2,128,384]{3,2,1,0:T(8,128)} custom-call(f32[2,8]{1,0:T(2,128)} %bitcast.80, f32[2,2,128,384]{3,2,1,0:T(8,128)} %shard_map.68.kid_ref, f32[5,2,2,128,128]{4,3,2,1,0:T(8,128)} %broadcast_in_dim.67.table_ref), custom_call_target="tpu_custom_call" | custom-call | flops 11796480 | bytes 1572864 | tf_op jit(solution)/shard_map/pallas_call | solution.py:107
  77.5 6.4 %shard_map.70.kid_ref = f32[2,2,128,384]{3,2,1,0:T(8,128)} custom-call(f32[2,8]{1,0:T(2,128)} %bitcast.79, f32[2,2,128,384]{3,2,1,0:T(8,128)} %shard_map.69.kid_ref, f32[5,2,2,128,128]{4,3,2,1,0:T(8,128)} %broadcast_in_dim.68.table_ref), custom_call_target="tpu_custom_call" | custom-call | flops 11796480 | bytes 1572864 | tf_op jit(solution)/shard_map/pallas_call | solution.py:107
  83.9 6.4 %shard_map.71 = f32[2,256,384]{2,1,0:T(8,128)} custom-call(f32[2,8]{1,0:T(2,128)} %bitcast.78, f32[2,2,128,384]{3,2,1,0:T(8,128)} %shard_map.70.kid_ref, f32[5,2,2,128,128]{4,3,2,1,0:T(8,128)} %broadcast_in_dim.70.table_ref), custom_call_target="tpu_custom_call" | custom-call | flops 11796480 | bytes 1572864 | tf_op jit(solution)/shard_map/pallas_call | solution.py:107
  90.4 1.0 slice-done
  91.4 19.7 %all_to_all.10 = f32[16,2,16,256]{3,2,1,0:T(8,128)S(1)} all-to-all(f32[16,2,16,256]{3,2,1,0:T(8,128)S(1)} %bitcast.69), channel_id=1, replica_groups=mesh['pulse'=16,'range'=2] {'pulse'}, dimensions={0} | all-to-all | bytes 1048576 | tf_op jit(solution)/shard_map/all_to_all | solution.py:207
  111.2 0.8 copy.67
  (55 shorter events, 2.6 us)
Async XLA Ops:
  0.8 9.2 %collective-permute-start = (bf16[2,16,768]{2,1,0:T(8,128)(2,1)S(1)}, bf16[2,16,768]{2,1,0:T(8,128)(2,1)S(1)}, u32[]{:S(2)}, u32[]{:S(2)}) collective-permute-start(bf16[2,16,768]{2,1,0:T(8,128)(2,1)S(1)} %slice.124), channel_id=1, source_target_pairs={{1,0},{3,2},{5,4},{7,6},{9,8},{11,10},{13,12},{15,14},{17,16},{19,... | collective-permute-start | bytes 147464 | tf_op jit(solution)/shard_map/ppermute | solution.py:23
  7.1 0.7 copy-start.2
  9.4 1.0 copy-start.1
  34.8 1.2 %copy-start = (f32[2,16,4224]{2,1,0:T(8,128)S(1)}, f32[2,16,4224]{2,1,0:T(8,128)}, u32[]{:S(2)}) copy-start(f32[2,16,4224]{2,1,0:T(8,128)} %shard_map.67) | copy-start | bytes 1622020
  37.4 26.1 %all-to-all-start = ((f32[16,2,16,316]{3,2,1,0:T(8,128)}), f32[16,2,16,316]{3,2,1,0:T(8,128)S(1)}, u32[]{:S(2)}, u32[]{:S(2)}) async-start(f32[16,2,16,316]{3,2,1,0:T(8,128)} %maximum_bitcast_fusion.2), calls=%async_computation | async-start | bytes 1572864 | tf_op jit(solution)/shard_map/all_to_all | solution.py:197
  90.4 1.0 slice-start

commit v7 on v6

--- a/solution.py
+++ b/solution.py
@@ -23,16 +23,17 @@
     return lax.ppermute(shard, axis, pairs)
 
 
-def toeplitz_rows(vector, block, rows):
-    taps_len = vector.shape[0]
+def toeplitz_rows(filt, block, rows):
+    taps_len = filt.shape[1]
     width = rows + 1
-    line = jnp.concatenate([vector, jnp.zeros((width - taps_len,), vector.dtype)])
-    return jnp.tile(line, block)[: block * rows].reshape(block, rows)
+    line = jnp.concatenate([filt, jnp.zeros((filt.shape[0], width - taps_len), filt.dtype)], axis=1)
+    return jnp.tile(line, (1, block))[:, : block * rows].reshape(filt.shape[0], block, rows)
 
 
 def band_matrix(filt, block, rows):
-    real_band = toeplitz_rows(filt[0], block, rows).T
-    imag_band = toeplitz_rows(filt[1], block, rows).T
+    bands = toeplitz_rows(filt, block, rows)
+    real_band = bands[0].T
+    imag_band = bands[1].T
     upper = jnp.concatenate([real_band, imag_band], axis=1)
     lower = jnp.concatenate([-imag_band, real_band], axis=1)
     return jnp.concatenate([upper, lower], axis=0)
@@ -118,9 +119,11 @@
 
 
 def tap_weights(taps, weights):
-    reach = MARGIN - MAXOFF + 1
-    hit = taps[..., :, None] == jnp.arange(reach, dtype=taps.dtype)
-    return jnp.sum(jnp.where(hit, weights[..., :, None], 0.0), axis=-2)
+    spots = jnp.arange(MARGIN - MAXOFF + 1, dtype=taps.dtype)
+    total = jnp.where(taps[..., 0, None] == spots, weights[..., 0, None], 0.0)
+    for tap in range(1, taps.shape[-1]):
+        total = total + jnp.where(taps[..., tap, None] == spots, weights[..., tap, None], 0.0)
+    return total
 
 
 def per_row(table, groups):
@@ -169,8 +172,10 @@
     wide = jnp.concatenate([raw, rim], axis=2)
     level = padded_lanes(compress(wide, filt, blocks), bins + extra)
     all_weights = tap_weights(tap_index, tap_weight)
-    bits = [((beam_shift >> bit) & 1).astype(jnp.float32) for bit in range(3)]
-    all_rows = jnp.stack(bits + [jnp.cos(beam_phase), jnp.sin(beam_phase)])
+    kind = lax.broadcasted_iota(jnp.int32, (5,) + beam_shift.shape, 0)
+    bit_rows = ((beam_shift[None] >> jnp.minimum(kind, 2)) & 1).astype(jnp.float32)
+    angle_rows = jnp.where(kind == 3, jnp.cos(beam_phase)[None], jnp.sin(beam_phase)[None])
+    all_rows = jnp.where(kind < 3, bit_rows, angle_rows)
 
     def section_rows(beams):
         start = 2 * beams - 2

time: 113 us -> 122 us (1.080)
  local copies, waits for them, and re-layouts: 20.4 us -> 32.3 us
  other arithmetic: 5.82 us -> 3.16 us
    slice x4 -> x3, local copies, waits for them, and re-layouts: 1.44 us -> 10.2 us  [the longest x1 8.47 us: band_matrix(): imag_band = bands[1].T]
    unnamed x3 -> x0, other arithmetic: 2.09 us -> none
    squeeze x0 -> x5, local copies, waits for them, and re-layouts: none -> 1.67 us  [the longest x1 0.63 us: run_section(): all_weights[section]]
    another operation x5 -> x2, local copies, waits for them, and re-layouts: 1.53 us -> 2.46 us  [toeplitz_rows(): jnp.tile(line, (1, block))[:, :block * rows]]
  transfers between devices with their start and end apart: 2 -> 2, of which waited for: 1 -> 1; matrix products, arithmetic and copies ran while one was open for 13% -> 20% of each run, Pallas kernels for 0% -> 0%
where the time goes in v7:
time: 122 us; the launch traced here: 121 us
  Pallas kernels  44.2 us (36%)
  local copies, waits for them, and re-layouts  32.3 us (26%)
  blocking collectives  19.7 us (16%)
  waiting for transfers between devices  11.9 us (10%)
  starting transfers between devices  8.67 us (7%)
  other arithmetic  3.16 us (3%)
    pallas_call x8, Pallas kernels, merge_call(): pl.pallas_call(functools.partial(merge_kernel, beams, chained), out_shape...  44.2 us
    all_to_all x1, blocking collectives, on_device(): lax.all_to_all(level, 'pulse', split_axis=0, concat_axis=0, tiled=True)  19.7 us
    all_to_all x1, waiting for transfers between devices, on_device(): lax.all_to_all(pieces, 'pulse', split_axis=0, concat_axis=0, tiled=True)  11.9 us
    broadcast_in_dim x10, local copies, waits for them, and re-layouts, row_table(): jnp.broadcast_to(per_row(packed, rows // beams)[..., None], (5, 2, 2, row...  8.9 us
    slice x1, local copies, waits for them, and re-layouts, band_matrix(): imag_band = bands[1].T  8.47 us
    all_to_all x1, starting transfers between devices, on_device(): lax.all_to_all(pieces, 'pulse', split_axis=0, concat_axis=0, tiled=True)  7.39 us
    another operation x2, local copies, waits for them, and re-layouts, toeplitz_rows(): jnp.tile(line, (1, block))[:, :block * rows]  2.46 us
  transfers between devices with their start and end apart: 2, of which 1 were waited for; matrix products, arithmetic and copies ran while one was open for 20% of the time, Pallas kernels for 0%

profile of v7, /device:TPU:0, one launch (start us, length us, event | category | flops | bytes accessed | tf_op | source)
XLA Modules:
  0.0 121.1 jit_solution(3417256621554305581)
XLA Ops:
  0.0 0.8 slice.155
  0.8 1.3 %collective-permute-start = (bf16[2,16,768]{2,1,0:T(8,128)(2,1)S(1)}, bf16[2,16,768]{2,1,0:T(8,128)(2,1)S(1)}, u32[]{:S(2)}, u32[]{:S(2)}) collective-permute-start(bf16[2,16,768]{2,1,0:T(8,128)(2,1)S(1)} %slice.155), channel_id=1, source_target_pairs={{1,0},{3,2},{5,4},{7,6},{9,8},{11,10},{13,12},{15,14},{17,16},{19,... | collective-permute-start | bytes 147464 | tf_op jit(solution)/shard_map/ppermute | solution.py:23
  2.1 0.8 fusion.19
  3.3 0.8 fusion.20
  4.4 0.8 fusion.18
  5.2 0.7 concatenate.27
  6.0 2.4 %tile.58 = bf16[2,196864]{1,0:T(2,128)(2,1)S(1)} reshape(bf16[2,256,769]{2,1,0:T(8,128)(2,1)S(1)} %tile.57) | data formatting | bytes 1574912 | tf_op jit(solution)/shard_map/tile | solution.py:30
  8.4 8.5 %slice_reduce_fusion = (bf16[196608]{0:T(1024)(128)(2,1)S(1)}, bf16[196608]{0:T(1024)(128)(2,1)S(1)}) fusion(bf16[2,196864]{1,0:T(2,128)(2,1)S(1)} %tile.58), kind=kLoop, calls=%fused_computation.12 | loop fusion | bytes 1572864 | tf_op jit(solution)/shard_map/slice | solution.py:36
  16.9 0.4 squeeze.47
  17.2 0.2 copy.64
  17.4 0.1 copy-done.4
  17.6 0.1 fusion.12
  17.8 0.6 slice_bitcast_fusion.2
  18.8 0.1 copy.68
  19.0 0.1 copy.69
  19.1 0.4 squeeze.46
  19.5 0.2 copy.63
  19.7 0.2 reshape.71
  19.9 0.2 fusion.17
  20.3 0.8 fusion
  21.3 0.3 copy.65
  21.7 0.8 pad_maximum_fusion.3.kid_ref
  22.6 0.7 broadcast_in_dim.117.table_ref
  23.3 4.7 %shard_map.64.kid_ref = f32[2,2,8,4224]{3,2,1,0:T(8,128)} custom-call(f32[2,8]{1,0:T(2,128)} %get-tuple-element.36.weight_ref, f32[2,2,8,4224]{3,2,1,0:T(8,128)} %pad_maximum_fusion.3.kid_ref, f32[5,2,2,8,128]{4,3,2,1,0:T(8,128)} %broadcast_in_dim.117.table_ref), custom_call_target="tpu_custom_call" | custom-call | flops 8110080 | bytes 1081344 | tf_op jit(solution)/shard_map/pallas_call | solution.py:108
  28.0 0.7 broadcast_in_dim.118.table_ref
  28.7 4.6 %shard_map.65.kid_ref = f32[2,2,8,4224]{3,2,1,0:T(8,128)} custom-call(f32[2,8]{1,0:T(2,128)} %get-tuple-element.37.weight_ref, f32[2,2,8,4224]{3,2,1,0:T(8,128)} %shard_map.64.kid_ref, f32[5,2,2,8,128]{4,3,2,1,0:T(8,128)} %broadcast_in_dim.118.table_ref), custom_call_target="tpu_custom_call" | custom-call | flops 8110080 | bytes 1081344 | tf_op jit(solution)/shard_map/pallas_call | solution.py:108
  33.3 0.7 broadcast_in_dim.119.table_ref
  34.1 4.6 %shard_map.66.kid_ref = f32[2,2,8,4224]{3,2,1,0:T(8,128)} custom-call(f32[2,8]{1,0:T(2,128)} %get-tuple-element.38.weight_ref, f32[2,2,8,4224]{3,2,1,0:T(8,128)} %shard_map.65.kid_ref, f32[5,2,2,8,128]{4,3,2,1,0:T(8,128)} %broadcast_in_dim.119.table_ref), custom_call_target="tpu_custom_call" | custom-call | flops 8110080 | bytes 1081344 | tf_op jit(solution)/shard_map/pallas_call | solution.py:108
  38.7 0.7 broadcast_in_dim.121.table_ref
  39.4 4.5 %shard_map.67 = f32[2,16,4224]{2,1,0:T(8,128)} custom-call(f32[2,8]{1,0:T(2,128)} %get-tuple-element.39.weight_ref, f32[2,2,8,4224]{3,2,1,0:T(8,128)} %shard_map.66.kid_ref, f32[5,2,2,8,128]{4,3,2,1,0:T(8,128)} %broadcast_in_dim.121.table_ref), custom_call_target="tpu_custom_call" | custom-call | flops 8110080 | bytes 1081344 | tf_op jit(solution)/shard_map/pallas_call | solution.py:108
  43.9 1.1 slice.206
  45.2 0.2 copy.80
  45.5 1.0 maximum_bitcast_fusion.2
  46.5 7.4 %all-to-all-start = ((f32[16,2,16,316]{3,2,1,0:T(8,128)}), f32[16,2,16,316]{3,2,1,0:T(8,128)S(1)}, u32[]{:S(2)}, u32[]{:S(2)}) async-start(f32[16,2,16,316]{3,2,1,0:T(8,128)} %maximum_bitcast_fusion.2), calls=%async_computation | async-start | bytes 1572864 | tf_op jit(solution)/shard_map/all_to_all | solution.py:202
  54.8 0.1 tile.67
  54.9 1.5 %broadcast_in_dim.122.table_ref = f32[5,2,2,128,128]{4,3,2,1,0:T(8,128)} broadcast(f32[5,2,2,128]{3,2,1,0:T(2,128)S(1)} %tile.67), dimensions={0,1,2,3} | broadcast | bytes 1320960 | tf_op jit(solution)/shard_map/broadcast_in_dim | solution.py:143
  56.3 1.5 %broadcast_in_dim.123.table_ref = f32[5,2,2,128,128]{4,3,2,1,0:T(8,128)} broadcast(f32[5,2,2,128]{3,2,1,0:T(2,128)S(1)} %tile.70), dimensions={0,1,2,3} | broadcast | bytes 1320960 | tf_op jit(solution)/shard_map/broadcast_in_dim | solution.py:143
  57.8 1.5 %broadcast_in_dim.124.table_ref = f32[5,2,2,128,128]{4,3,2,1,0:T(8,128)} broadcast(f32[5,2,2,128]{3,2,1,0:T(2,128)S(1)} %tile.73), dimensions={0,1,2,3} | broadcast | bytes 1320960 | tf_op jit(solution)/shard_map/broadcast_in_dim | solution.py:143
  59.3 1.5 %broadcast_in_dim.126.table_ref = f32[5,2,2,128,128]{4,3,2,1,0:T(8,128)} broadcast(f32[5,2,2,128]{3,2,1,0:T(2,128)S(1)} %broadcast_in_dim.125), dimensions={0,1,2,3} | broadcast | bytes 1320960 | tf_op jit(solution)/shard_map/broadcast_in_dim | solution.py:143
  60.8 11.9 %all-to-all-done = f32[16,2,16,316]{3,2,1,0:T(8,128)S(1)} async-done(((f32[16,2,16,316]{3,2,1,0:T(8,128)}), f32[16,2,16,316]{3,2,1,0:T(8,128)S(1)}, u32[]{:S(2)}, u32[]{:S(2)}) %all-to-all-start) | async-done | bytes 647200 | tf_op jit(solution)/shard_map/all_to_all | solution.py:202
  72.8 0.9 pad_maximum_fusion.1.kid_ref
  73.8 6.4 %shard_map.68.kid_ref = f32[2,2,128,384]{3,2,1,0:T(8,128)} custom-call(f32[2,8]{1,0:T(2,128)} %get-tuple-element.40.weight_ref, f32[2,2,128,384]{3,2,1,0:T(8,128)} %pad_maximum_fusion.1.kid_ref, f32[5,2,2,128,128]{4,3,2,1,0:T(8,128)} %broadcast_in_dim.122.table_ref), custom_call_target="tpu_custom_call" | custom-call | flops 11796480 | bytes 1572864 | tf_op jit(solution)/shard_map/pallas_call | solution.py:108
  80.2 6.4 %shard_map.69.kid_ref = f32[2,2,128,384]{3,2,1,0:T(8,128)} custom-call(f32[2,8]{1,0:T(2,128)} %get-tuple-element.41.weight_ref, f32[2,2,128,384]{3,2,1,0:T(8,128)} %shard_map.68.kid_ref, f32[5,2,2,128,128]{4,3,2,1,0:T(8,128)} %broadcast_in_dim.123.table_ref), custom_call_target="tpu_custom_call" | custom-call | flops 11796480 | bytes 1572864 | tf_op jit(solution)/shard_map/pallas_call | solution.py:108
  86.6 6.4 %shard_map.70.kid_ref = f32[2,2,128,384]{3,2,1,0:T(8,128)} custom-call(f32[2,8]{1,0:T(2,128)} %get-tuple-element.42.weight_ref, f32[2,2,128,384]{3,2,1,0:T(8,128)} %shard_map.69.kid_ref, f32[5,2,2,128,128]{4,3,2,1,0:T(8,128)} %broadcast_in_dim.124.table_ref), custom_call_target="tpu_custom_call" | custom-call | flops 11796480 | bytes 1572864 | tf_op jit(solution)/shard_map/pallas_call | solution.py:108
  93.0 6.4 %shard_map.71 = f32[2,256,384]{2,1,0:T(8,128)} custom-call(f32[2,8]{1,0:T(2,128)} %get-tuple-element.43.weight_ref, f32[2,2,128,384]{3,2,1,0:T(8,128)} %shard_map.70.kid_ref, f32[5,2,2,128,128]{4,3,2,1,0:T(8,128)} %broadcast_in_dim.126.table_ref), custom_call_target="tpu_custom_call" | custom-call | flops 11796480 | bytes 1572864 | tf_op jit(solution)/shard_map/pallas_call | solution.py:108
  99.5 1.0 slice-done
  100.5 19.7 %all_to_all.10 = f32[16,2,16,256]{3,2,1,0:T(8,128)S(1)} all-to-all(f32[16,2,16,256]{3,2,1,0:T(8,128)S(1)} %bitcast.75), channel_id=1, replica_groups=mesh['pulse'=16,'range'=2] {'pulse'}, dimensions={0} | all-to-all | bytes 1048576 | tf_op jit(solution)/shard_map/all_to_all | solution.py:212
  120.3 0.8 copy.79
  (64 shorter events, 3.1 us)
Async XLA Ops:
  0.8 18.8 %collective-permute-start = (bf16[2,16,768]{2,1,0:T(8,128)(2,1)S(1)}, bf16[2,16,768]{2,1,0:T(8,128)(2,1)S(1)}, u32[]{:S(2)}, u32[]{:S(2)}) collective-permute-start(bf16[2,16,768]{2,1,0:T(8,128)(2,1)S(1)} %slice.155), channel_id=1, source_target_pairs={{1,0},{3,2},{5,4},{7,6},{9,8},{11,10},{13,12},{15,14},{17,16},{19,... | collective-permute-start | bytes 147464 | tf_op jit(solution)/shard_map/ppermute | solution.py:23
  16.8 0.7 copy-start.4
  17.4 2.3 %copy-start.1 = (bf16[2,16,4096]{2,1,0:T(8,128)(2,1)S(1)}, bf16[2,16,4096]{2,1,0:T(8,128)(2,1)}, u32[]{:S(2)}) copy-start(bf16[2,16,4096]{2,1,0:T(8,128)(2,1)} %param.6) | copy-start | bytes 786436
  17.6 2.3 %copy-start.2 = (f32[5,2,510]{2,1,0:T(2,128)}, f32[5,2,510]{2,1,0:T(2,128)S(1)}, u32[]{:S(2)}) copy-start(f32[5,2,510]{2,1,0:T(2,128)S(1)} %select_select_fusion) | copy-start | bytes 61204
  21.7 0.9 slice-start.1
  43.9 1.2 copy-start
  45.5 8.4 %copy-start.3 = (f32[5,2,510]{2,1,0:T(2,128)S(1)}, f32[5,2,510]{2,1,0:T(2,128)}, u32[]{:S(2)}) copy-start(f32[5,2,510]{2,1,0:T(2,128)} %copy-done.2) | copy-start | bytes 61204
  46.5 26.1 %all-to-all-start = ((f32[16,2,16,316]{3,2,1,0:T(8,128)}), f32[16,2,16,316]{3,2,1,0:T(8,128)S(1)}, u32[]{:S(2)}, u32[]{:S(2)}) async-start(f32[16,2,16,316]{3,2,1,0:T(8,128)} %maximum_bitcast_fusion.2), calls=%async_computation | async-start | bytes 1572864 | tf_op jit(solution)/shard_map/all_to_all | solution.py:202
  99.4 1.0 slice-start

commit v8 on v7

--- a/solution.py
+++ b/solution.py
@@ -23,17 +23,16 @@
     return lax.ppermute(shard, axis, pairs)
 
 
-def toeplitz_rows(filt, block, rows):
-    taps_len = filt.shape[1]
+def toeplitz_rows(vector, block, rows):
+    taps_len = vector.shape[0]
     width = rows + 1
-    line = jnp.concatenate([filt, jnp.zeros((filt.shape[0], width - taps_len), filt.dtype)], axis=1)
-    return jnp.tile(line, (1, block))[:, : block * rows].reshape(filt.shape[0], block, rows)
+    line = jnp.concatenate([vector, jnp.zeros((width - taps_len,), vector.dtype)])
+    return jnp.tile(line, block)[: block * rows].reshape(block, rows)
 
 
 def band_matrix(filt, block, rows):
-    bands = toeplitz_rows(filt, block, rows)
-    real_band = bands[0].T
-    imag_band = bands[1].T
+    real_band = toeplitz_rows(filt[0], block, rows).T
+    imag_band = toeplitz_rows(filt[1], block, rows).T
     upper = jnp.concatenate([real_band, imag_band], axis=1)
     lower = jnp.concatenate([-imag_band, real_band], axis=1)
     return jnp.concatenate([upper, lower], axis=0)

time: 122 us -> 113 us (0.926)
  local copies, waits for them, and re-layouts: 32.3 us -> 23.4 us
    slice x1 -> x3, local copies, waits for them, and re-layouts: 8.47 us -> 0.83 us  [the longest x1 0.78 us: band_matrix(): imag_band = toeplitz_rows(filt[1], block, rows).T]
    another operation x2 -> x4, local copies, waits for them, and re-layouts: 2.46 us -> 1.45 us  [toeplitz_rows(): return jnp.tile(line, block)[:block * rows].reshape(block, rows)]
  transfers between devices with their start and end apart: 2 -> 2, of which waited for: 1 -> 1; matrix products, arithmetic and copies ran while one was open for 20% -> 13% of each run, Pallas kernels for 0% -> 0%
where the time goes in v8:
time: 113 us; the launch traced here: 112 us
  Pallas kernels  44.3 us (39%)
  local copies, waits for them, and re-layouts  23.4 us (21%)
  blocking collectives  19.7 us (17%)
  waiting for transfers between devices  11.9 us (11%)
  starting transfers between devices  8.66 us (8%)
  other arithmetic  3.16 us (3%)
    pallas_call x8, Pallas kernels, merge_call(): pl.pallas_call(functools.partial(merge_kernel, beams, chained), out_shape...  44.3 us
    all_to_all x1, blocking collectives, on_device(): lax.all_to_all(level, 'pulse', split_axis=0, concat_axis=0, tiled=True)  19.7 us
    all_to_all x1, waiting for transfers between devices, on_device(): lax.all_to_all(pieces, 'pulse', split_axis=0, concat_axis=0, tiled=True)  11.9 us
    broadcast_in_dim x10, local copies, waits for them, and re-layouts, row_table(): jnp.broadcast_to(per_row(packed, rows // beams)[..., None], (5, 2, 2, row...  8.9 us
    all_to_all x1, starting transfers between devices, on_device(): lax.all_to_all(pieces, 'pulse', split_axis=0, concat_axis=0, tiled=True)  7.38 us
  transfers between devices with their start and end apart: 2, of which 1 were waited for; matrix products, arithmetic and copies ran while one was open for 13% of the time, Pallas kernels for 0%

profile of v8, /device:TPU:0, one launch (start us, length us, event | category | flops | bytes accessed | tf_op | source)
XLA Modules:
  0.0 112.3 jit_solution(11436062877139675278)
XLA Ops:
  0.0 0.8 slice.156
  0.8 1.3 %collective-permute-start = (bf16[2,16,768]{2,1,0:T(8,128)(2,1)S(1)}, bf16[2,16,768]{2,1,0:T(8,128)(2,1)S(1)}, u32[]{:S(2)}, u32[]{:S(2)}) collective-permute-start(bf16[2,16,768]{2,1,0:T(8,128)(2,1)S(1)} %slice.156), channel_id=1, source_target_pairs={{1,0},{3,2},{5,4},{7,6},{9,8},{11,10},{13,12},{15,14},{17,16},{19,... | collective-permute-start | bytes 147464 | tf_op jit(solution)/shard_map/ppermute | solution.py:23
  2.1 0.8 slice_reduce_fusion
  2.9 0.8 fusion.19
  4.1 0.8 fusion.20
  5.2 0.8 fusion.18
  6.0 0.7 tile.69
  6.8 0.4 reshape.72
  7.1 0.2 copy.64
  7.4 0.1 copy-done.4
  7.6 0.1 fusion.12
  7.7 0.6 slice_bitcast_fusion.2
  8.7 0.1 copy.68
  8.9 0.1 copy.69
  9.1 0.7 tile.67
  9.8 0.4 reshape.71
  10.2 0.2 copy.63
  10.4 0.4 copy-done.1
  10.8 0.2 reshape.70
  11.0 0.2 fusion.17
  11.4 0.8 fusion
  12.4 0.3 copy.65
  12.8 0.8 pad_maximum_fusion.3.kid_ref
  13.6 0.7 broadcast_in_dim.116.table_ref
  14.3 4.7 %shard_map.64.kid_ref = f32[2,2,8,4224]{3,2,1,0:T(8,128)} custom-call(f32[2,8]{1,0:T(2,128)} %get-tuple-element.36.weight_ref, f32[2,2,8,4224]{3,2,1,0:T(8,128)} %pad_maximum_fusion.3.kid_ref, f32[5,2,2,8,128]{4,3,2,1,0:T(8,128)} %broadcast_in_dim.116.table_ref), custom_call_target="tpu_custom_call" | custom-call | flops 8110080 | bytes 1081344 | tf_op jit(solution)/shard_map/pallas_call | solution.py:107
  19.1 0.7 broadcast_in_dim.117.table_ref
  19.8 4.6 %shard_map.65.kid_ref = f32[2,2,8,4224]{3,2,1,0:T(8,128)} custom-call(f32[2,8]{1,0:T(2,128)} %get-tuple-element.37.weight_ref, f32[2,2,8,4224]{3,2,1,0:T(8,128)} %shard_map.64.kid_ref, f32[5,2,2,8,128]{4,3,2,1,0:T(8,128)} %broadcast_in_dim.117.table_ref), custom_call_target="tpu_custom_call" | custom-call | flops 8110080 | bytes 1081344 | tf_op jit(solution)/shard_map/pallas_call | solution.py:107
  24.4 0.7 broadcast_in_dim.118.table_ref
  25.1 4.6 %shard_map.66.kid_ref = f32[2,2,8,4224]{3,2,1,0:T(8,128)} custom-call(f32[2,8]{1,0:T(2,128)} %get-tuple-element.38.weight_ref, f32[2,2,8,4224]{3,2,1,0:T(8,128)} %shard_map.65.kid_ref, f32[5,2,2,8,128]{4,3,2,1,0:T(8,128)} %broadcast_in_dim.118.table_ref), custom_call_target="tpu_custom_call" | custom-call | flops 8110080 | bytes 1081344 | tf_op jit(solution)/shard_map/pallas_call | solution.py:107
  29.7 0.7 broadcast_in_dim.120.table_ref
  30.4 4.7 %shard_map.67 = f32[2,16,4224]{2,1,0:T(8,128)} custom-call(f32[2,8]{1,0:T(2,128)} %get-tuple-element.39.weight_ref, f32[2,2,8,4224]{3,2,1,0:T(8,128)} %shard_map.66.kid_ref, f32[5,2,2,8,128]{4,3,2,1,0:T(8,128)} %broadcast_in_dim.120.table_ref), custom_call_target="tpu_custom_call" | custom-call | flops 8110080 | bytes 1081344 | tf_op jit(solution)/shard_map/pallas_call | solution.py:107
  35.2 1.1 %slice.209 = f32[2,16,4096]{2,1,0:T(8,128)S(1)} slice(f32[2,16,4224]{2,1,0:T(8,128)} %shard_map.67), slice={[0:2], [0:16], [0:4096]} | slice | bytes 1048576 | tf_op jit(solution)/shard_map/slice | solution.py:193
  36.4 0.2 copy.80
  36.8 1.0 maximum_bitcast_fusion.2
  37.8 7.4 %all-to-all-start = ((f32[16,2,16,316]{3,2,1,0:T(8,128)}), f32[16,2,16,316]{3,2,1,0:T(8,128)S(1)}, u32[]{:S(2)}, u32[]{:S(2)}) async-start(f32[16,2,16,316]{3,2,1,0:T(8,128)} %maximum_bitcast_fusion.2), calls=%async_computation | async-start | bytes 1572864 | tf_op jit(solution)/shard_map/all_to_all | solution.py:201
  46.1 1.5 %broadcast_in_dim.121.table_ref = f32[5,2,2,128,128]{4,3,2,1,0:T(8,128)} broadcast(f32[5,2,2,128]{3,2,1,0:T(2,128)S(1)} %tile.78), dimensions={0,1,2,3} | broadcast | bytes 1320960 | tf_op jit(solution)/shard_map/broadcast_in_dim | solution.py:142
  47.6 1.5 %broadcast_in_dim.122.table_ref = f32[5,2,2,128,128]{4,3,2,1,0:T(8,128)} broadcast(f32[5,2,2,128]{3,2,1,0:T(2,128)S(1)} %tile.81), dimensions={0,1,2,3} | broadcast | bytes 1320960 | tf_op jit(solution)/shard_map/broadcast_in_dim | solution.py:142
  49.0 1.5 %broadcast_in_dim.123.table_ref = f32[5,2,2,128,128]{4,3,2,1,0:T(8,128)} broadcast(f32[5,2,2,128]{3,2,1,0:T(2,128)S(1)} %tile.84), dimensions={0,1,2,3} | broadcast | bytes 1320960 | tf_op jit(solution)/shard_map/broadcast_in_dim | solution.py:142
  50.5 1.5 %broadcast_in_dim.125.table_ref = f32[5,2,2,128,128]{4,3,2,1,0:T(8,128)} broadcast(f32[5,2,2,128]{3,2,1,0:T(2,128)S(1)} %broadcast_in_dim.124), dimensions={0,1,2,3} | broadcast | bytes 1320960 | tf_op jit(solution)/shard_map/broadcast_in_dim | solution.py:142
  52.0 11.9 %all-to-all-done = f32[16,2,16,316]{3,2,1,0:T(8,128)S(1)} async-done(((f32[16,2,16,316]{3,2,1,0:T(8,128)}), f32[16,2,16,316]{3,2,1,0:T(8,128)S(1)}, u32[]{:S(2)}, u32[]{:S(2)}) %all-to-all-start) | async-done | bytes 647200 | tf_op jit(solution)/shard_map/all_to_all | solution.py:201
  64.1 0.9 pad_maximum_fusion.1.kid_ref
  65.0 6.4 %shard_map.68.kid_ref = f32[2,2,128,384]{3,2,1,0:T(8,128)} custom-call(f32[2,8]{1,0:T(2,128)} %get-tuple-element.40.weight_ref, f32[2,2,128,384]{3,2,1,0:T(8,128)} %pad_maximum_fusion.1.kid_ref, f32[5,2,2,128,128]{4,3,2,1,0:T(8,128)} %broadcast_in_dim.121.table_ref), custom_call_target="tpu_custom_call" | custom-call | flops 11796480 | bytes 1572864 | tf_op jit(solution)/shard_map/pallas_call | solution.py:107
  71.4 6.4 %shard_map.69.kid_ref = f32[2,2,128,384]{3,2,1,0:T(8,128)} custom-call(f32[2,8]{1,0:T(2,128)} %get-tuple-element.41.weight_ref, f32[2,2,128,384]{3,2,1,0:T(8,128)} %shard_map.68.kid_ref, f32[5,2,2,128,128]{4,3,2,1,0:T(8,128)} %broadcast_in_dim.122.table_ref), custom_call_target="tpu_custom_call" | custom-call | flops 11796480 | bytes 1572864 | tf_op jit(solution)/shard_map/pallas_call | solution.py:107
  77.8 6.4 %shard_map.70.kid_ref = f32[2,2,128,384]{3,2,1,0:T(8,128)} custom-call(f32[2,8]{1,0:T(2,128)} %get-tuple-element.42.weight_ref, f32[2,2,128,384]{3,2,1,0:T(8,128)} %shard_map.69.kid_ref, f32[5,2,2,128,128]{4,3,2,1,0:T(8,128)} %broadcast_in_dim.123.table_ref), custom_call_target="tpu_custom_call" | custom-call | flops 11796480 | bytes 1572864 | tf_op jit(solution)/shard_map/pallas_call | solution.py:107
  84.2 6.4 %shard_map.71 = f32[2,256,384]{2,1,0:T(8,128)} custom-call(f32[2,8]{1,0:T(2,128)} %get-tuple-element.43.weight_ref, f32[2,2,128,384]{3,2,1,0:T(8,128)} %shard_map.70.kid_ref, f32[5,2,2,128,128]{4,3,2,1,0:T(8,128)} %broadcast_in_dim.125.table_ref), custom_call_target="tpu_custom_call" | custom-call | flops 11796480 | bytes 1572864 | tf_op jit(solution)/shard_map/pallas_call | solution.py:107
  90.7 1.0 slice-done
  91.8 19.7 %all_to_all.10 = f32[16,2,16,256]{3,2,1,0:T(8,128)S(1)} all-to-all(f32[16,2,16,256]{3,2,1,0:T(8,128)S(1)} %bitcast.75), channel_id=1, replica_groups=mesh['pulse'=16,'range'=2] {'pulse'}, dimensions={0} | all-to-all | bytes 1048576 | tf_op jit(solution)/shard_map/all_to_all | solution.py:211
  111.5 0.8 copy.79
  (69 shorter events, 3.2 us)
Async XLA Ops:
  0.8 9.6 %collective-permute-start = (bf16[2,16,768]{2,1,0:T(8,128)(2,1)S(1)}, bf16[2,16,768]{2,1,0:T(8,128)(2,1)S(1)}, u32[]{:S(2)}, u32[]{:S(2)}) collective-permute-start(bf16[2,16,768]{2,1,0:T(8,128)(2,1)S(1)} %slice.156), channel_id=1, source_target_pairs={{1,0},{3,2},{5,4},{7,6},{9,8},{11,10},{13,12},{15,14},{17,16},{19,... | collective-permute-start | bytes 147464 | tf_op jit(solution)/shard_map/ppermute | solution.py:23
  6.8 0.7 copy-start.4
  7.6 2.6 %copy-start.2 = (f32[5,2,510]{2,1,0:T(2,128)}, f32[5,2,510]{2,1,0:T(2,128)S(1)}, u32[]{:S(2)}) copy-start(f32[5,2,510]{2,1,0:T(2,128)S(1)} %select_select_fusion) | copy-start | bytes 61204
  9.8 1.0 copy-start.1
  12.7 0.9 slice-start.1
  35.2 1.2 %copy-start = (f32[2,16,4224]{2,1,0:T(8,128)S(1)}, f32[2,16,4224]{2,1,0:T(8,128)}, u32[]{:S(2)}) copy-start(f32[2,16,4224]{2,1,0:T(8,128)} %shard_map.67) | copy-start | bytes 1622020
  36.8 8.4 %copy-start.3 = (f32[5,2,510]{2,1,0:T(2,128)S(1)}, f32[5,2,510]{2,1,0:T(2,128)}, u32[]{:S(2)}) copy-start(f32[5,2,510]{2,1,0:T(2,128)} %copy-done.2) | copy-start | bytes 61204
  37.8 26.1 %all-to-all-start = ((f32[16,2,16,316]{3,2,1,0:T(8,128)}), f32[16,2,16,316]{3,2,1,0:T(8,128)S(1)}, u32[]{:S(2)}, u32[]{:S(2)}) async-start(f32[16,2,16,316]{3,2,1,0:T(8,128)} %maximum_bitcast_fusion.2), calls=%async_computation | async-start | bytes 1572864 | tf_op jit(solution)/shard_map/all_to_all | solution.py:201
  90.7 1.0 slice-start

commit v9 on v8

--- a/solution.py
+++ b/solution.py
@@ -206,10 +206,16 @@
     for bit in range(cross_sections):
         section = local_sections + bit
         level = run_section(level, section, local_beams << bit, bit < cross_sections - 1, tables[bit])
-    level = level[..., :piece_bins].reshape(parts, pulse_count, local_beams, piece_bins)
-    level = jnp.transpose(level, (1, 0, 2, 3))
-    level = lax.all_to_all(level, "pulse", split_axis=0, concat_axis=0, tiled=True)
-    return jnp.transpose(level, (1, 2, 0, 3)).reshape(parts, local_beams, bins)
+    blocks = level[..., :piece_bins].reshape(parts, pulse_count, local_beams, piece_bins)
+    me = lax.axis_index("pulse")
+    received = [lax.dynamic_index_in_dim(blocks, me, axis=1, keepdims=False)]
+    for step in range(1, pulse_count):
+        outgoing = lax.dynamic_index_in_dim(blocks, (me + step) % pulse_count, axis=1, keepdims=False)
+        pairs = [(i, (i + step) % pulse_count) for i in range(pulse_count)]
+        received.append(lax.ppermute(outgoing, "pulse", pairs))
+    by_offset = jnp.stack([received[(pulse_count - j) % pulse_count] for j in range(pulse_count)], axis=2)
+    ordered = jnp.roll(by_offset, me, axis=2)
+    return ordered.reshape(parts, local_beams, bins)
 
 
 def solution(mesh):

time: 113 us -> 122 us (1.080)
  starting transfers between devices: 8.66 us -> 30.1 us
  blocking collectives: 19.7 us -> 0 us
  waiting for transfers between devices: 11.9 us -> 17.3 us
  local copies, waits for them, and re-layouts: 23.4 us -> 24.7 us
    ppermute x0 -> x15, starting transfers between devices: none -> 21.4 us  [on_device(): received.append(lax.ppermute(outgoing, 'pulse', pairs))]
    all_to_all x1 -> x0, blocking collectives: 19.7 us -> none  [on_device(): lax.all_to_all(level, 'pulse', split_axis=0, concat_axis=0, tiled=True)]
    ppermute x0 -> x15, waiting for transfers between devices: none -> 5.59 us  [on_device(): received.append(lax.ppermute(outgoing, 'pulse', pairs))]
    concatenate x0 -> x1, local copies, waits for them, and re-layouts: none -> 1.83 us  [on_device(): ordered = jnp.roll(by_offset, me, axis=2)]
  transfers between devices with their start and end apart: 2 -> 17, of which waited for: 1 -> 5; matrix products, arithmetic and copies ran while one was open for 13% -> 12% of each run, Pallas kernels for 0% -> 0%
where the time goes in v9:
time: 122 us; the launch traced here: 121 us
  Pallas kernels  44.5 us (36%)
  starting transfers between devices  30.1 us (25%)
  local copies, waits for them, and re-layouts  24.7 us (20%)
  waiting for transfers between devices  17.3 us (14%)
  other arithmetic  3.2 us (3%)
    pallas_call x8, Pallas kernels, merge_call(): pl.pallas_call(functools.partial(merge_kernel, beams, chained), out_shape...  44.5 us
    ppermute x15, starting transfers between devices, on_device(): received.append(lax.ppermute(outgoing, 'pulse', pairs))  21.4 us
    all_to_all x1, waiting for transfers between devices, on_device(): lax.all_to_all(pieces, 'pulse', split_axis=0, concat_axis=0, tiled=True)  11.7 us
    broadcast_in_dim x10, local copies, waits for them, and re-layouts, row_table(): jnp.broadcast_to(per_row(packed, rows // beams)[..., None], (5, 2, 2, row...  8.94 us
    all_to_all x1, starting transfers between devices, on_device(): lax.all_to_all(pieces, 'pulse', split_axis=0, concat_axis=0, tiled=True)  7.38 us
    ppermute x15, waiting for transfers between devices, on_device(): received.append(lax.ppermute(outgoing, 'pulse', pairs))  5.59 us
  transfers between devices with their start and end apart: 17, of which 5 were waited for; matrix products, arithmetic and copies ran while one was open for 12% of the time, Pallas kernels for 0%

profile of v9, /device:TPU:0, one launch (start us, length us, event | category | flops | bytes accessed | tf_op | source)
XLA Modules:
  0.0 121.3 jit_solution(10486968737311339418)
XLA Ops:
  0.0 0.8 slice.156
  0.8 1.3 %collective-permute-start = (bf16[2,16,768]{2,1,0:T(8,128)(2,1)S(1)}, bf16[2,16,768]{2,1,0:T(8,128)(2,1)S(1)}, u32[]{:S(2)}, u32[]{:S(2)}) collective-permute-start(bf16[2,16,768]{2,1,0:T(8,128)(2,1)S(1)} %slice.156), channel_id=1, source_target_pairs={{1,0},{3,2},{5,4},{7,6},{9,8},{11,10},{13,12},{15,14},{17,16},{19,... | collective-permute-start | bytes 147464 | tf_op jit(solution)/shard_map/ppermute | solution.py:23
  2.1 0.8 fusion.20
  3.0 0.8 fusion.19
  4.4 0.8 slice_reduce_fusion
  5.3 0.7 tile.69
  7.0 0.6 slice_bitcast_fusion.2
  7.9 0.7 tile.67
  10.4 0.8 fusion
  11.8 0.8 pad_maximum_fusion.3.kid_ref
  12.6 0.7 broadcast_in_dim.116.table_ref
  13.3 4.7 %shard_map.64.kid_ref = f32[2,2,8,4224]{3,2,1,0:T(8,128)} custom-call(f32[2,8]{1,0:T(2,128)} %get-tuple-element.52.weight_ref, f32[2,2,8,4224]{3,2,1,0:T(8,128)} %pad_maximum_fusion.3.kid_ref, f32[5,2,2,8,128]{4,3,2,1,0:T(8,128)} %broadcast_in_dim.116.table_ref), custom_call_target="tpu_custom_call" | custom-call | flops 8110080 | bytes 1081344 | tf_op jit(solution)/shard_map/pallas_call | solution.py:107
  18.1 0.7 broadcast_in_dim.117.table_ref
  18.8 4.6 %shard_map.65.kid_ref = f32[2,2,8,4224]{3,2,1,0:T(8,128)} custom-call(f32[2,8]{1,0:T(2,128)} %get-tuple-element.53.weight_ref, f32[2,2,8,4224]{3,2,1,0:T(8,128)} %shard_map.64.kid_ref, f32[5,2,2,8,128]{4,3,2,1,0:T(8,128)} %broadcast_in_dim.117.table_ref), custom_call_target="tpu_custom_call" | custom-call | flops 8110080 | bytes 1081344 | tf_op jit(solution)/shard_map/pallas_call | solution.py:107
  23.4 0.7 broadcast_in_dim.118.table_ref
  24.1 4.6 %shard_map.66.kid_ref = f32[2,2,8,4224]{3,2,1,0:T(8,128)} custom-call(f32[2,8]{1,0:T(2,128)} %get-tuple-element.54.weight_ref, f32[2,2,8,4224]{3,2,1,0:T(8,128)} %shard_map.65.kid_ref, f32[5,2,2,8,128]{4,3,2,1,0:T(8,128)} %broadcast_in_dim.118.table_ref), custom_call_target="tpu_custom_call" | custom-call | flops 8110080 | bytes 1081344 | tf_op jit(solution)/shard_map/pallas_call | solution.py:107
  28.7 0.7 broadcast_in_dim.120.table_ref
  29.4 4.7 %shard_map.67 = f32[2,16,4224]{2,1,0:T(8,128)} custom-call(f32[2,8]{1,0:T(2,128)} %get-tuple-element.55.weight_ref, f32[2,2,8,4224]{3,2,1,0:T(8,128)} %shard_map.66.kid_ref, f32[5,2,2,8,128]{4,3,2,1,0:T(8,128)} %broadcast_in_dim.120.table_ref), custom_call_target="tpu_custom_call" | custom-call | flops 8110080 | bytes 1081344 | tf_op jit(solution)/shard_map/pallas_call | solution.py:107
  34.2 1.1 slice.209
  35.8 1.0 maximum_bitcast_fusion.2
  36.7 7.4 %all-to-all-start = ((f32[16,2,16,316]{3,2,1,0:T(8,128)}), f32[16,2,16,316]{3,2,1,0:T(8,128)S(1)}, u32[]{:S(2)}, u32[]{:S(2)}) async-start(f32[16,2,16,316]{3,2,1,0:T(8,128)} %maximum_bitcast_fusion.2), calls=%async_computation | async-start | bytes 1572864 | tf_op jit(solution)/shard_map/all_to_all | solution.py:201
  45.2 1.5 %broadcast_in_dim.121.table_ref = f32[5,2,2,128,128]{4,3,2,1,0:T(8,128)} broadcast(f32[5,2,2,128]{3,2,1,0:T(2,128)S(1)} %tile.78), dimensions={0,1,2,3} | broadcast | bytes 1320960 | tf_op jit(solution)/shard_map/broadcast_in_dim | solution.py:142
  46.7 1.5 %broadcast_in_dim.122.table_ref = f32[5,2,2,128,128]{4,3,2,1,0:T(8,128)} broadcast(f32[5,2,2,128]{3,2,1,0:T(2,128)S(1)} %tile.81), dimensions={0,1,2,3} | broadcast | bytes 1320960 | tf_op jit(solution)/shard_map/broadcast_in_dim | solution.py:142
  48.2 1.5 %broadcast_in_dim.123.table_ref = f32[5,2,2,128,128]{4,3,2,1,0:T(8,128)} broadcast(f32[5,2,2,128]{3,2,1,0:T(2,128)S(1)} %tile.84), dimensions={0,1,2,3} | broadcast | bytes 1320960 | tf_op jit(solution)/shard_map/broadcast_in_dim | solution.py:142
  49.7 1.5 %broadcast_in_dim.125.table_ref = f32[5,2,2,128,128]{4,3,2,1,0:T(8,128)} broadcast(f32[5,2,2,128]{3,2,1,0:T(2,128)S(1)} %broadcast_in_dim.124), dimensions={0,1,2,3} | broadcast | bytes 1320960 | tf_op jit(solution)/shard_map/broadcast_in_dim | solution.py:142
  51.1 11.7 %all-to-all-done = f32[16,2,16,316]{3,2,1,0:T(8,128)S(1)} async-done(((f32[16,2,16,316]{3,2,1,0:T(8,128)}), f32[16,2,16,316]{3,2,1,0:T(8,128)S(1)}, u32[]{:S(2)}, u32[]{:S(2)}) %all-to-all-start) | async-done | bytes 647200 | tf_op jit(solution)/shard_map/all_to_all | solution.py:201
  63.0 1.0 pad_maximum_fusion.1.kid_ref
  64.0 6.4 %shard_map.68.kid_ref = f32[2,2,128,384]{3,2,1,0:T(8,128)} custom-call(f32[2,8]{1,0:T(2,128)} %get-tuple-element.56.weight_ref, f32[2,2,128,384]{3,2,1,0:T(8,128)} %pad_maximum_fusion.1.kid_ref, f32[5,2,2,128,128]{4,3,2,1,0:T(8,128)} %broadcast_in_dim.121.table_ref), custom_call_target="tpu_custom_call" | custom-call | flops 11796480 | bytes 1572864 | tf_op jit(solution)/shard_map/pallas_call | solution.py:107
  70.4 6.4 %shard_map.69.kid_ref = f32[2,2,128,384]{3,2,1,0:T(8,128)} custom-call(f32[2,8]{1,0:T(2,128)} %get-tuple-element.57.weight_ref, f32[2,2,128,384]{3,2,1,0:T(8,128)} %shard_map.68.kid_ref, f32[5,2,2,128,128]{4,3,2,1,0:T(8,128)} %broadcast_in_dim.122.table_ref), custom_call_target="tpu_custom_call" | custom-call | flops 11796480 | bytes 1572864 | tf_op jit(solution)/shard_map/pallas_call | solution.py:107
  76.9 6.4 %shard_map.70.kid_ref = f32[2,2,128,384]{3,2,1,0:T(8,128)} custom-call(f32[2,8]{1,0:T(2,128)} %get-tuple-element.58.weight_ref, f32[2,2,128,384]{3,2,1,0:T(8,128)} %shard_map.69.kid_ref, f32[5,2,2,128,128]{4,3,2,1,0:T(8,128)} %broadcast_in_dim.123.table_ref), custom_call_target="tpu_custom_call" | custom-call | flops 11796480 | bytes 1572864 | tf_op jit(solution)/shard_map/pallas_call | solution.py:107
  83.3 6.6 %shard_map.71 = f32[2,256,384]{2,1,0:T(8,128)} custom-call(f32[2,8]{1,0:T(2,128)} %get-tuple-element.59.weight_ref, f32[2,2,128,384]{3,2,1,0:T(8,128)} %shard_map.70.kid_ref, f32[5,2,2,128,128]{4,3,2,1,0:T(8,128)} %broadcast_in_dim.125.table_ref), custom_call_target="tpu_custom_call" | custom-call | flops 11796480 | bytes 1572864 | tf_op jit(solution)/shard_map/pallas_call | solution.py:107
  89.9 1.0 slice-done
  91.0 4.0 %collective-permute-start.1 = (f32[2,16,256]{2,1,0:T(8,128)S(1)}, f32[2,16,256]{2,1,0:T(8,128)S(1)}, u32[]{:S(2)}, u32[]{:S(2)}) collective-permute-start(f32[2,16,256]{2,1,0:T(8,128)S(1)} %get-tuple-element.47), channel_id=1, source_target_pairs={{0,30},{2,0},{4,2},{6,4},{8,6},{10,8},{12,10},{14,12},{16,14},{18,... | collective-permute-start | bytes 98312 | tf_op jit(solution)/shard_map/ppermute | solution.py:215
  95.2 1.8 %collective-permute-start.4 = (f32[2,16,256]{2,1,0:T(8,128)S(1)}, f32[2,16,256]{2,1,0:T(8,128)S(1)}, u32[]{:S(2)}, u32[]{:S(2)}) collective-permute-start(f32[2,16,256]{2,1,0:T(8,128)S(1)} %get-tuple-element.44), channel_id=1, source_target_pairs={{0,24},{2,26},{4,28},{6,30},{8,0},{10,2},{12,4},{14,6},{16,8},{18,... | collective-permute-start | bytes 98312 | tf_op jit(solution)/shard_map/ppermute | solution.py:215
  97.0 0.7 collective-permute-start.5
  97.7 2.9 %collective-permute-start.6 = (f32[2,16,256]{2,1,0:T(8,128)S(1)}, f32[2,16,256]{2,1,0:T(8,128)S(1)}, u32[]{:S(2)}, u32[]{:S(2)}) collective-permute-start(f32[2,16,256]{2,1,0:T(8,128)S(1)} %get-tuple-element.42), channel_id=1, source_target_pairs={{0,20},{2,22},{4,24},{6,26},{8,28},{10,30},{12,0},{14,2},{16,4},{1... | collective-permute-start | bytes 98312 | tf_op jit(solution)/shard_map/ppermute | solution.py:215
  100.9 1.5 %collective-permute-start.8 = (f32[2,16,256]{2,1,0:T(8,128)S(1)}, f32[2,16,256]{2,1,0:T(8,128)S(1)}, u32[]{:S(2)}, u32[]{:S(2)}) collective-permute-start(f32[2,16,256]{2,1,0:T(8,128)S(1)} %get-tuple-element.40), channel_id=1, source_target_pairs={{0,16},{2,18},{4,20},{6,22},{8,24},{10,26},{12,28},{14,30},{16,0},... | collective-permute-start | bytes 98312 | tf_op jit(solution)/shard_map/ppermute | solution.py:215
  102.3 2.1 %collective-permute-start.9 = (f32[2,16,256]{2,1,0:T(8,128)S(1)}, f32[2,16,256]{2,1,0:T(8,128)S(1)}, u32[]{:S(2)}, u32[]{:S(2)}) collective-permute-start(f32[2,16,256]{2,1,0:T(8,128)S(1)} %get-tuple-element.39), channel_id=1, source_target_pairs={{0,14},{2,16},{4,18},{6,20},{8,22},{10,24},{12,26},{14,28},{16,30}... | collective-permute-start | bytes 98312 | tf_op jit(solution)/shard_map/ppermute | solution.py:215
  104.4 2.5 %collective-permute-start.10 = (f32[2,16,256]{2,1,0:T(8,128)S(1)}, f32[2,16,256]{2,1,0:T(8,128)S(1)}, u32[]{:S(2)}, u32[]{:S(2)}) collective-permute-start(f32[2,16,256]{2,1,0:T(8,128)S(1)} %get-tuple-element.38), channel_id=1, source_target_pairs={{0,12},{2,14},{4,16},{6,18},{8,20},{10,22},{12,24},{14,26},{16,28}... | collective-permute-start | bytes 98312 | tf_op jit(solution)/shard_map/ppermute | solution.py:215
  106.9 1.3 %collective-permute-start.12 = (f32[2,16,256]{2,1,0:T(8,128)S(1)}, f32[2,16,256]{2,1,0:T(8,128)S(1)}, u32[]{:S(2)}, u32[]{:S(2)}) collective-permute-start(f32[2,16,256]{2,1,0:T(8,128)S(1)} %get-tuple-element.36), channel_id=1, source_target_pairs={{0,8},{2,10},{4,12},{6,14},{8,16},{10,18},{12,20},{14,22},{16,24},... | collective-permute-start | bytes 98312 | tf_op jit(solution)/shard_map/ppermute | solution.py:215
  108.2 2.1 %collective-permute-start.13 = (f32[2,16,256]{2,1,0:T(8,128)S(1)}, f32[2,16,256]{2,1,0:T(8,128)S(1)}, u32[]{:S(2)}, u32[]{:S(2)}) collective-permute-start(f32[2,16,256]{2,1,0:T(8,128)S(1)} %get-tuple-element.35), channel_id=1, source_target_pairs={{0,6},{2,8},{4,10},{6,12},{8,14},{10,16},{12,18},{14,20},{16,22},{... | collective-permute-start | bytes 98312 | tf_op jit(solution)/shard_map/ppermute | solution.py:215
  110.4 2.0 %collective-permute-start.14 = (f32[2,16,256]{2,1,0:T(8,128)S(1)}, f32[2,16,256]{2,1,0:T(8,128)S(1)}, u32[]{:S(2)}, u32[]{:S(2)}) collective-permute-start(f32[2,16,256]{2,1,0:T(8,128)S(1)} %get-tuple-element.34), channel_id=1, source_target_pairs={{0,4},{2,6},{4,8},{6,10},{8,12},{10,14},{12,16},{14,18},{16,20},{1... | collective-permute-start | bytes 98312 | tf_op jit(solution)/shard_map/ppermute | solution.py:215
  112.8 1.1 collective-permute-done.11
  113.9 0.8 collective-permute-done.13
  114.7 2.3 %collective-permute-done.14 = f32[2,16,256]{2,1,0:T(8,128)S(1)} collective-permute-done((f32[2,16,256]{2,1,0:T(8,128)S(1)}, f32[2,16,256]{2,1,0:T(8,128)S(1)}, u32[]{:S(2)}, u32[]{:S(2)}) %collective-permute-start.14) | collective-permute-done | bytes 32800 | tf_op jit(solution)/shard_map/ppermute | solution.py:215
  117.0 1.4 %collective-permute-done.15 = f32[2,16,256]{2,1,0:T(8,128)S(1)} collective-permute-done((f32[2,16,256]{2,1,0:T(8,128)S(1)}, f32[2,16,256]{2,1,0:T(8,128)S(1)}, u32[]{:S(2)}, u32[]{:S(2)}) %collective-permute-start.15) | collective-permute-done | bytes 32800 | tf_op jit(solution)/shard_map/ppermute | solution.py:215
  118.5 1.8 %concatenate.41 = f32[2,16,32,256]{3,2,1,0:T(8,128)S(1)} concatenate(f32[2,16,1,256]{3,2,1,0:T(1,128)S(1)} %stack.61, f32[2,16,1,256]{3,2,1,0:T(1,128)S(1)} %stack.62, f32[2,16,1,256]{3,2,1,0:T(1,128)S(1)} %stack.63, f32[2,16,1,256]{3,2,1,0:T(1,128)S(1)} %stack.64, f32[2,16,1,256]{3,2,1,0:T(1,128)S(1)} %stack.65, f32[2,16,1,256]{3,2,1,0:T(1,128)S(1)} %stack.66, ...), dimensions={2} | concatenate | bytes 2097152 | tf_op jit(solution)/shard_map/jit(_roll_dynamic)/concatenate | solution.py:217
  120.4 0.9 reshape.80
  (118 shorter events, 6.6 us)
Async XLA Ops:
  0.8 8.9 %collective-permute-start = (bf16[2,16,768]{2,1,0:T(8,128)(2,1)S(1)}, bf16[2,16,768]{2,1,0:T(8,128)(2,1)S(1)}, u32[]{:S(2)}, u32[]{:S(2)}) collective-permute-start(bf16[2,16,768]{2,1,0:T(8,128)(2,1)S(1)} %slice.156), channel_id=1, source_target_pairs={{1,0},{3,2},{5,4},{7,6},{9,8},{11,10},{13,12},{15,14},{17,16},{19,... | collective-permute-start | bytes 147464 | tf_op jit(solution)/shard_map/ppermute | solution.py:23
  6.0 0.7 copy-start.4
  6.0 0.8 copy-start.5
  6.9 2.1 %copy-start.2 = (f32[5,2,510]{2,1,0:T(2,128)}, f32[5,2,510]{2,1,0:T(2,128)S(1)}, u32[]{:S(2)}) copy-start(f32[5,2,510]{2,1,0:T(2,128)S(1)} %select_select_fusion) | copy-start | bytes 61204
  8.6 1.1 copy-start.1
  11.7 0.9 slice-start.1
  34.2 1.2 copy-start
  35.8 8.4 %copy-start.3 = (f32[5,2,510]{2,1,0:T(2,128)S(1)}, f32[5,2,510]{2,1,0:T(2,128)}, u32[]{:S(2)}) copy-start(f32[5,2,510]{2,1,0:T(2,128)} %copy-done.2) | copy-start | bytes 61204
  36.7 26.1 %all-to-all-start = ((f32[16,2,16,316]{3,2,1,0:T(8,128)}), f32[16,2,16,316]{3,2,1,0:T(8,128)S(1)}, u32[]{:S(2)}, u32[]{:S(2)}) async-start(f32[16,2,16,316]{3,2,1,0:T(8,128)} %maximum_bitcast_fusion.2), calls=%async_computation | async-start | bytes 1572864 | tf_op jit(solution)/shard_map/all_to_all | solution.py:201
  89.9 1.0 slice-start
  91.0 6.7 %collective-permute-start.1 = (f32[2,16,256]{2,1,0:T(8,128)S(1)}, f32[2,16,256]{2,1,0:T(8,128)S(1)}, u32[]{:S(2)}, u32[]{:S(2)}) collective-permute-start(f32[2,16,256]{2,1,0:T(8,128)S(1)} %get-tuple-element.47), channel_id=1, source_target_pairs={{0,30},{2,0},{4,2},{6,4},{8,6},{10,8},{12,10},{14,12},{16,14},{18,... | collective-permute-start | bytes 98312 | tf_op jit(solution)/shard_map/ppermute | solution.py:215
  95.0 5.6 %collective-permute-start.2 = (f32[2,16,256]{2,1,0:T(8,128)S(1)}, f32[2,16,256]{2,1,0:T(8,128)S(1)}, u32[]{:S(2)}, u32[]{:S(2)}) collective-permute-start(f32[2,16,256]{2,1,0:T(8,128)S(1)} %get-tuple-element.46), channel_id=1, source_target_pairs={{0,28},{2,30},{4,0},{6,2},{8,4},{10,6},{12,8},{14,10},{16,12},{18,... | collective-permute-start | bytes 98312 | tf_op jit(solution)/shard_map/ppermute | solution.py:215
  95.2 5.7 %collective-permute-start.3 = (f32[2,16,256]{2,1,0:T(8,128)S(1)}, f32[2,16,256]{2,1,0:T(8,128)S(1)}, u32[]{:S(2)}, u32[]{:S(2)}) collective-permute-start(f32[2,16,256]{2,1,0:T(8,128)S(1)} %get-tuple-element.45), channel_id=1, source_target_pairs={{0,26},{2,28},{4,30},{6,0},{8,2},{10,4},{12,6},{14,8},{16,10},{18,... | collective-permute-start | bytes 98312 | tf_op jit(solution)/shard_map/ppermute | solution.py:215
  95.2 7.2 %collective-permute-start.4 = (f32[2,16,256]{2,1,0:T(8,128)S(1)}, f32[2,16,256]{2,1,0:T(8,128)S(1)}, u32[]{:S(2)}, u32[]{:S(2)}) collective-permute-start(f32[2,16,256]{2,1,0:T(8,128)S(1)} %get-tuple-element.44), channel_id=1, source_target_pairs={{0,24},{2,26},{4,28},{6,30},{8,0},{10,2},{12,4},{14,6},{16,8},{18,... | collective-permute-start | bytes 98312 | tf_op jit(solution)/shard_map/ppermute | solution.py:215
  97.0 7.5 %collective-permute-start.5 = (f32[2,16,256]{2,1,0:T(8,128)S(1)}, f32[2,16,256]{2,1,0:T(8,128)S(1)}, u32[]{:S(2)}, u32[]{:S(2)}) collective-permute-start(f32[2,16,256]{2,1,0:T(8,128)S(1)} %get-tuple-element.43), channel_id=1, source_target_pairs={{0,22},{2,24},{4,26},{6,28},{8,30},{10,0},{12,2},{14,4},{16,6},{18... | collective-permute-start | bytes 98312 | tf_op jit(solution)/shard_map/ppermute | solution.py:215
  97.7 9.3 %collective-permute-start.6 = (f32[2,16,256]{2,1,0:T(8,128)S(1)}, f32[2,16,256]{2,1,0:T(8,128)S(1)}, u32[]{:S(2)}, u32[]{:S(2)}) collective-permute-start(f32[2,16,256]{2,1,0:T(8,128)S(1)} %get-tuple-element.42), channel_id=1, source_target_pairs={{0,20},{2,22},{4,24},{6,26},{8,28},{10,30},{12,0},{14,2},{16,4},{1... | collective-permute-start | bytes 98312 | tf_op jit(solution)/shard_map/ppermute | solution.py:215
  100.6 6.3 %collective-permute-start.7 = (f32[2,16,256]{2,1,0:T(8,128)S(1)}, f32[2,16,256]{2,1,0:T(8,128)S(1)}, u32[]{:S(2)}, u32[]{:S(2)}) collective-permute-start(f32[2,16,256]{2,1,0:T(8,128)S(1)} %get-tuple-element.41), channel_id=1, source_target_pairs={{0,18},{2,20},{4,22},{6,24},{8,26},{10,28},{12,30},{14,0},{16,2},{... | collective-permute-start | bytes 98312 | tf_op jit(solution)/shard_map/ppermute | solution.py:215
  100.9 7.3 %collective-permute-start.8 = (f32[2,16,256]{2,1,0:T(8,128)S(1)}, f32[2,16,256]{2,1,0:T(8,128)S(1)}, u32[]{:S(2)}, u32[]{:S(2)}) collective-permute-start(f32[2,16,256]{2,1,0:T(8,128)S(1)} %get-tuple-element.40), channel_id=1, source_target_pairs={{0,16},{2,18},{4,20},{6,22},{8,24},{10,26},{12,28},{14,30},{16,0},... | collective-permute-start | bytes 98312 | tf_op jit(solution)/shard_map/ppermute | solution.py:215
  102.3 8.0 %collective-permute-start.9 = (f32[2,16,256]{2,1,0:T(8,128)S(1)}, f32[2,16,256]{2,1,0:T(8,128)S(1)}, u32[]{:S(2)}, u32[]{:S(2)}) collective-permute-start(f32[2,16,256]{2,1,0:T(8,128)S(1)} %get-tuple-element.39), channel_id=1, source_target_pairs={{0,14},{2,16},{4,18},{6,20},{8,22},{10,24},{12,26},{14,28},{16,30}... | collective-permute-start | bytes 98312 | tf_op jit(solution)/shard_map/ppermute | solution.py:215
  104.4 8.0 %collective-permute-start.10 = (f32[2,16,256]{2,1,0:T(8,128)S(1)}, f32[2,16,256]{2,1,0:T(8,128)S(1)}, u32[]{:S(2)}, u32[]{:S(2)}) collective-permute-start(f32[2,16,256]{2,1,0:T(8,128)S(1)} %get-tuple-element.38), channel_id=1, source_target_pairs={{0,12},{2,14},{4,16},{6,18},{8,20},{10,22},{12,24},{14,26},{16,28}... | collective-permute-start | bytes 98312 | tf_op jit(solution)/shard_map/ppermute | solution.py:215
  106.9 6.9 %collective-permute-start.11 = (f32[2,16,256]{2,1,0:T(8,128)S(1)}, f32[2,16,256]{2,1,0:T(8,128)S(1)}, u32[]{:S(2)}, u32[]{:S(2)}) collective-permute-start(f32[2,16,256]{2,1,0:T(8,128)S(1)} %get-tuple-element.37), channel_id=1, source_target_pairs={{0,10},{2,12},{4,14},{6,16},{8,18},{10,20},{12,22},{14,24},{16,26}... | collective-permute-start | bytes 98312 | tf_op jit(solution)/shard_map/ppermute | solution.py:215
  106.9 6.9 %collective-permute-start.12 = (f32[2,16,256]{2,1,0:T(8,128)S(1)}, f32[2,16,256]{2,1,0:T(8,128)S(1)}, u32[]{:S(2)}, u32[]{:S(2)}) collective-permute-start(f32[2,16,256]{2,1,0:T(8,128)S(1)} %get-tuple-element.36), channel_id=1, source_target_pairs={{0,8},{2,10},{4,12},{6,14},{8,16},{10,18},{12,20},{14,22},{16,24},... | collective-permute-start | bytes 98312 | tf_op jit(solution)/shard_map/ppermute | solution.py:215
  108.2 6.4 %collective-permute-start.13 = (f32[2,16,256]{2,1,0:T(8,128)S(1)}, f32[2,16,256]{2,1,0:T(8,128)S(1)}, u32[]{:S(2)}, u32[]{:S(2)}) collective-permute-start(f32[2,16,256]{2,1,0:T(8,128)S(1)} %get-tuple-element.35), channel_id=1, source_target_pairs={{0,6},{2,8},{4,10},{6,12},{8,14},{10,16},{12,18},{14,20},{16,22},{... | collective-permute-start | bytes 98312 | tf_op jit(solution)/shard_map/ppermute | solution.py:215
  110.4 6.6 %collective-permute-start.14 = (f32[2,16,256]{2,1,0:T(8,128)S(1)}, f32[2,16,256]{2,1,0:T(8,128)S(1)}, u32[]{:S(2)}, u32[]{:S(2)}) collective-permute-start(f32[2,16,256]{2,1,0:T(8,128)S(1)} %get-tuple-element.34), channel_id=1, source_target_pairs={{0,4},{2,6},{4,8},{6,10},{8,12},{10,14},{12,16},{14,18},{16,20},{1... | collective-permute-start | bytes 98312 | tf_op jit(solution)/shard_map/ppermute | solution.py:215
  112.4 6.0 %collective-permute-start.15 = (f32[2,16,256]{2,1,0:T(8,128)S(1)}, f32[2,16,256]{2,1,0:T(8,128)S(1)}, u32[]{:S(2)}, u32[]{:S(2)}) collective-permute-start(f32[2,16,256]{2,1,0:T(8,128)S(1)} %get-tuple-element.33), channel_id=1, source_target_pairs={{0,2},{2,4},{4,6},{6,8},{8,10},{10,12},{12,14},{14,16},{16,18},{18... | collective-permute-start | bytes 98312 | tf_op jit(solution)/shard_map/ppermute | solution.py:215

commit v10 on v8

--- a/solution.py
+++ b/solution.py
@@ -188,11 +188,11 @@
         level = run_section(level, section, 1 << section, section < local_sections - 1)
     piece_bins = bins // pulse_count
     need = cross_sections * MARGIN
-    flat = level[:, :, : bins + need]
-    flat = jnp.pad(flat, ((0, 0), (0, 0), (0, piece_bins - need)))
+    carry = -(-(piece_bins + need) // LANE) * LANE - piece_bins
+    flat = padded_lanes(level, bins + piece_bins)
     head = flat[:, :, :bins].reshape(parts, local_beams, pulse_count, piece_bins)
     tail = flat[:, :, piece_bins:].reshape(parts, local_beams, pulse_count, piece_bins)[
-        :, :, :, :need
+        :, :, :, :carry
     ]
     pieces = jnp.transpose(jnp.concatenate([head, tail], axis=3), (2, 0, 1, 3))
     cross_rows = pulse_count * local_beams // 2
@@ -201,7 +201,7 @@
     level = lax.all_to_all(pieces, "pulse", split_axis=0, concat_axis=0, tiled=True)
     level, tables = lax.optimization_barrier((level, tables))
     level = jnp.transpose(level, (1, 0, 2, 3))
-    level = padded_lanes(level.reshape(parts, pulse_count * local_beams, piece_bins + need), piece_bins + need)
+    level = level.reshape(parts, pulse_count * local_beams, piece_bins + carry)
     level = split_kids(level, local_beams)
     for bit in range(cross_sections):
         section = local_sections + bit

time: 113 us -> 113 us (level)
  no operation moved by 1% of the time
where the time goes in v10:
time: 113 us; the launch traced here: 112 us
  Pallas kernels  44.3 us (39%)
  local copies, waits for them, and re-layouts  23.3 us (21%)
  blocking collectives  19.7 us (17%)
  waiting for transfers between devices  11.9 us (11%)
  starting transfers between devices  8.66 us (8%)
  other arithmetic  3.16 us (3%)
    pallas_call x8, Pallas kernels, merge_call(): pl.pallas_call(functools.partial(merge_kernel, beams, chained), out_shape...  44.3 us
    all_to_all x1, blocking collectives, on_device(): lax.all_to_all(level, 'pulse', split_axis=0, concat_axis=0, tiled=True)  19.7 us
    all_to_all x1, waiting for transfers between devices, on_device(): lax.all_to_all(pieces, 'pulse', split_axis=0, concat_axis=0, tiled=True)  11.9 us
    broadcast_in_dim x10, local copies, waits for them, and re-layouts, row_table(): jnp.broadcast_to(per_row(packed, rows // beams)[..., None], (5, 2, 2, row...  8.9 us
    all_to_all x1, starting transfers between devices, on_device(): lax.all_to_all(pieces, 'pulse', split_axis=0, concat_axis=0, tiled=True)  7.38 us
  transfers between devices with their start and end apart: 2, of which 1 were waited for; matrix products, arithmetic and copies ran while one was open for 13% of the time, Pallas kernels for 0%

profile of v10, /device:TPU:0, one launch (start us, length us, event | category | flops | bytes accessed | tf_op | source)
XLA Modules:
  0.0 112.3 jit_solution(10970417446671088351)
XLA Ops:
  0.0 0.8 slice.152
  0.8 1.3 %collective-permute-start = (bf16[2,16,768]{2,1,0:T(8,128)(2,1)S(1)}, bf16[2,16,768]{2,1,0:T(8,128)(2,1)S(1)}, u32[]{:S(2)}, u32[]{:S(2)}) collective-permute-start(bf16[2,16,768]{2,1,0:T(8,128)(2,1)S(1)} %slice.152), channel_id=1, source_target_pairs={{1,0},{3,2},{5,4},{7,6},{9,8},{11,10},{13,12},{15,14},{17,16},{19,... | collective-permute-start | bytes 147464 | tf_op jit(solution)/shard_map/ppermute | solution.py:23
  2.1 0.8 slice_reduce_fusion
  2.9 0.8 fusion.20
  4.1 0.8 fusion.21
  5.2 0.8 fusion.19
  6.0 0.7 tile.69
  6.8 0.4 reshape.66
  7.1 0.2 copy.64
  7.4 0.1 copy-done.3
  7.6 0.1 fusion.12
  7.7 0.6 slice_bitcast_fusion.2
  8.7 0.1 copy.68
  8.9 0.1 copy.69
  9.1 0.7 tile.67
  9.8 0.4 reshape.65
  10.2 0.2 copy.63
  10.4 0.4 copy-done
  10.8 0.2 reshape.64
  11.0 0.2 fusion.18
  11.4 0.8 fusion
  12.4 0.3 copy.65
  12.8 0.8 pad_maximum_fusion.3.kid_ref
  13.6 0.7 broadcast_in_dim.116.table_ref
  14.3 4.7 %shard_map.64.kid_ref = f32[2,2,8,4224]{3,2,1,0:T(8,128)} custom-call(f32[2,8]{1,0:T(2,128)} %get-tuple-element.38.weight_ref, f32[2,2,8,4224]{3,2,1,0:T(8,128)} %pad_maximum_fusion.3.kid_ref, f32[5,2,2,8,128]{4,3,2,1,0:T(8,128)} %broadcast_in_dim.116.table_ref), custom_call_target="tpu_custom_call" | custom-call | flops 8110080 | bytes 1081344 | tf_op jit(solution)/shard_map/pallas_call | solution.py:107
  19.1 0.7 broadcast_in_dim.117.table_ref
  19.8 4.6 %shard_map.65.kid_ref = f32[2,2,8,4224]{3,2,1,0:T(8,128)} custom-call(f32[2,8]{1,0:T(2,128)} %get-tuple-element.39.weight_ref, f32[2,2,8,4224]{3,2,1,0:T(8,128)} %shard_map.64.kid_ref, f32[5,2,2,8,128]{4,3,2,1,0:T(8,128)} %broadcast_in_dim.117.table_ref), custom_call_target="tpu_custom_call" | custom-call | flops 8110080 | bytes 1081344 | tf_op jit(solution)/shard_map/pallas_call | solution.py:107
  24.4 0.7 broadcast_in_dim.118.table_ref
  25.1 4.6 %shard_map.66.kid_ref = f32[2,2,8,4224]{3,2,1,0:T(8,128)} custom-call(f32[2,8]{1,0:T(2,128)} %get-tuple-element.40.weight_ref, f32[2,2,8,4224]{3,2,1,0:T(8,128)} %shard_map.65.kid_ref, f32[5,2,2,8,128]{4,3,2,1,0:T(8,128)} %broadcast_in_dim.118.table_ref), custom_call_target="tpu_custom_call" | custom-call | flops 8110080 | bytes 1081344 | tf_op jit(solution)/shard_map/pallas_call | solution.py:107
  29.7 0.7 broadcast_in_dim.120.table_ref
  30.4 4.7 %shard_map.67 = f32[2,16,4224]{2,1,0:T(8,128)} custom-call(f32[2,8]{1,0:T(2,128)} %get-tuple-element.41.weight_ref, f32[2,2,8,4224]{3,2,1,0:T(8,128)} %shard_map.66.kid_ref, f32[5,2,2,8,128]{4,3,2,1,0:T(8,128)} %broadcast_in_dim.120.table_ref), custom_call_target="tpu_custom_call" | custom-call | flops 8110080 | bytes 1081344 | tf_op jit(solution)/shard_map/pallas_call | solution.py:107
  35.2 1.3 %fusion.16 = (f32[2,16,4096]{2,1,0:T(8,128)S(1)}, f32[2,16,4096]{2,1,0:T(8,128)S(1)}) fusion(f32[2,16,4224]{2,1,0:T(8,128)} %shard_map.67), kind=kLoop, calls=%fused_computation.49 | loop fusion | bytes 2113536 | tf_op jit(solution)/shard_map/slice | solution.py:193
  36.5 0.2 copy.80
  36.8 1.0 maximum_bitcast_fusion.2
  37.8 7.4 %all-to-all-start = ((f32[16,2,16,384]{3,2,1,0:T(8,128)}), f32[16,2,16,384]{3,2,1,0:T(8,128)S(1)}, u32[]{:S(2)}, u32[]{:S(2)}) async-start(f32[16,2,16,384]{3,2,1,0:T(8,128)} %maximum_bitcast_fusion.2), calls=%async_computation | async-start | bytes 1572864 | tf_op jit(solution)/shard_map/all_to_all | solution.py:201
  46.1 1.5 %broadcast_in_dim.121.table_ref = f32[5,2,2,128,128]{4,3,2,1,0:T(8,128)} broadcast(f32[5,2,2,128]{3,2,1,0:T(2,128)S(1)} %tile.78), dimensions={0,1,2,3} | broadcast | bytes 1320960 | tf_op jit(solution)/shard_map/broadcast_in_dim | solution.py:142
  47.6 1.5 %broadcast_in_dim.122.table_ref = f32[5,2,2,128,128]{4,3,2,1,0:T(8,128)} broadcast(f32[5,2,2,128]{3,2,1,0:T(2,128)S(1)} %tile.81), dimensions={0,1,2,3} | broadcast | bytes 1320960 | tf_op jit(solution)/shard_map/broadcast_in_dim | solution.py:142
  49.0 1.5 %broadcast_in_dim.123.table_ref = f32[5,2,2,128,128]{4,3,2,1,0:T(8,128)} broadcast(f32[5,2,2,128]{3,2,1,0:T(2,128)S(1)} %tile.84), dimensions={0,1,2,3} | broadcast | bytes 1320960 | tf_op jit(solution)/shard_map/broadcast_in_dim | solution.py:142
  50.5 1.5 %broadcast_in_dim.125.table_ref = f32[5,2,2,128,128]{4,3,2,1,0:T(8,128)} broadcast(f32[5,2,2,128]{3,2,1,0:T(2,128)S(1)} %broadcast_in_dim.124), dimensions={0,1,2,3} | broadcast | bytes 1320960 | tf_op jit(solution)/shard_map/broadcast_in_dim | solution.py:142
  52.0 11.9 %all-to-all-done = f32[16,2,16,384]{3,2,1,0:T(8,128)S(1)} async-done(((f32[16,2,16,384]{3,2,1,0:T(8,128)}), f32[16,2,16,384]{3,2,1,0:T(8,128)S(1)}, u32[]{:S(2)}, u32[]{:S(2)}) %all-to-all-start) | async-done | bytes 786464 | tf_op jit(solution)/shard_map/all_to_all | solution.py:201
  64.0 0.9 pad_maximum_fusion.1.kid_ref
  64.9 6.4 %shard_map.68.kid_ref = f32[2,2,128,384]{3,2,1,0:T(8,128)} custom-call(f32[2,8]{1,0:T(2,128)} %get-tuple-element.42.weight_ref, f32[2,2,128,384]{3,2,1,0:T(8,128)} %pad_maximum_fusion.1.kid_ref, f32[5,2,2,128,128]{4,3,2,1,0:T(8,128)} %broadcast_in_dim.121.table_ref), custom_call_target="tpu_custom_call" | custom-call | flops 11796480 | bytes 1572864 | tf_op jit(solution)/shard_map/pallas_call | solution.py:107
  71.4 6.4 %shard_map.69.kid_ref = f32[2,2,128,384]{3,2,1,0:T(8,128)} custom-call(f32[2,8]{1,0:T(2,128)} %get-tuple-element.43.weight_ref, f32[2,2,128,384]{3,2,1,0:T(8,128)} %shard_map.68.kid_ref, f32[5,2,2,128,128]{4,3,2,1,0:T(8,128)} %broadcast_in_dim.122.table_ref), custom_call_target="tpu_custom_call" | custom-call | flops 11796480 | bytes 1572864 | tf_op jit(solution)/shard_map/pallas_call | solution.py:107
  77.8 6.4 %shard_map.70.kid_ref = f32[2,2,128,384]{3,2,1,0:T(8,128)} custom-call(f32[2,8]{1,0:T(2,128)} %get-tuple-element.44.weight_ref, f32[2,2,128,384]{3,2,1,0:T(8,128)} %shard_map.69.kid_ref, f32[5,2,2,128,128]{4,3,2,1,0:T(8,128)} %broadcast_in_dim.123.table_ref), custom_call_target="tpu_custom_call" | custom-call | flops 11796480 | bytes 1572864 | tf_op jit(solution)/shard_map/pallas_call | solution.py:107
  84.2 6.4 %shard_map.71 = f32[2,256,384]{2,1,0:T(8,128)} custom-call(f32[2,8]{1,0:T(2,128)} %get-tuple-element.45.weight_ref, f32[2,2,128,384]{3,2,1,0:T(8,128)} %shard_map.70.kid_ref, f32[5,2,2,128,128]{4,3,2,1,0:T(8,128)} %broadcast_in_dim.125.table_ref), custom_call_target="tpu_custom_call" | custom-call | flops 11796480 | bytes 1572864 | tf_op jit(solution)/shard_map/pallas_call | solution.py:107
  90.6 1.0 slice-done
  91.7 19.7 %all_to_all.10 = f32[16,2,16,256]{3,2,1,0:T(8,128)S(1)} all-to-all(f32[16,2,16,256]{3,2,1,0:T(8,128)S(1)} %bitcast.69), channel_id=1, replica_groups=mesh['pulse'=16,'range'=2] {'pulse'}, dimensions={0} | all-to-all | bytes 1048576 | tf_op jit(solution)/shard_map/all_to_all | solution.py:211
  111.4 0.8 copy.79
  (65 shorter events, 3.1 us)
Async XLA Ops:
  0.8 9.6 %collective-permute-start = (bf16[2,16,768]{2,1,0:T(8,128)(2,1)S(1)}, bf16[2,16,768]{2,1,0:T(8,128)(2,1)S(1)}, u32[]{:S(2)}, u32[]{:S(2)}) collective-permute-start(bf16[2,16,768]{2,1,0:T(8,128)(2,1)S(1)} %slice.152), channel_id=1, source_target_pairs={{1,0},{3,2},{5,4},{7,6},{9,8},{11,10},{13,12},{15,14},{17,16},{19,... | collective-permute-start | bytes 147464 | tf_op jit(solution)/shard_map/ppermute | solution.py:23
  6.8 0.7 copy-start.3
  7.6 2.6 %copy-start.1 = (f32[5,2,510]{2,1,0:T(2,128)}, f32[5,2,510]{2,1,0:T(2,128)S(1)}, u32[]{:S(2)}) copy-start(f32[5,2,510]{2,1,0:T(2,128)S(1)} %select_select_fusion) | copy-start | bytes 61204
  9.8 1.0 copy-start
  12.7 0.9 slice-start.1
  36.8 8.4 %copy-start.2 = (f32[5,2,510]{2,1,0:T(2,128)S(1)}, f32[5,2,510]{2,1,0:T(2,128)}, u32[]{:S(2)}) copy-start(f32[5,2,510]{2,1,0:T(2,128)} %copy-done.1) | copy-start | bytes 61204
  37.8 26.1 %all-to-all-start = ((f32[16,2,16,384]{3,2,1,0:T(8,128)}), f32[16,2,16,384]{3,2,1,0:T(8,128)S(1)}, u32[]{:S(2)}, u32[]{:S(2)}) async-start(f32[16,2,16,384]{3,2,1,0:T(8,128)} %maximum_bitcast_fusion.2), calls=%async_computation | async-start | bytes 1572864 | tf_op jit(solution)/shard_map/all_to_all | solution.py:201
  90.6 1.0 slice-start

commit v11 on v10

--- a/solution.py
+++ b/solution.py
@@ -57,14 +57,17 @@
     return jnp.stack([real_part, imag_part])
 
 
-def merge_kernel(beams, chained, weight_ref, kid_ref, table_ref, out_ref):
+def merge_kernel(beams, chained, grouped, weight_ref, kid_ref, table_ref, out_ref):
     length = kid_ref.shape[-1]
     reach = MARGIN - MAXOFF + 1
     acc = [[None, None], [None, None]]
     for c in range(2):
         interp = []
         for part in range(2):
-            x = kid_ref[c, part]
+            if grouped:
+                x = jnp.concatenate([kid_ref[2 * g + c, part] for g in range(kid_ref.shape[0] // 2)], axis=0)
+            else:
+                x = kid_ref[c, part]
             total = weight_ref[c, 0] * x
             for offset in range(1, reach):
                 total = total + weight_ref[c, offset] * pltpu.roll(x, length - offset, 1)
@@ -85,7 +88,7 @@
                 acc[half] = [real_part, imag_part]
             else:
                 acc[half] = [acc[half][0] + real_part, acc[half][1] + imag_part]
-    rows = kid_ref.shape[2]
+    rows = kid_ref.shape[0] // 2 * kid_ref.shape[2] if grouped else kid_ref.shape[2]
     for half in range(2):
         for part in range(2):
             value = acc[half][part] * half_root
@@ -99,13 +102,14 @@
                     out_ref[part, start : start + beams] = block
 
 
-def merge_call(beams, chained, weights, kids, table):
-    _, _, rows, length = kids.shape
+def merge_call(beams, chained, weights, kids, table, grouped=False):
+    length = kids.shape[-1]
+    rows = kids.shape[0] // 2 * kids.shape[2] if grouped else kids.shape[2]
     vmem = pltpu.VMEM
     elems = 2 * 2 * rows * length
     shape = (2, 2, rows, length) if chained else (2, 2 * rows, length)
     return pl.pallas_call(
-        functools.partial(merge_kernel, beams, chained),
+        functools.partial(merge_kernel, beams, chained, grouped),
         out_shape=jax.ShapeDtypeStruct(shape, jnp.float32),
         in_specs=[
             pl.BlockSpec(memory_space=pltpu.SMEM),
@@ -142,10 +146,10 @@
     return jnp.broadcast_to(per_row(packed, rows // beams)[..., None], (5, 2, 2, rows, LANE))
 
 
-def merge_section(kids, beams, chained, weights, packed, table=None):
+def merge_section(kids, beams, chained, weights, packed, table=None, grouped=False):
     if table is None:
         table = row_table(packed, beams, kids.shape[2])
-    return merge_call(beams, chained, weights, kids, table)
+    return merge_call(beams, chained, weights, kids, table, grouped)
 
 
 def padded_lanes(level, width):
@@ -180,8 +184,8 @@
         start = 2 * beams - 2
         return all_rows[:, :, start : start + 2 * beams]
 
-    def run_section(kids, section, beams, chained, table=None):
-        return merge_section(kids, beams, chained, all_weights[section], section_rows(beams), table)
+    def run_section(kids, section, beams, chained, table=None, grouped=False):
+        return merge_section(kids, beams, chained, all_weights[section], section_rows(beams), table, grouped)
 
     level = split_kids(level, 1)
     for section in range(local_sections):
@@ -200,12 +204,9 @@
     tables = lax.optimization_barrier(tables)
     level = lax.all_to_all(pieces, "pulse", split_axis=0, concat_axis=0, tiled=True)
     level, tables = lax.optimization_barrier((level, tables))
-    level = jnp.transpose(level, (1, 0, 2, 3))
-    level = level.reshape(parts, pulse_count * local_beams, piece_bins + carry)
-    level = split_kids(level, local_beams)
     for bit in range(cross_sections):
         section = local_sections + bit
-        level = run_section(level, section, local_beams << bit, bit < cross_sections - 1, tables[bit])
+        level = run_section(level, section, local_beams << bit, bit < cross_sections - 1, tables[bit], bit == 0)
     level = level[..., :piece_bins].reshape(parts, pulse_count, local_beams, piece_bins)
     level = jnp.transpose(level, (1, 0, 2, 3))
     level = lax.all_to_all(level, "pulse", split_axis=0, concat_axis=0, tiled=True)

time: 113 us -> 113 us (level)
  no operation moved by 1% of the time
where the time goes in v11:
time: 113 us; the launch traced here: 112 us
  Pallas kernels  44.3 us (39%)
  local copies, waits for them, and re-layouts  24.1 us (21%)
  blocking collectives  19.7 us (17%)
  waiting for transfers between devices  11.9 us (11%)
  starting transfers between devices  8.66 us (8%)
  other arithmetic  2.23 us (2%)
    pallas_call x8, Pallas kernels, merge_call(): pl.pallas_call(functools.partial(merge_kernel, beams, chained, grouped),...  44.3 us
    all_to_all x1, blocking collectives, on_device(): lax.all_to_all(level, 'pulse', split_axis=0, concat_axis=0, tiled=True)  19.7 us
    all_to_all x1, waiting for transfers between devices, on_device(): lax.all_to_all(pieces, 'pulse', split_axis=0, concat_axis=0, tiled=True)  11.9 us
    broadcast_in_dim x10, local copies, waits for them, and re-layouts, row_table(): jnp.broadcast_to(per_row(packed, rows // beams)[..., None], (5, 2, 2, row...  8.9 us
    all_to_all x1, starting transfers between devices, on_device(): lax.all_to_all(pieces, 'pulse', split_axis=0, concat_axis=0, tiled=True)  7.38 us
  transfers between devices with their start and end apart: 2, of which 1 were waited for; matrix products, arithmetic and copies ran while one was open for 13% of the time, Pallas kernels for 0%

profile of v11, /device:TPU:0, one launch (start us, length us, event | category | flops | bytes accessed | tf_op | source)
XLA Modules:
  0.0 112.1 jit_solution(3943818107101594400)
XLA Ops:
  0.0 0.8 slice.146
  0.8 1.3 %collective-permute-start = (bf16[2,16,768]{2,1,0:T(8,128)(2,1)S(1)}, bf16[2,16,768]{2,1,0:T(8,128)(2,1)S(1)}, u32[]{:S(2)}, u32[]{:S(2)}) collective-permute-start(bf16[2,16,768]{2,1,0:T(8,128)(2,1)S(1)} %slice.146), channel_id=1, source_target_pairs={{1,0},{3,2},{5,4},{7,6},{9,8},{11,10},{13,12},{15,14},{17,16},{19,... | collective-permute-start | bytes 147464 | tf_op jit(solution)/shard_map/ppermute | solution.py:23
  2.1 0.8 slice_reduce_fusion
  2.9 0.8 fusion.19
  4.1 0.8 fusion.20
  5.2 0.8 fusion.18
  6.0 0.7 tile.69
  6.8 0.4 reshape.66
  7.1 0.2 copy.63
  7.4 0.1 copy-done.4
  7.6 0.1 fusion.12
  7.7 0.6 slice_bitcast_fusion.2
  8.7 0.1 copy.67
  8.9 0.1 copy.68
  9.1 0.7 tile.67
  9.8 0.4 reshape.65
  10.2 0.2 copy.62
  10.4 0.4 copy-done.1
  10.8 0.2 reshape.64
  11.0 0.2 fusion.17
  11.4 0.8 fusion
  12.4 0.3 copy.64
  12.8 0.8 pad_maximum_fusion.2.kid_ref
  13.6 0.7 broadcast_in_dim.116.table_ref
  14.3 4.7 %shard_map.64.kid_ref = f32[2,2,8,4224]{3,2,1,0:T(8,128)} custom-call(f32[2,8]{1,0:T(2,128)} %get-tuple-element.36.weight_ref, f32[2,2,8,4224]{3,2,1,0:T(8,128)} %pad_maximum_fusion.2.kid_ref, f32[5,2,2,8,128]{4,3,2,1,0:T(8,128)} %broadcast_in_dim.116.table_ref), custom_call_target="tpu_custom_call" | custom-call | flops 8110080 | bytes 1081344 | tf_op jit(solution)/shard_map/pallas_call | solution.py:111
  19.1 0.7 broadcast_in_dim.117.table_ref
  19.8 4.6 %shard_map.65.kid_ref = f32[2,2,8,4224]{3,2,1,0:T(8,128)} custom-call(f32[2,8]{1,0:T(2,128)} %get-tuple-element.37.weight_ref, f32[2,2,8,4224]{3,2,1,0:T(8,128)} %shard_map.64.kid_ref, f32[5,2,2,8,128]{4,3,2,1,0:T(8,128)} %broadcast_in_dim.117.table_ref), custom_call_target="tpu_custom_call" | custom-call | flops 8110080 | bytes 1081344 | tf_op jit(solution)/shard_map/pallas_call | solution.py:111
  24.4 0.7 broadcast_in_dim.118.table_ref
  25.1 4.6 %shard_map.66.kid_ref = f32[2,2,8,4224]{3,2,1,0:T(8,128)} custom-call(f32[2,8]{1,0:T(2,128)} %get-tuple-element.38.weight_ref, f32[2,2,8,4224]{3,2,1,0:T(8,128)} %shard_map.65.kid_ref, f32[5,2,2,8,128]{4,3,2,1,0:T(8,128)} %broadcast_in_dim.118.table_ref), custom_call_target="tpu_custom_call" | custom-call | flops 8110080 | bytes 1081344 | tf_op jit(solution)/shard_map/pallas_call | solution.py:111
  29.7 0.7 broadcast_in_dim.120.table_ref
  30.4 4.7 %shard_map.67 = f32[2,16,4224]{2,1,0:T(8,128)} custom-call(f32[2,8]{1,0:T(2,128)} %get-tuple-element.39.weight_ref, f32[2,2,8,4224]{3,2,1,0:T(8,128)} %shard_map.66.kid_ref, f32[5,2,2,8,128]{4,3,2,1,0:T(8,128)} %broadcast_in_dim.120.table_ref), custom_call_target="tpu_custom_call" | custom-call | flops 8110080 | bytes 1081344 | tf_op jit(solution)/shard_map/pallas_call | solution.py:111
  35.2 1.3 %fusion.15 = (f32[2,16,4096]{2,1,0:T(8,128)S(1)}, f32[2,16,4096]{2,1,0:T(8,128)S(1)}) fusion(f32[2,16,4224]{2,1,0:T(8,128)} %shard_map.67), kind=kLoop, calls=%fused_computation.47 | loop fusion | bytes 2113536 | tf_op jit(solution)/shard_map/slice | solution.py:197
  36.5 0.2 copy.78
  36.8 1.0 maximum_bitcast_fusion.2
  37.8 7.4 %all-to-all-start = ((f32[16,2,16,384]{3,2,1,0:T(8,128)}), f32[16,2,16,384]{3,2,1,0:T(8,128)S(1)}, u32[]{:S(2)}, u32[]{:S(2)}) async-start(f32[16,2,16,384]{3,2,1,0:T(8,128)} %maximum_bitcast_fusion.2), calls=%async_computation | async-start | bytes 1572864 | tf_op jit(solution)/shard_map/all_to_all | solution.py:205
  46.1 1.5 %broadcast_in_dim.121.table_ref = f32[5,2,2,128,128]{4,3,2,1,0:T(8,128)} broadcast(f32[5,2,2,128]{3,2,1,0:T(2,128)S(1)} %tile.78), dimensions={0,1,2,3} | broadcast | bytes 1320960 | tf_op jit(solution)/shard_map/broadcast_in_dim | solution.py:146
  47.6 1.5 %broadcast_in_dim.122.table_ref = f32[5,2,2,128,128]{4,3,2,1,0:T(8,128)} broadcast(f32[5,2,2,128]{3,2,1,0:T(2,128)S(1)} %tile.81), dimensions={0,1,2,3} | broadcast | bytes 1320960 | tf_op jit(solution)/shard_map/broadcast_in_dim | solution.py:146
  49.0 1.5 %broadcast_in_dim.123.table_ref = f32[5,2,2,128,128]{4,3,2,1,0:T(8,128)} broadcast(f32[5,2,2,128]{3,2,1,0:T(2,128)S(1)} %tile.84), dimensions={0,1,2,3} | broadcast | bytes 1320960 | tf_op jit(solution)/shard_map/broadcast_in_dim | solution.py:146
  50.5 1.5 %broadcast_in_dim.125.table_ref = f32[5,2,2,128,128]{4,3,2,1,0:T(8,128)} broadcast(f32[5,2,2,128]{3,2,1,0:T(2,128)S(1)} %broadcast_in_dim.124), dimensions={0,1,2,3} | broadcast | bytes 1320960 | tf_op jit(solution)/shard_map/broadcast_in_dim | solution.py:146
  52.0 11.9 %all-to-all-done.kid_ref = f32[16,2,16,384]{3,2,1,0:T(8,128)S(1)} async-done(((f32[16,2,16,384]{3,2,1,0:T(8,128)}), f32[16,2,16,384]{3,2,1,0:T(8,128)S(1)}, u32[]{:S(2)}, u32[]{:S(2)}) %all-to-all-start) | async-done | bytes 786464 | tf_op jit(solution)/shard_map/all_to_all | solution.py:205
  63.9 0.9 copy-done
  64.8 6.5 %shard_map.68.kid_ref = f32[2,2,128,384]{3,2,1,0:T(8,128)} custom-call(f32[2,8]{1,0:T(2,128)} %get-tuple-element.40.weight_ref, f32[16,2,16,384]{3,2,1,0:T(8,128)} %copy-done, f32[5,2,2,128,128]{4,3,2,1,0:T(8,128)} %broadcast_in_dim.121.table_ref), custom_call_target="tpu_custom_call" | custom-call | flops 11796480 | bytes 1572864 | tf_op jit(solution)/shard_map/pallas_call | solution.py:111
  71.2 6.4 %shard_map.69.kid_ref = f32[2,2,128,384]{3,2,1,0:T(8,128)} custom-call(f32[2,8]{1,0:T(2,128)} %get-tuple-element.41.weight_ref, f32[2,2,128,384]{3,2,1,0:T(8,128)} %shard_map.68.kid_ref, f32[5,2,2,128,128]{4,3,2,1,0:T(8,128)} %broadcast_in_dim.122.table_ref), custom_call_target="tpu_custom_call" | custom-call | flops 11796480 | bytes 1572864 | tf_op jit(solution)/shard_map/pallas_call | solution.py:111
  77.6 6.4 %shard_map.70.kid_ref = f32[2,2,128,384]{3,2,1,0:T(8,128)} custom-call(f32[2,8]{1,0:T(2,128)} %get-tuple-element.42.weight_ref, f32[2,2,128,384]{3,2,1,0:T(8,128)} %shard_map.69.kid_ref, f32[5,2,2,128,128]{4,3,2,1,0:T(8,128)} %broadcast_in_dim.123.table_ref), custom_call_target="tpu_custom_call" | custom-call | flops 11796480 | bytes 1572864 | tf_op jit(solution)/shard_map/pallas_call | solution.py:111
  84.0 6.4 %shard_map.71 = f32[2,256,384]{2,1,0:T(8,128)} custom-call(f32[2,8]{1,0:T(2,128)} %get-tuple-element.43.weight_ref, f32[2,2,128,384]{3,2,1,0:T(8,128)} %shard_map.70.kid_ref, f32[5,2,2,128,128]{4,3,2,1,0:T(8,128)} %broadcast_in_dim.125.table_ref), custom_call_target="tpu_custom_call" | custom-call | flops 11796480 | bytes 1572864 | tf_op jit(solution)/shard_map/pallas_call | solution.py:111
  90.4 1.0 slice-done
  91.5 19.7 %all_to_all.10 = f32[16,2,16,256]{3,2,1,0:T(8,128)S(1)} all-to-all(f32[16,2,16,256]{3,2,1,0:T(8,128)S(1)} %bitcast.63), channel_id=1, replica_groups=mesh['pulse'=16,'range'=2] {'pulse'}, dimensions={0} | all-to-all | bytes 1048576 | tf_op jit(solution)/shard_map/all_to_all | solution.py:212
  111.3 0.8 copy.77
  (64 shorter events, 3.0 us)
Async XLA Ops:
  0.8 9.6 %collective-permute-start = (bf16[2,16,768]{2,1,0:T(8,128)(2,1)S(1)}, bf16[2,16,768]{2,1,0:T(8,128)(2,1)S(1)}, u32[]{:S(2)}, u32[]{:S(2)}) collective-permute-start(bf16[2,16,768]{2,1,0:T(8,128)(2,1)S(1)} %slice.146), channel_id=1, source_target_pairs={{1,0},{3,2},{5,4},{7,6},{9,8},{11,10},{13,12},{15,14},{17,16},{19,... | collective-permute-start | bytes 147464 | tf_op jit(solution)/shard_map/ppermute | solution.py:23
  6.8 0.7 copy-start.4
  7.6 2.6 %copy-start.2 = (f32[5,2,510]{2,1,0:T(2,128)}, f32[5,2,510]{2,1,0:T(2,128)S(1)}, u32[]{:S(2)}) copy-start(f32[5,2,510]{2,1,0:T(2,128)S(1)} %select_select_fusion) | copy-start | bytes 61204
  9.8 1.0 copy-start.1
  12.7 0.9 slice-start.1
  36.8 8.4 %copy-start.3 = (f32[5,2,510]{2,1,0:T(2,128)S(1)}, f32[5,2,510]{2,1,0:T(2,128)}, u32[]{:S(2)}) copy-start(f32[5,2,510]{2,1,0:T(2,128)} %copy-done.2) | copy-start | bytes 61204
  37.8 26.1 %all-to-all-start = ((f32[16,2,16,384]{3,2,1,0:T(8,128)}), f32[16,2,16,384]{3,2,1,0:T(8,128)S(1)}, u32[]{:S(2)}, u32[]{:S(2)}) async-start(f32[16,2,16,384]{3,2,1,0:T(8,128)} %maximum_bitcast_fusion.2), calls=%async_computation | async-start | bytes 1572864 | tf_op jit(solution)/shard_map/all_to_all | solution.py:205
  63.9 0.9 copy-start
  90.4 1.0 slice-start

commit v12 on v8

--- a/solution.py
+++ b/solution.py
@@ -57,7 +57,9 @@
     return jnp.stack([real_part, imag_part])
 
 
-def merge_kernel(beams, chained, weight_ref, kid_ref, table_ref, out_ref):
+def merge_kernel(beams, chained, slot, weight_ref, kid_ref, table_ref, out_ref):
+    if slot is not None:
+        table_ref = table_ref.at[slot]
     length = kid_ref.shape[-1]
     reach = MARGIN - MAXOFF + 1
     acc = [[None, None], [None, None]]
@@ -99,13 +101,13 @@
                     out_ref[part, start : start + beams] = block
 
 
-def merge_call(beams, chained, weights, kids, table):
+def merge_call(beams, chained, weights, kids, table, slot=None):
     _, _, rows, length = kids.shape
     vmem = pltpu.VMEM
     elems = 2 * 2 * rows * length
     shape = (2, 2, rows, length) if chained else (2, 2 * rows, length)
     return pl.pallas_call(
-        functools.partial(merge_kernel, beams, chained),
+        functools.partial(merge_kernel, beams, chained, slot),
         out_shape=jax.ShapeDtypeStruct(shape, jnp.float32),
         in_specs=[
             pl.BlockSpec(memory_space=pltpu.SMEM),
@@ -142,10 +144,10 @@
     return jnp.broadcast_to(per_row(packed, rows // beams)[..., None], (5, 2, 2, rows, LANE))
 
 
-def merge_section(kids, beams, chained, weights, packed, table=None):
+def merge_section(kids, beams, chained, weights, packed, table=None, slot=None):
     if table is None:
         table = row_table(packed, beams, kids.shape[2])
-    return merge_call(beams, chained, weights, kids, table)
+    return merge_call(beams, chained, weights, kids, table, slot)
 
 
 def padded_lanes(level, width):
@@ -180,12 +182,16 @@
         start = 2 * beams - 2
         return all_rows[:, :, start : start + 2 * beams]
 
-    def run_section(kids, section, beams, chained, table=None):
-        return merge_section(kids, beams, chained, all_weights[section], section_rows(beams), table)
+    def run_section(kids, section, beams, chained, table=None, slot=None):
+        return merge_section(kids, beams, chained, all_weights[section], section_rows(beams), table, slot)
 
     level = split_kids(level, 1)
+    kid_rows = level.shape[2]
+    local_tables = jnp.stack(
+        [row_table(section_rows(1 << section), 1 << section, kid_rows) for section in range(local_sections)]
+    )
     for section in range(local_sections):
-        level = run_section(level, section, 1 << section, section < local_sections - 1)
+        level = run_section(level, section, 1 << section, section < local_sections - 1, local_tables, section)
     piece_bins = bins // pulse_count
     need = cross_sections * MARGIN
     flat = level[:, :, : bins + need]

time: 113 us -> 112 us (level)
  local copies, waits for them, and re-layouts: 23.4 us -> 20.6 us
  other arithmetic: 3.16 us -> 4.62 us
    broadcast_in_dim x10 -> x5, local copies, waits for them, and re-layouts: 8.9 us -> 5.88 us  [row_table(): jnp.broadcast_to(per_row(packed, rows // beams)[..., None], (5, 2, 2, row...]
  transfers between devices with their start and end apart: 2 -> 2, of which waited for: 1 -> 1; matrix products, arithmetic and copies ran while one was open for 13% -> 15% of each run, Pallas kernels for 0% -> 0%
where the time goes in v12:
time: 112 us; the launch traced here: 111 us
  Pallas kernels  44.6 us (40%)
  local copies, waits for them, and re-layouts  20.6 us (18%)
  blocking collectives  19.7 us (18%)
  waiting for transfers between devices  11.9 us (11%)
  starting transfers between devices  8.67 us (8%)
  other arithmetic  4.62 us (4%)
    pallas_call x8, Pallas kernels, merge_call(): pl.pallas_call(functools.partial(merge_kernel, beams, chained, slot), out...  44.6 us
    all_to_all x1, blocking collectives, on_device(): lax.all_to_all(level, 'pulse', split_axis=0, concat_axis=0, tiled=True)  19.7 us
    all_to_all x1, waiting for transfers between devices, on_device(): lax.all_to_all(pieces, 'pulse', split_axis=0, concat_axis=0, tiled=True)  11.9 us
    all_to_all x1, starting transfers between devices, on_device(): lax.all_to_all(pieces, 'pulse', split_axis=0, concat_axis=0, tiled=True)  7.39 us
    broadcast_in_dim x5, local copies, waits for them, and re-layouts, row_table(): jnp.broadcast_to(per_row(packed, rows // beams)[..., None], (5, 2, 2, row...  5.88 us
  transfers between devices with their start and end apart: 2, of which 1 were waited for; matrix products, arithmetic and copies ran while one was open for 15% of the time, Pallas kernels for 0%

profile of v12, /device:TPU:0, one launch (start us, length us, event | category | flops | bytes accessed | tf_op | source)
XLA Modules:
  0.0 111.4 jit_solution(11478944237712153266)
XLA Ops:
  0.0 0.8 slice.156
  0.8 1.3 %collective-permute-start = (bf16[2,16,768]{2,1,0:T(8,128)(2,1)S(1)}, bf16[2,16,768]{2,1,0:T(8,128)(2,1)S(1)}, u32[]{:S(2)}, u32[]{:S(2)}) collective-permute-start(bf16[2,16,768]{2,1,0:T(8,128)(2,1)S(1)} %slice.156), channel_id=1, source_target_pairs={{1,0},{3,2},{5,4},{7,6},{9,8},{11,10},{13,12},{15,14},{17,16},{19,... | collective-permute-start | bytes 147464 | tf_op jit(solution)/shard_map/ppermute | solution.py:23
  2.1 0.8 fusion.18
  2.9 0.8 select_select_fusion
  3.9 0.8 slice_reduce_fusion
  4.7 0.8 fusion.19
  5.8 0.8 fusion.20
  7.0 0.1 fusion.12
  7.1 0.6 slice_bitcast_fusion.2
  7.9 0.1 copy.68
  8.1 0.1 copy.69
  8.3 0.7 tile.65
  9.0 0.4 reshape.87
  9.4 0.2 copy.64
  9.9 0.8 pad_maximum_fusion.4.table_ref
  10.7 0.7 tile.63
  11.5 0.4 reshape.86
  11.8 0.2 copy.63
  12.0 0.4 copy-done.1
  12.4 0.2 reshape.85
  12.6 0.2 fusion.17
  12.8 0.1 pad_maximum_fusion
  13.0 0.8 fusion
  14.0 0.3 copy.65
  14.4 0.8 pad_maximum_fusion.3.kid_ref
  15.3 4.8 %shard_map.64.kid_ref = f32[2,2,8,4224]{3,2,1,0:T(8,128)} custom-call(f32[2,8]{1,0:T(2,128)} %get-tuple-element.36.weight_ref, f32[2,2,8,4224]{3,2,1,0:T(8,128)} %pad_maximum_fusion.3.kid_ref, f32[4,5,2,2,8,128]{5,4,3,2,1,0:T(8,128)} %pad_maximum_fusion.4.table_ref), custom_call_target="tpu_custom_call" | custom-call | flops 8110080 | bytes 1081344 | tf_op jit(solution)/shard_map/pallas_call | solution.py:109
  20.1 4.7 %shard_map.65.kid_ref = f32[2,2,8,4224]{3,2,1,0:T(8,128)} custom-call(f32[2,8]{1,0:T(2,128)} %get-tuple-element.37.weight_ref, f32[2,2,8,4224]{3,2,1,0:T(8,128)} %shard_map.64.kid_ref, f32[4,5,2,2,8,128]{5,4,3,2,1,0:T(8,128)} %pad_maximum_fusion.4.table_ref), custom_call_target="tpu_custom_call" | custom-call | flops 8110080 | bytes 1081344 | tf_op jit(solution)/shard_map/pallas_call | solution.py:109
  24.8 4.7 %shard_map.66.kid_ref = f32[2,2,8,4224]{3,2,1,0:T(8,128)} custom-call(f32[2,8]{1,0:T(2,128)} %get-tuple-element.38.weight_ref, f32[2,2,8,4224]{3,2,1,0:T(8,128)} %shard_map.65.kid_ref, f32[4,5,2,2,8,128]{5,4,3,2,1,0:T(8,128)} %pad_maximum_fusion.4.table_ref), custom_call_target="tpu_custom_call" | custom-call | flops 8110080 | bytes 1081344 | tf_op jit(solution)/shard_map/pallas_call | solution.py:109
  29.4 4.8 %shard_map.67 = f32[2,16,4224]{2,1,0:T(8,128)} custom-call(f32[2,8]{1,0:T(2,128)} %get-tuple-element.39.weight_ref, f32[2,2,8,4224]{3,2,1,0:T(8,128)} %shard_map.66.kid_ref, f32[4,5,2,2,8,128]{5,4,3,2,1,0:T(8,128)} %pad_maximum_fusion.4.table_ref), custom_call_target="tpu_custom_call" | custom-call | flops 8110080 | bytes 1081344 | tf_op jit(solution)/shard_map/pallas_call | solution.py:109
  34.2 1.1 %slice.209 = f32[2,16,4096]{2,1,0:T(8,128)S(1)} slice(f32[2,16,4224]{2,1,0:T(8,128)} %shard_map.67), slice={[0:2], [0:16], [0:4096]} | slice | bytes 1048576 | tf_op jit(solution)/shard_map/slice | solution.py:199
  35.5 0.2 copy.80
  35.8 1.0 maximum_bitcast_fusion.2
  36.9 7.4 %all-to-all-start = ((f32[16,2,16,316]{3,2,1,0:T(8,128)}), f32[16,2,16,316]{3,2,1,0:T(8,128)S(1)}, u32[]{:S(2)}, u32[]{:S(2)}) async-start(f32[16,2,16,316]{3,2,1,0:T(8,128)} %maximum_bitcast_fusion.2), calls=%async_computation | async-start | bytes 1572864 | tf_op jit(solution)/shard_map/all_to_all | solution.py:207
  45.0 0.1 tile.75
  45.1 0.1 tile.72
  45.2 1.5 %broadcast_in_dim.94.table_ref = f32[5,2,2,128,128]{4,3,2,1,0:T(8,128)} broadcast(f32[5,2,2,128]{3,2,1,0:T(2,128)S(1)} %tile.72), dimensions={0,1,2,3} | broadcast | bytes 1320960 | tf_op jit(solution)/shard_map/broadcast_in_dim | solution.py:144
  46.6 1.5 %broadcast_in_dim.95.table_ref = f32[5,2,2,128,128]{4,3,2,1,0:T(8,128)} broadcast(f32[5,2,2,128]{3,2,1,0:T(2,128)S(1)} %tile.75), dimensions={0,1,2,3} | broadcast | bytes 1320960 | tf_op jit(solution)/shard_map/broadcast_in_dim | solution.py:144
  48.1 1.5 %broadcast_in_dim.96.table_ref = f32[5,2,2,128,128]{4,3,2,1,0:T(8,128)} broadcast(f32[5,2,2,128]{3,2,1,0:T(2,128)S(1)} %tile.78), dimensions={0,1,2,3} | broadcast | bytes 1320960 | tf_op jit(solution)/shard_map/broadcast_in_dim | solution.py:144
  49.6 1.5 %broadcast_in_dim.98.table_ref = f32[5,2,2,128,128]{4,3,2,1,0:T(8,128)} broadcast(f32[5,2,2,128]{3,2,1,0:T(2,128)S(1)} %broadcast_in_dim.97), dimensions={0,1,2,3} | broadcast | bytes 1320960 | tf_op jit(solution)/shard_map/broadcast_in_dim | solution.py:144
  51.0 11.9 %all-to-all-done = f32[16,2,16,316]{3,2,1,0:T(8,128)S(1)} async-done(((f32[16,2,16,316]{3,2,1,0:T(8,128)}), f32[16,2,16,316]{3,2,1,0:T(8,128)S(1)}, u32[]{:S(2)}, u32[]{:S(2)}) %all-to-all-start) | async-done | bytes 647200 | tf_op jit(solution)/shard_map/all_to_all | solution.py:207
  63.1 0.9 pad_maximum_fusion.1.kid_ref
  64.1 6.5 %shard_map.68.kid_ref = f32[2,2,128,384]{3,2,1,0:T(8,128)} custom-call(f32[2,8]{1,0:T(2,128)} %get-tuple-element.40.weight_ref, f32[2,2,128,384]{3,2,1,0:T(8,128)} %pad_maximum_fusion.1.kid_ref, f32[5,2,2,128,128]{4,3,2,1,0:T(8,128)} %broadcast_in_dim.94.table_ref), custom_call_target="tpu_custom_call" | custom-call | flops 11796480 | bytes 1572864 | tf_op jit(solution)/shard_map/pallas_call | solution.py:109
  70.5 6.4 %shard_map.69.kid_ref = f32[2,2,128,384]{3,2,1,0:T(8,128)} custom-call(f32[2,8]{1,0:T(2,128)} %get-tuple-element.41.weight_ref, f32[2,2,128,384]{3,2,1,0:T(8,128)} %shard_map.68.kid_ref, f32[5,2,2,128,128]{4,3,2,1,0:T(8,128)} %broadcast_in_dim.95.table_ref), custom_call_target="tpu_custom_call" | custom-call | flops 11796480 | bytes 1572864 | tf_op jit(solution)/shard_map/pallas_call | solution.py:109
  76.9 6.4 %shard_map.70.kid_ref = f32[2,2,128,384]{3,2,1,0:T(8,128)} custom-call(f32[2,8]{1,0:T(2,128)} %get-tuple-element.42.weight_ref, f32[2,2,128,384]{3,2,1,0:T(8,128)} %shard_map.69.kid_ref, f32[5,2,2,128,128]{4,3,2,1,0:T(8,128)} %broadcast_in_dim.96.table_ref), custom_call_target="tpu_custom_call" | custom-call | flops 11796480 | bytes 1572864 | tf_op jit(solution)/shard_map/pallas_call | solution.py:109
  83.3 6.4 %shard_map.71 = f32[2,256,384]{2,1,0:T(8,128)} custom-call(f32[2,8]{1,0:T(2,128)} %get-tuple-element.43.weight_ref, f32[2,2,128,384]{3,2,1,0:T(8,128)} %shard_map.70.kid_ref, f32[5,2,2,128,128]{4,3,2,1,0:T(8,128)} %broadcast_in_dim.98.table_ref), custom_call_target="tpu_custom_call" | custom-call | flops 11796480 | bytes 1572864 | tf_op jit(solution)/shard_map/pallas_call | solution.py:109
  89.7 1.0 slice-done
  90.8 19.7 %all_to_all.10 = f32[16,2,16,256]{3,2,1,0:T(8,128)S(1)} all-to-all(f32[16,2,16,256]{3,2,1,0:T(8,128)S(1)} %bitcast.75), channel_id=1, replica_groups=mesh['pulse'=16,'range'=2] {'pulse'}, dimensions={0} | all-to-all | bytes 1048576 | tf_op jit(solution)/shard_map/all_to_all | solution.py:217
  110.6 0.8 copy.79
  (63 shorter events, 3.2 us)
Async XLA Ops:
  0.8 11.2 %collective-permute-start = (bf16[2,16,768]{2,1,0:T(8,128)(2,1)S(1)}, bf16[2,16,768]{2,1,0:T(8,128)(2,1)S(1)}, u32[]{:S(2)}, u32[]{:S(2)}) collective-permute-start(bf16[2,16,768]{2,1,0:T(8,128)(2,1)S(1)} %slice.156), channel_id=1, source_target_pairs={{1,0},{3,2},{5,4},{7,6},{9,8},{11,10},{13,12},{15,14},{17,16},{19,... | collective-permute-start | bytes 147464 | tf_op jit(solution)/shard_map/ppermute | solution.py:23
  11.4 1.0 copy-start.1
  34.2 1.2 %copy-start = (f32[2,16,4224]{2,1,0:T(8,128)S(1)}, f32[2,16,4224]{2,1,0:T(8,128)}, u32[]{:S(2)}) copy-start(f32[2,16,4224]{2,1,0:T(8,128)} %shard_map.67) | copy-start | bytes 1622020
  36.9 26.1 %all-to-all-start = ((f32[16,2,16,316]{3,2,1,0:T(8,128)}), f32[16,2,16,316]{3,2,1,0:T(8,128)S(1)}, u32[]{:S(2)}, u32[]{:S(2)}) async-start(f32[16,2,16,316]{3,2,1,0:T(8,128)} %maximum_bitcast_fusion.2), calls=%async_computation | async-start | bytes 1572864 | tf_op jit(solution)/shard_map/all_to_all | solution.py:207
  89.7 1.0 slice-start

commit v13 on v12

--- a/solution.py
+++ b/solution.py
@@ -57,9 +57,18 @@
     return jnp.stack([real_part, imag_part])
 
 
-def merge_kernel(beams, chained, slot, weight_ref, kid_ref, table_ref, out_ref):
+def merge_kernel(beams, chained, slot, section, index_ref, tap_ref, kid_ref, table_ref, out_ref):
     if slot is not None:
         table_ref = table_ref.at[slot]
+    weight = []
+    for c in range(2):
+        row = []
+        for d in range(MARGIN - MAXOFF + 1):
+            total = jnp.where(index_ref[section, c, 0] == d, tap_ref[section, c, 0], 0.0)
+            for tap in range(1, index_ref.shape[-1]):
+                total = total + jnp.where(index_ref[section, c, tap] == d, tap_ref[section, c, tap], 0.0)
+            row.append(total)
+        weight.append(row)
     length = kid_ref.shape[-1]
     reach = MARGIN - MAXOFF + 1
     acc = [[None, None], [None, None]]
@@ -67,9 +76,9 @@
         interp = []
         for part in range(2):
             x = kid_ref[c, part]
-            total = weight_ref[c, 0] * x
+            total = weight[c][0] * x
             for offset in range(1, reach):
-                total = total + weight_ref[c, offset] * pltpu.roll(x, length - offset, 1)
+                total = total + weight[c][offset] * pltpu.roll(x, length - offset, 1)
             interp.append(total)
         for half in range(2):
             moved = []
@@ -102,21 +111,23 @@
 
 
 def merge_call(beams, chained, weights, kids, table, slot=None):
+    section, tap_index, tap_weight = weights
     _, _, rows, length = kids.shape
     vmem = pltpu.VMEM
     elems = 2 * 2 * rows * length
     shape = (2, 2, rows, length) if chained else (2, 2 * rows, length)
     return pl.pallas_call(
-        functools.partial(merge_kernel, beams, chained, slot),
+        functools.partial(merge_kernel, beams, chained, slot, section),
         out_shape=jax.ShapeDtypeStruct(shape, jnp.float32),
         in_specs=[
+            pl.BlockSpec(memory_space=pltpu.SMEM),
             pl.BlockSpec(memory_space=pltpu.SMEM),
             pl.BlockSpec(memory_space=vmem),
             pl.BlockSpec(memory_space=vmem),
         ],
         out_specs=pl.BlockSpec(memory_space=vmem),
         cost_estimate=pl.CostEstimate(flops=60 * elems, transcendentals=0, bytes_accessed=8 * elems),
-    )(weights, kids, table)
+    )(tap_index, tap_weight, kids, table)
 
 
 def tap_weights(taps, weights):
@@ -172,7 +183,6 @@
     rim = shifted(raw[:, :, :rim_len], "range", -1)
     wide = jnp.concatenate([raw, rim], axis=2)
     level = padded_lanes(compress(wide, filt, blocks), bins + extra)
-    all_weights = tap_weights(tap_index, tap_weight)
     kind = lax.broadcasted_iota(jnp.int32, (5,) + beam_shift.shape, 0)
     bit_rows = ((beam_shift[None] >> jnp.minimum(kind, 2)) & 1).astype(jnp.float32)
     angle_rows = jnp.where(kind == 3, jnp.cos(beam_phase)[None], jnp.sin(beam_phase)[None])
@@ -183,7 +193,7 @@
         return all_rows[:, :, start : start + 2 * beams]
 
     def run_section(kids, section, beams, chained, table=None, slot=None):
-        return merge_section(kids, beams, chained, all_weights[section], section_rows(beams), table, slot)
+        return merge_section(kids, beams, chained, (section, tap_index, tap_weight), section_rows(beams), table, slot)
 
     level = split_kids(level, 1)
     kid_rows = level.shape[2]

time: 112 us -> 111 us (level)
  local copies, waits for them, and re-layouts: 20.6 us -> 19.1 us
    slice x2 -> x0, local copies, waits for them, and re-layouts: 1.68 us -> none  [tap_weights(): total = jnp.where(taps[..., 0, None] == spots, weights[..., 0, None], 0.0)]
    unnamed x6 -> x12, local copies, waits for them, and re-layouts: 0.67 us -> 2.04 us
  transfers between devices with their start and end apart: 2 -> 2, of which waited for: 1 -> 1; matrix products, arithmetic and copies ran while one was open for 15% -> 13% of each run, Pallas kernels for 0% -> 0%
where the time goes in v13:
time: 111 us; the launch traced here: 110 us
  Pallas kernels  44.7 us (40%)
  blocking collectives  19.7 us (18%)
  local copies, waits for them, and re-layouts  19.1 us (17%)
  waiting for transfers between devices  11.9 us (11%)
  starting transfers between devices  8.66 us (8%)
  other arithmetic  4.51 us (4%)
    pallas_call x8, Pallas kernels, merge_call(): pl.pallas_call(functools.partial(merge_kernel, beams, chained, slot, sect...  44.7 us
    all_to_all x1, blocking collectives, on_device(): lax.all_to_all(level, 'pulse', split_axis=0, concat_axis=0, tiled=True)  19.7 us
    all_to_all x1, waiting for transfers between devices, on_device(): lax.all_to_all(pieces, 'pulse', split_axis=0, concat_axis=0, tiled=True)  11.9 us
    all_to_all x1, starting transfers between devices, on_device(): lax.all_to_all(pieces, 'pulse', split_axis=0, concat_axis=0, tiled=True)  7.38 us
    broadcast_in_dim x5, local copies, waits for them, and re-layouts, row_table(): jnp.broadcast_to(per_row(packed, rows // beams)[..., None], (5, 2, 2, row...  5.89 us
  transfers between devices with their start and end apart: 2, of which 1 were waited for; matrix products, arithmetic and copies ran while one was open for 13% of the time, Pallas kernels for 0%

profile of v13, /device:TPU:0, one launch (start us, length us, event | category | flops | bytes accessed | tf_op | source)
XLA Modules:
  0.0 109.8 jit_solution(3560468918861133803)
XLA Ops:
  0.0 0.8 slice.92
  0.8 1.3 %collective-permute-start = (bf16[2,16,768]{2,1,0:T(8,128)(2,1)S(1)}, bf16[2,16,768]{2,1,0:T(8,128)(2,1)S(1)}, u32[]{:S(2)}, u32[]{:S(2)}) collective-permute-start(bf16[2,16,768]{2,1,0:T(8,128)(2,1)S(1)} %slice.92), channel_id=1, source_target_pairs={{1,0},{3,2},{5,4},{7,6},{9,8},{11,10},{13,12},{15,14},{17,16},{19,... | collective-permute-start | bytes 147464 | tf_op jit(solution)/shard_map/ppermute | solution.py:23
  2.1 0.8 fusion.15
  2.9 0.8 select_select_fusion
  3.9 0.8 slice_reduce_fusion
  4.8 0.1 copy.84
  4.9 0.1 stack_broadcast_in_dim.29
  5.0 0.1 copy.85
  5.2 0.7 tile.65
  5.9 0.4 reshape.87
  6.3 0.2 copy.80
  6.9 0.8 pad_maximum_fusion.4.table_ref
  7.6 0.7 copy.103.index_ref
  8.3 0.7 copy.104.tap_ref
  9.0 0.7 tile.63
  9.8 0.4 reshape.86
  10.1 0.2 copy.79
  10.3 0.4 copy-done.1
  10.7 0.2 reshape.85
  10.9 0.2 fusion.14
  11.1 0.1 pad_maximum_fusion
  11.3 0.8 fusion
  12.3 0.3 copy.81
  12.7 0.8 pad_maximum_fusion.3.kid_ref
  13.6 4.8 %shard_map.64.kid_ref = f32[2,2,8,4224]{3,2,1,0:T(8,128)} custom-call(s32[8,2,4]{2,1,0:T(2,128)} %copy.103.index_ref, f32[8,2,4]{2,1,0:T(2,128)} %copy.104.tap_ref, f32[2,2,8,4224]{3,2,1,0:T(8,128)} %pad_maximum_fusion.3.kid_ref, f32[4,5,2,2,8,128]{5,4,3,2,1,0:T(8,128)} %pad_maximum_fusion.4.table_ref), custom_call_target="tpu_custom_call" | custom-call | flops 8110080 | bytes 1081344 | tf_op jit(solution)/shard_map/pallas_call | solution.py:119
  18.4 4.7 %shard_map.65.kid_ref = f32[2,2,8,4224]{3,2,1,0:T(8,128)} custom-call(s32[8,2,4]{2,1,0:T(2,128)} %copy.103.index_ref, f32[8,2,4]{2,1,0:T(2,128)} %copy.104.tap_ref, f32[2,2,8,4224]{3,2,1,0:T(8,128)} %shard_map.64.kid_ref, f32[4,5,2,2,8,128]{5,4,3,2,1,0:T(8,128)} %pad_maximum_fusion.4.table_ref), custom_call_target="tpu_custom_call" | custom-call | flops 8110080 | bytes 1081344 | tf_op jit(solution)/shard_map/pallas_call | solution.py:119
  23.1 4.7 %shard_map.66.kid_ref = f32[2,2,8,4224]{3,2,1,0:T(8,128)} custom-call(s32[8,2,4]{2,1,0:T(2,128)} %copy.103.index_ref, f32[8,2,4]{2,1,0:T(2,128)} %copy.104.tap_ref, f32[2,2,8,4224]{3,2,1,0:T(8,128)} %shard_map.65.kid_ref, f32[4,5,2,2,8,128]{5,4,3,2,1,0:T(8,128)} %pad_maximum_fusion.4.table_ref), custom_call_target="tpu_custom_call" | custom-call | flops 8110080 | bytes 1081344 | tf_op jit(solution)/shard_map/pallas_call | solution.py:119
  27.8 4.8 %shard_map.67 = f32[2,16,4224]{2,1,0:T(8,128)} custom-call(s32[8,2,4]{2,1,0:T(2,128)} %copy.103.index_ref, f32[8,2,4]{2,1,0:T(2,128)} %copy.104.tap_ref, f32[2,2,8,4224]{3,2,1,0:T(8,128)} %shard_map.66.kid_ref, f32[4,5,2,2,8,128]{5,4,3,2,1,0:T(8,128)} %pad_maximum_fusion.4.table_ref), custom_call_target="tpu_custom_call" | custom-call | flops 8110080 | bytes 1081344 | tf_op jit(solution)/shard_map/pallas_call | solution.py:119
  32.6 1.1 %slice.137 = f32[2,16,4096]{2,1,0:T(8,128)S(1)} slice(f32[2,16,4224]{2,1,0:T(8,128)} %shard_map.67), slice={[0:2], [0:16], [0:4096]} | slice | bytes 1048576 | tf_op jit(solution)/shard_map/slice | solution.py:209
  33.8 0.2 copy.112
  34.2 1.0 maximum_bitcast_fusion.2
  35.2 7.4 %all-to-all-start = ((f32[16,2,16,316]{3,2,1,0:T(8,128)}), f32[16,2,16,316]{3,2,1,0:T(8,128)S(1)}, u32[]{:S(2)}, u32[]{:S(2)}) async-start(f32[16,2,16,316]{3,2,1,0:T(8,128)} %maximum_bitcast_fusion.2), calls=%async_computation | async-start | bytes 1572864 | tf_op jit(solution)/shard_map/all_to_all | solution.py:217
  43.2 0.1 tile.78
  43.3 0.1 tile.75
  43.4 0.1 tile.72
  43.5 1.5 %broadcast_in_dim.43.table_ref = f32[5,2,2,128,128]{4,3,2,1,0:T(8,128)} broadcast(f32[5,2,2,128]{3,2,1,0:T(2,128)S(1)} %tile.72), dimensions={0,1,2,3} | broadcast | bytes 1320960 | tf_op jit(solution)/shard_map/broadcast_in_dim | solution.py:155
  45.0 1.5 %broadcast_in_dim.44.table_ref = f32[5,2,2,128,128]{4,3,2,1,0:T(8,128)} broadcast(f32[5,2,2,128]{3,2,1,0:T(2,128)S(1)} %tile.75), dimensions={0,1,2,3} | broadcast | bytes 1320960 | tf_op jit(solution)/shard_map/broadcast_in_dim | solution.py:155
  46.4 1.5 %broadcast_in_dim.45.table_ref = f32[5,2,2,128,128]{4,3,2,1,0:T(8,128)} broadcast(f32[5,2,2,128]{3,2,1,0:T(2,128)S(1)} %tile.78), dimensions={0,1,2,3} | broadcast | bytes 1320960 | tf_op jit(solution)/shard_map/broadcast_in_dim | solution.py:155
  47.9 1.5 %broadcast_in_dim.47.table_ref = f32[5,2,2,128,128]{4,3,2,1,0:T(8,128)} broadcast(f32[5,2,2,128]{3,2,1,0:T(2,128)S(1)} %broadcast_in_dim.46), dimensions={0,1,2,3} | broadcast | bytes 1320960 | tf_op jit(solution)/shard_map/broadcast_in_dim | solution.py:155
  49.4 11.9 %all-to-all-done = f32[16,2,16,316]{3,2,1,0:T(8,128)S(1)} async-done(((f32[16,2,16,316]{3,2,1,0:T(8,128)}), f32[16,2,16,316]{3,2,1,0:T(8,128)S(1)}, u32[]{:S(2)}, u32[]{:S(2)}) %all-to-all-start) | async-done | bytes 647200 | tf_op jit(solution)/shard_map/all_to_all | solution.py:217
  61.5 0.9 pad_maximum_fusion.1.kid_ref
  62.4 6.5 %shard_map.68.kid_ref = f32[2,2,128,384]{3,2,1,0:T(8,128)} custom-call(s32[8,2,4]{2,1,0:T(2,128)} %copy.103.index_ref, f32[8,2,4]{2,1,0:T(2,128)} %copy.104.tap_ref, f32[2,2,128,384]{3,2,1,0:T(8,128)} %pad_maximum_fusion.1.kid_ref, f32[5,2,2,128,128]{4,3,2,1,0:T(8,128)} %broadcast_in_dim.43.table_ref), custom_call_target="tpu_custom_call" | custom-call | flops 11796480 | bytes 1572864 | tf_op jit(solution)/shard_map/pallas_call | solution.py:119
  68.9 6.4 %shard_map.69.kid_ref = f32[2,2,128,384]{3,2,1,0:T(8,128)} custom-call(s32[8,2,4]{2,1,0:T(2,128)} %copy.103.index_ref, f32[8,2,4]{2,1,0:T(2,128)} %copy.104.tap_ref, f32[2,2,128,384]{3,2,1,0:T(8,128)} %shard_map.68.kid_ref, f32[5,2,2,128,128]{4,3,2,1,0:T(8,128)} %broadcast_in_dim.44.table_ref), custom_call_target="tpu_custom_call" | custom-call | flops 11796480 | bytes 1572864 | tf_op jit(solution)/shard_map/pallas_call | solution.py:119
  75.3 6.4 %shard_map.70.kid_ref = f32[2,2,128,384]{3,2,1,0:T(8,128)} custom-call(s32[8,2,4]{2,1,0:T(2,128)} %copy.103.index_ref, f32[8,2,4]{2,1,0:T(2,128)} %copy.104.tap_ref, f32[2,2,128,384]{3,2,1,0:T(8,128)} %shard_map.69.kid_ref, f32[5,2,2,128,128]{4,3,2,1,0:T(8,128)} %broadcast_in_dim.45.table_ref), custom_call_target="tpu_custom_call" | custom-call | flops 11796480 | bytes 1572864 | tf_op jit(solution)/shard_map/pallas_call | solution.py:119
  81.7 6.4 %shard_map.71 = f32[2,256,384]{2,1,0:T(8,128)} custom-call(s32[8,2,4]{2,1,0:T(2,128)} %copy.103.index_ref, f32[8,2,4]{2,1,0:T(2,128)} %copy.104.tap_ref, f32[2,2,128,384]{3,2,1,0:T(8,128)} %shard_map.70.kid_ref, f32[5,2,2,128,128]{4,3,2,1,0:T(8,128)} %broadcast_in_dim.47.table_ref), custom_call_target="tpu_custom_call" | custom-call | flops 11796480 | bytes 1572864 | tf_op jit(solution)/shard_map/pallas_call | solution.py:119
  88.1 1.0 slice-done
  89.2 19.7 %all_to_all.10 = f32[16,2,16,256]{3,2,1,0:T(8,128)S(1)} all-to-all(f32[16,2,16,256]{3,2,1,0:T(8,128)S(1)} %bitcast.51), channel_id=1, replica_groups=mesh['pulse'=16,'range'=2] {'pulse'}, dimensions={0} | all-to-all | bytes 1048576 | tf_op jit(solution)/shard_map/all_to_all | solution.py:227
  109.0 0.8 copy.111
  (57 shorter events, 2.3 us)
Async XLA Ops:
  0.8 9.5 %collective-permute-start = (bf16[2,16,768]{2,1,0:T(8,128)(2,1)S(1)}, bf16[2,16,768]{2,1,0:T(8,128)(2,1)S(1)}, u32[]{:S(2)}, u32[]{:S(2)}) collective-permute-start(bf16[2,16,768]{2,1,0:T(8,128)(2,1)S(1)} %slice.92), channel_id=1, source_target_pairs={{1,0},{3,2},{5,4},{7,6},{9,8},{11,10},{13,12},{15,14},{17,16},{19,... | collective-permute-start | bytes 147464 | tf_op jit(solution)/shard_map/ppermute | solution.py:23
  6.3 1.3 %copy-start.2 = (s32[8,2,4]{0,2,1:T(4,128)S(1)}, s32[8,2,4]{0,2,1:T(4,128)}, u32[]{:S(2)}) copy-start(s32[8,2,4]{0,2,1:T(4,128)} %param.8) | copy-start | bytes 772
  6.3 2.0 %copy-start.3 = (f32[8,2,4]{0,2,1:T(4,128)S(1)}, f32[8,2,4]{0,2,1:T(4,128)}, u32[]{:S(2)}) copy-start(f32[8,2,4]{0,2,1:T(4,128)} %param.9) | copy-start | bytes 772
  9.7 1.0 copy-start.1
  32.6 1.2 %copy-start = (f32[2,16,4224]{2,1,0:T(8,128)S(1)}, f32[2,16,4224]{2,1,0:T(8,128)}, u32[]{:S(2)}) copy-start(f32[2,16,4224]{2,1,0:T(8,128)} %shard_map.67) | copy-start | bytes 1622020
  35.2 26.1 %all-to-all-start = ((f32[16,2,16,316]{3,2,1,0:T(8,128)}), f32[16,2,16,316]{3,2,1,0:T(8,128)S(1)}, u32[]{:S(2)}, u32[]{:S(2)}) async-start(f32[16,2,16,316]{3,2,1,0:T(8,128)} %maximum_bitcast_fusion.2), calls=%async_computation | async-start | bytes 1572864 | tf_op jit(solution)/shard_map/all_to_all | solution.py:217
  88.1 1.0 slice-start
